TPU v7x, 1024 devices: a whole 8x8x8 slice. The times are simulated.
1024 devices in a mesh: dp: 2 (over x_hi), expert: 32 (over y, x_lo), fsdp: 16 (over z, core).
Axes of the slice: x: 8 (x_hi: 2, x_lo: 4; x = x_hi * 4 + x_lo), y: 8, z: 8, core: 2. Of those that a mesh axis runs over, the one named last changes fastest.
Arguments:
- tokens: bfloat16 [2048, 2048], P(('dp', 'expert'), 'fsdp'), may hold values from -6 to 6
- grad_out: bfloat16 [2048, 2048], P(('dp', 'expert'), 'fsdp'), may hold values from -6 to 6
- expert_ids: int32 [2048, 6], P(('dp', 'expert')), may hold values from 0 to 63, all different within a row; in each aligned block of 32 rows (0 to 31, 32 to 63, ...) at most 3 rows name the same one
- gate_weights: float32 [2048, 6], P(('dp', 'expert')), may hold values from 0.05 to 1
- w_gate: bfloat16 [64, 1408, 2048], P('expert', 'fsdp'), may hold values from -0.125 to 0.125
- w_up: bfloat16 [64, 1408, 2048], P('expert', 'fsdp'), may hold values from -0.125 to 0.125
- w_down: bfloat16 [64, 1408, 2048], P('expert', None, 'fsdp'), may hold values from -0.15625 to 0.15625
Outputs:
- mixed: bfloat16 [2048, 2048], P(('dp', 'expert'), 'fsdp')
- grad_tokens: bfloat16 [2048, 2048], P(('dp', 'expert'), 'fsdp')
- grad_w_gate: bfloat16 [64, 1408, 2048], P('expert', 'fsdp', 'dp')
- grad_w_up: bfloat16 [64, 1408, 2048], P('expert', 'fsdp', 'dp')
- grad_w_down: bfloat16 [64, 1408, 2048], P('expert', 'dp', 'fsdp')
Inputs may be any that keep to these rules, and one draw needn't show every extreme that they name: `expert_ids`: in each aligned block of 32 rows (the tokens of one index of dp and expert) no expert is named by more than 3 rows, a bound that some block reaches; a row names distinct experts.
All inputs are finite; a program needn't handle non-finite values.
Results may differ from a plain program's by a relative error of at most 0.025.
Values may be sent and summed in bfloat16 or wider, within the bound.
No kernel may reach another device: no remote copies, remote signals or barrier semaphores. Data moves between devices by JAX's collectives and lax.ppermute only.
A program may use at most 32 MiB of HBM per device.

v0:
```python
import jax
import jax.numpy as jnp
from jax import lax
from jax.sharding import PartitionSpec as P


def rounded(values):
    return lax.optimization_barrier(values.astype(jnp.bfloat16)).astype(jnp.float32)


def silu_parts(pre_act):
    sigmoid_value = jax.nn.sigmoid(pre_act)
    return (pre_act * sigmoid_value, sigmoid_value * (1.0 + pre_act * (1.0 - sigmoid_value)))


def body(tokens, grad_out, expert_ids, gate_weights, w_gate, w_up, w_down):
    tok_rows = tokens.shape[0]
    choose = expert_ids.shape[1]
    exp_local = w_gate.shape[0]
    model_width = w_gate.shape[2]
    owners = lax.axis_size("expert")
    experts_all = owners * exp_local
    capacity = max(2, min(tok_rows, 5 * choose * tok_rows // (4 * experts_all)))
    slot_count = experts_all * capacity
    flat_ids = expert_ids.reshape(-1)
    onehot = (flat_ids[:, None] == jnp.arange(experts_all, dtype=jnp.int32)[None, :]).astype(
        jnp.int32
    )
    before = jnp.cumsum(onehot, axis=0) - onehot
    slot_rank = jnp.sum(before * onehot, axis=1)
    slot_of = (flat_ids * capacity + slot_rank).reshape(tok_rows, choose)
    placed = (slot_of[:, :, None] == jnp.arange(slot_count, dtype=jnp.int32)[None, None, :]).astype(
        jnp.float32
    )
    picker = jnp.sum(placed, axis=1).T
    weighted = jnp.einsum("tks,tk->st", placed, gate_weights, precision=lax.Precision.HIGHEST)
    picker_half = picker.astype(jnp.bfloat16)
    scaled_grad = jnp.dot(
        weighted, grad_out.astype(jnp.float32), precision=lax.Precision.HIGHEST
    ).astype(jnp.bfloat16)
    full_rows = lax.all_gather(tokens, "fsdp", axis=1, tiled=True)
    outgoing = jnp.dot(picker_half, full_rows, preferred_element_type=jnp.float32).astype(
        jnp.bfloat16
    )
    rows_in, grads_in = (
        lax.all_to_all(outgoing, "expert", split_axis=0, concat_axis=0, tiled=True),
        lax.all_to_all(scaled_grad, "expert", split_axis=0, concat_axis=0, tiled=True),
    )
    received = rows_in.reshape(owners, exp_local, capacity, model_width)
    cotangent = grads_in.reshape(owners, exp_local, capacity, -1)
    gate_pre = jnp.einsum("jecd,efd->jecf", received, w_gate, preferred_element_type=jnp.float32)
    up_pre = jnp.einsum("jecd,efd->jecf", received, w_up, preferred_element_type=jnp.float32)
    activation, slope_term = silu_parts(gate_pre)
    hidden = (activation * up_pre).astype(jnp.bfloat16)
    hidden_all = lax.all_gather(hidden, "fsdp", axis=3, tiled=True)
    expert_out = jnp.einsum(
        "jecf,efd->jecd", hidden_all, w_down, preferred_element_type=jnp.float32
    ).astype(jnp.bfloat16)
    hidden_parts = rounded(
        jnp.einsum("jecd,efd->jecf", cotangent, w_down, preferred_element_type=jnp.float32)
    )
    grad_hidden = lax.psum_scatter(
        hidden_parts.astype(jnp.bfloat16), "fsdp", scatter_dimension=3, tiled=True
    ).astype(jnp.float32)
    grad_gate_pre = (grad_hidden * up_pre * slope_term).astype(jnp.bfloat16)
    grad_up_pre = (grad_hidden * activation).astype(jnp.bfloat16)
    input_parts = jnp.einsum(
        "jecf,efd->jecd", grad_gate_pre, w_gate, preferred_element_type=jnp.float32
    )
    input_parts = rounded(
        input_parts
        + jnp.einsum("jecf,efd->jecd", grad_up_pre, w_up, preferred_element_type=jnp.float32)
    )
    input_slices = lax.psum_scatter(
        input_parts.astype(jnp.bfloat16), "fsdp", scatter_dimension=3, tiled=True
    )
    mixed_slots, input_slots = (
        lax.all_to_all(
            expert_out.reshape(slot_count, -1), "expert", split_axis=0, concat_axis=0, tiled=True
        ),
        lax.all_to_all(
            input_slices.reshape(slot_count, -1), "expert", split_axis=0, concat_axis=0, tiled=True
        ),
    )
    mixed = jnp.dot(
        weighted.T, mixed_slots.astype(jnp.float32), precision=lax.Precision.HIGHEST
    ).astype(jnp.bfloat16)
    grad_tokens = jnp.dot(
        picker.T, input_slots.astype(jnp.float32), precision=lax.Precision.HIGHEST
    ).astype(jnp.bfloat16)
    grad_gate_w = rounded(
        jnp.einsum("jecf,jecd->efd", grad_gate_pre, received, preferred_element_type=jnp.float32)
    )
    grad_up_w = rounded(
        jnp.einsum("jecf,jecd->efd", grad_up_pre, received, preferred_element_type=jnp.float32)
    )
    grad_down_w = rounded(
        jnp.einsum("jecf,jecd->efd", hidden_all, cotangent, preferred_element_type=jnp.float32)
    )
    summed_gate, summed_up = (
        lax.psum_scatter(
            grad_gate_w.astype(jnp.bfloat16), "dp", scatter_dimension=2, tiled=True
        ).astype(jnp.float32),
        lax.psum_scatter(
            grad_up_w.astype(jnp.bfloat16), "dp", scatter_dimension=2, tiled=True
        ).astype(jnp.float32),
    )
    summed_down = lax.psum_scatter(
        grad_down_w.astype(jnp.bfloat16), "dp", scatter_dimension=1, tiled=True
    )
    return (
        mixed,
        grad_tokens,
        summed_gate.astype(jnp.bfloat16),
        summed_up.astype(jnp.bfloat16),
        summed_down,
    )


def solution(mesh):
    in_specs = (
        P(("dp", "expert"), "fsdp"),
        P(("dp", "expert"), "fsdp"),
        P(("dp", "expert"), None),
        P(("dp", "expert"), None),
        P("expert", "fsdp", None),
        P("expert", "fsdp", None),
        P("expert", None, "fsdp"),
    )
    out_specs = (
        P(("dp", "expert"), "fsdp"),
        P(("dp", "expert"), "fsdp"),
        P("expert", "fsdp", "dp"),
        P("expert", "fsdp", "dp"),
        P("expert", "dp", "fsdp"),
    )
    return jax.shard_map(body, mesh=mesh, in_specs=in_specs, out_specs=out_specs, check_vma=False)
```

profile of v0, /device:TPU:1, one launch (start us, length us, event | category | flops | bytes accessed | tf_op | source)
XLA Modules:
  0.0 336.4 jit_solution(16328677287022787553)
XLA Ops:
  7.2 0.0 copy-start
  7.2 0.8 copy.58
  8.0 0.8 copy.46
  8.8 0.1 eq.35
  8.9 0.6 reduce-window.6
  9.5 0.2 slice_reduce_fusion
  9.8 0.1 bitcast_bitcast_fusion
  9.9 0.1 reduce_sum.21
  10.0 0.1 copy.49
  10.1 0.7 multiply_add_fusion
  10.8 0.1 iota_compare_fusion
  10.9 0.3 fusion.13
  11.2 1.0 convolution_convert_fusion.2
  12.2 0.7 all_to_all.33
  12.8 11.3 %all-to-all-start.2 = ((bf16[32,6,128]{2,1,0:T(8,128)(2,1)}), bf16[32,6,128]{2,1,0:T(8,128)(2,1)S(1)}, u32[]{:S(2)}, u32[]{:S(2)}) async-start(bf16[32,6,128]{2,1,0:T(8,128)(2,1)} %all_to_all.33), calls=%async_computation.2 | async-start | bytes 131072 | tf_op jit(solution)/shard_map/all_to_all | solution.py:47
  24.1 0.1 convert_reduce_fusion
  24.2 30.9 %all_gather.6 = bf16[32,2048]{1,0:T(8,128)(2,1)S(1)} all-gather(bf16[32,128]{1,0:T(8,128)(2,1)} %param.7), channel_id=1, replica_groups=mesh['dp'=2,'expert'=32,'fsdp'=16] {'fsdp'}, dimensions={1}, use_global_device_ids=true | all-gather | bytes 139264 | tf_op jit(solution)/shard_map/all_gather | solution.py:41
  55.1 0.4 convolution_convert_fusion.1
  55.5 0.0 copy-start.1
  55.5 1.2 all_to_all.28
  56.7 9.8 %all-to-all-start = ((bf16[32,6,2048]{2,1,0:T(8,128)(2,1)}), bf16[32,6,2048]{2,1,0:T(8,128)(2,1)S(1)}, u32[]{:S(2)}, u32[]{:S(2)}) async-start(bf16[32,6,2048]{2,1,0:T(8,128)(2,1)} %all_to_all.28), calls=%async_computation | async-start | bytes 2097152 | tf_op jit(solution)/shard_map/all_to_all | solution.py:46
  66.5 0.0 reduce-scatter.16.cloned.1.call-start
  66.6 0.4 fusion.4
  67.0 3.6 %copy.66 = bf16[32,2,3,1408]{0,2,1,3:T(4,128)(2,1)} copy(bf16[32,2,3,1408]{3,0,2,1:T(8,128)(2,1)S(1)} %fusion.4) | data formatting | bytes 1081344
  70.6 6.1 %reshape.62 = bf16[1408,192]{1,0:T(8,128)(2,1)} reshape(bf16[1408,2,3,32]{3,2,1,0:T(4,128)(2,1)} %bitcast.97) | data formatting | bytes 1081344
  76.7 0.0 reduce-scatter.16.cloned.1.call-update
  76.7 0.0 reduce-scatter.18.cloned.1.call-start
  76.7 55.9 %reduce-scatter.16.cloned.1.call-done = bf16[88,192]{1,0:T(8,128)(2,1)} async-done(((bf16[1408,192]{1,0:T(8,128)(2,1)}), bf16[88,192]{1,0:T(8,128)(2,1)}) %reduce-scatter.16.cloned.1.call-update) | async-done | bytes 33808
  132.6 0.9 reshape.63
  133.5 0.1 copy.67
  133.7 0.4 copy.50
  134.1 0.4 convolution_bitcast_fusion.4
  134.5 0.4 fusion.16
  134.9 0.4 fusion.8
  135.3 0.4 fusion.5
  135.7 4.8 %copy.68 = bf16[32,2,3,2048]{0,2,1,3:T(4,128)(2,1)} copy(bf16[32,2,3,2048]{3,0,2,1:T(8,128)(2,1)S(1)} %fusion.5) | data formatting | bytes 1572864
  140.4 8.2 %reshape.64 = bf16[2048,192]{1,0:T(8,128)(2,1)} reshape(bf16[2048,2,3,32]{3,2,1,0:T(4,128)(2,1)} %bitcast.92) | data formatting | bytes 1572864
  148.6 0.0 reduce-scatter.18.cloned.1.call-update
  148.6 0.0 reduce-scatter.10.cloned.1.call-start
  148.7 1.3 fusion.2
  149.9 0.0 reduce-scatter.10.cloned.1.call-update
  150.0 0.0 reduce-scatter.12.cloned.1.call-start
  150.0 1.3 fusion.3
  151.3 0.0 reduce-scatter.12.cloned.1.call-update
  151.3 0.0 reduce-scatter.14.cloned.1.call-start
  151.4 0.1 copy.51
  151.5 26.3 %all_gather.7 = bf16[32,2,3,1408]{0,1,2,3:T(2,128)(2,1)S(1)} all-gather(bf16[32,2,3,88]{0,1,2,3:T(2,128)(2,1)S(1)} %copy.51), channel_id=1, replica_groups=mesh['dp'=2,'expert'=32,'fsdp'=16] {'fsdp'}, dimensions={3}, use_global_device_ids=true | all-gather | bytes 574464 | tf_op jit(solution)/shard_map/all_gather | solution.py:55
  177.8 3.5 %copy.52 = bf16[32,2,3,1408]{3,0,2,1:T(8,128)(2,1)S(1)} copy(bf16[32,2,3,1408]{0,1,2,3:T(2,128)(2,1)S(1)} %all_gather.7) | data formatting | bytes 1081344 | tf_op jit(solution)/shard_map/all_gather | solution.py:55
  181.3 0.0 copy-start.2
  181.3 1.3 fusion
  182.6 0.0 reduce-scatter.14.cloned.1.call-update
  182.6 0.3 convolution_convert_fusion.3
  183.0 18.7 %all_to_all.42 = bf16[32,6,128]{2,1,0:T(8,128)(2,1)S(1)} all-to-all(bf16[32,6,128]{2,1,0:T(8,128)(2,1)S(1)} %copy.53), channel_id=1, replica_groups=mesh['dp'=2,'expert'=32,'fsdp'=16] {'expert'}, dimensions={0} | all-to-all | bytes 98304 | tf_op jit(solution)/shard_map/all_to_all | solution.py:78
  201.7 9.1 %reduce-scatter.18.cloned.1.call-done = bf16[128,192]{1,0:T(8,128)(2,1)} async-done(((bf16[2048,192]{1,0:T(8,128)(2,1)}), bf16[128,192]{1,0:T(8,128)(2,1)}) %reduce-scatter.18.cloned.1.call-update) | async-done | bytes 49168
  210.8 1.0 reshape.65
  211.9 0.2 copy.69
  212.0 0.6 copy.55
  212.7 9.1 %all-to-all-start.3 = ((bf16[32,6,128]{2,1,0:T(8,128)(2,1)}), bf16[32,6,128]{2,1,0:T(8,128)(2,1)S(1)}, u32[]{:S(2)}, u32[]{:S(2)}) async-start(bf16[32,6,128]{2,1,0:T(8,128)(2,1)} %copy.55), calls=%async_computation.3 | async-start | bytes 131072 | tf_op jit(solution)/shard_map/all_to_all | solution.py:81
  221.8 0.8 convolution_convert_fusion.5
  222.6 8.6 %all-to-all-done.3 = bf16[32,6,128]{2,1,0:T(8,128)(2,1)S(1)} async-done(((bf16[32,6,128]{2,1,0:T(8,128)(2,1)}), bf16[32,6,128]{2,1,0:T(8,128)(2,1)S(1)}, u32[]{:S(2)}, u32[]{:S(2)}) %all-to-all-start.3) | async-done | bytes 49184 | tf_op jit(solution)/shard_map/all_to_all | solution.py:81
  231.2 0.8 convolution_convert_fusion.4
  231.9 17.7 %reduce-scatter.10.cloned.1.call-done = bf16[2,88,1024]{2,1,0:T(8,128)(2,1)} async-done(((bf16[2,88,2048]{2,1,0:T(8,128)(2,1)}), bf16[2,88,1024]{2,1,0:T(8,128)(2,1)}) %reduce-scatter.10.cloned.1.call-update) | async-done | bytes 360464 | tf_op jit(solution)/shard_map/reduce_scatter | solution.py:101
  249.7 40.3 %reduce-scatter.12.cloned.1.call-done = bf16[2,88,1024]{2,1,0:T(8,128)(2,1)} async-done(((bf16[2,88,2048]{2,1,0:T(8,128)(2,1)}), bf16[2,88,1024]{2,1,0:T(8,128)(2,1)}) %reduce-scatter.12.cloned.1.call-update) | async-done | bytes 360464 | tf_op jit(solution)/shard_map/reduce_scatter | solution.py:104
  290.0 39.9 %reduce-scatter.14.cloned.1.call-done = bf16[2,704,128]{2,1,0:T(8,128)(2,1)} async-done(((bf16[2,1408,128]{2,1,0:T(8,128)(2,1)}), bf16[2,704,128]{2,1,0:T(8,128)(2,1)}) %reduce-scatter.14.cloned.1.call-update) | async-done | bytes 360464 | tf_op jit(solution)/shard_map/reduce_scatter | solution.py:108
  (16 shorter events, 0.2 us)
Async XLA Ops:
  7.2 127.3 %copy-start = (bf16[2,88,2048]{2,1,0:T(8,128)(2,1)S(1)}, bf16[2,88,2048]{2,1,0:T(8,128)(2,1)}, u32[]{:S(2)}) copy-start(bf16[2,88,2048]{2,1,0:T(8,128)(2,1)} %param.12) | copy-start | bytes 2162692
  12.8 43.9 %all-to-all-start.2 = ((bf16[32,6,128]{2,1,0:T(8,128)(2,1)}), bf16[32,6,128]{2,1,0:T(8,128)(2,1)S(1)}, u32[]{:S(2)}, u32[]{:S(2)}) async-start(bf16[32,6,128]{2,1,0:T(8,128)(2,1)} %all_to_all.33), calls=%async_computation.2 | async-start | bytes 131072 | tf_op jit(solution)/shard_map/all_to_all | solution.py:47
  55.5 11.1 %copy-start.1 = (bf16[2,1408,128]{2,1,0:T(8,128)(2,1)S(1)}, bf16[2,1408,128]{2,1,0:T(8,128)(2,1)}, u32[]{:S(2)}) copy-start(bf16[2,1408,128]{2,1,0:T(8,128)(2,1)} %param.13) | copy-start | bytes 2162692
  56.7 76.9 %all-to-all-start = ((bf16[32,6,2048]{2,1,0:T(8,128)(2,1)}), bf16[32,6,2048]{2,1,0:T(8,128)(2,1)S(1)}, u32[]{:S(2)}, u32[]{:S(2)}) async-start(bf16[32,6,2048]{2,1,0:T(8,128)(2,1)} %all_to_all.28), calls=%async_computation | async-start | bytes 2097152 | tf_op jit(solution)/shard_map/all_to_all | solution.py:46
  66.5 66.1 %reduce-scatter.16.cloned.1.call-start = ((), (), s32[]{:S(2)}) async-start(), calls=%async_computation.12 | async-start | bytes 765952
  76.7 57.5 %copy-start.3 = (bf16[2,88,2048]{2,1,0:T(8,128)(2,1)S(1)}, bf16[2,88,2048]{2,1,0:T(8,128)(2,1)}, u32[]{:S(2)}) copy-start(bf16[2,88,2048]{2,1,0:T(8,128)(2,1)} %param.11) | copy-start | bytes 2162692
  76.7 134.2 %reduce-scatter.18.cloned.1.call-start = ((), (), s32[]{:S(2)}) async-start(), calls=%async_computation.13 | async-start | bytes 1114112
  148.6 101.1 %reduce-scatter.10.cloned.1.call-start = ((), (), s32[]{:S(2)}) async-start(), calls=%async_computation.9 | async-start | bytes 1081344 | tf_op jit(solution)/shard_map/reduce_scatter | solution.py:101
  150.0 140.0 %reduce-scatter.12.cloned.1.call-start = ((), (), s32[]{:S(2)}) async-start(), calls=%async_computation.10 | async-start | bytes 1081344 | tf_op jit(solution)/shard_map/reduce_scatter | solution.py:104
  151.3 178.5 %reduce-scatter.14.cloned.1.call-start = ((), (), s32[]{:S(2)}) async-start(), calls=%async_computation.11 | async-start | bytes 1081344 | tf_op jit(solution)/shard_map/reduce_scatter | solution.py:108
  181.3 1.3 copy-start.2
  212.7 18.5 %all-to-all-start.3 = ((bf16[32,6,128]{2,1,0:T(8,128)(2,1)}), bf16[32,6,128]{2,1,0:T(8,128)(2,1)S(1)}, u32[]{:S(2)}, u32[]{:S(2)}) async-start(bf16[32,6,128]{2,1,0:T(8,128)(2,1)} %copy.55), calls=%async_computation.3 | async-start | bytes 131072 | tf_op jit(solution)/shard_map/all_to_all | solution.py:81
Sparse Core Ops, SparseCore 0:
  76.8 55.7 reduce-scatter.15
  148.7 62.0 reduce-scatter.17
  214.8 34.8 reduce-scatter.9
  253.9 36.0 reduce-scatter.11
  293.8 36.0 reduce-scatter.13
where the time goes:
time: 339 us; the launch traced here: 336 us
  waiting for transfers between devices  172 us (51%)
  blocking collectives  75.9 us (22%)
  local copies, waits for them, and re-layouts  33.6 us (10%)
  starting transfers between devices  30.4 us (9%)
  between operations  14 us (4%)
  matrix products  9.2 us (3%)
    unnamed x7, waiting for transfers between devices  65.1 us
    reduce_scatter x1, waiting for transfers between devices, body(): lax.psum_scatter(grad_up_w.astype(jnp.bfloat16), 'dp', scatter_dimension=...  40.3 us
    reduce_scatter x1, waiting for transfers between devices, body(): lax.psum_scatter(grad_down_w.astype(jnp.bfloat16), 'dp', scatter_dimensio...  39.9 us
    all_gather x1, blocking collectives, body(): full_rows = lax.all_gather(tokens, 'fsdp', axis=1, tiled=True)  30.9 us
    unnamed x18, local copies, waits for them, and re-layouts  26.5 us
    all_gather x1, blocking collectives, body(): hidden_all = lax.all_gather(hidden, 'fsdp', axis=3, tiled=True)  26.3 us
    all_to_all x1, blocking collectives, body(): lax.all_to_all(expert_out.reshape(slot_count, -1), 'expert', split_axis=0...  18.7 us
    reduce_scatter x1, waiting for transfers between devices, body(): lax.psum_scatter(grad_gate_w.astype(jnp.bfloat16), 'dp', scatter_dimensio...  17.7 us
  transfers between devices with their start and end apart: 8, of which 6 were waited for; matrix products, arithmetic and copies ran while one was open for 7% of the time, Pallas kernels for 0%

commit v1 on v0

--- a/solution.py
+++ b/solution.py
@@ -11,6 +11,18 @@
 def silu_parts(pre_act):
     sigmoid_value = jax.nn.sigmoid(pre_act)
     return (pre_act * sigmoid_value, sigmoid_value * (1.0 + pre_act * (1.0 - sigmoid_value)))
+
+
+def dp_reduce(part, axis):
+    groups = lax.axis_size("dp")
+    if groups != 2:
+        return lax.psum_scatter(part, "dp", scatter_dimension=axis, tiled=True)
+    me = lax.axis_index("dp")
+    halves = jnp.stack(jnp.split(part, 2, axis=axis))
+    keep = lax.dynamic_index_in_dim(halves, me, 0, keepdims=False)
+    send = lax.dynamic_index_in_dim(halves, 1 - me, 0, keepdims=False)
+    got = lax.ppermute(send, "dp", perm=[(0, 1), (1, 0)])
+    return (keep.astype(jnp.float32) + got.astype(jnp.float32)).astype(jnp.bfloat16)
 
 
 def body(tokens, grad_out, expert_ids, gate_weights, w_gate, w_up, w_down):
@@ -42,10 +54,11 @@
     outgoing = jnp.dot(picker_half, full_rows, preferred_element_type=jnp.float32).astype(
         jnp.bfloat16
     )
-    rows_in, grads_in = (
-        lax.all_to_all(outgoing, "expert", split_axis=0, concat_axis=0, tiled=True),
-        lax.all_to_all(scaled_grad, "expert", split_axis=0, concat_axis=0, tiled=True),
+    both_in = lax.all_to_all(
+        jnp.concatenate([outgoing, scaled_grad], axis=1),
+        "expert", split_axis=0, concat_axis=0, tiled=True,
     )
+    rows_in, grads_in = both_in[:, :model_width], both_in[:, model_width:]
     received = rows_in.reshape(owners, exp_local, capacity, model_width)
     cotangent = grads_in.reshape(owners, exp_local, capacity, -1)
     gate_pre = jnp.einsum("jecd,efd->jecf", received, w_gate, preferred_element_type=jnp.float32)
@@ -74,14 +87,14 @@
     input_slices = lax.psum_scatter(
         input_parts.astype(jnp.bfloat16), "fsdp", scatter_dimension=3, tiled=True
     )
-    mixed_slots, input_slots = (
-        lax.all_to_all(
-            expert_out.reshape(slot_count, -1), "expert", split_axis=0, concat_axis=0, tiled=True
+    feat = input_slices.shape[-1]
+    both_back = lax.all_to_all(
+        jnp.concatenate(
+            [expert_out.reshape(slot_count, -1), input_slices.reshape(slot_count, -1)], axis=1
         ),
-        lax.all_to_all(
-            input_slices.reshape(slot_count, -1), "expert", split_axis=0, concat_axis=0, tiled=True
-        ),
+        "expert", split_axis=0, concat_axis=0, tiled=True,
     )
+    mixed_slots, input_slots = both_back[:, :feat], both_back[:, feat:]
     mixed = jnp.dot(
         weighted.T, mixed_slots.astype(jnp.float32), precision=lax.Precision.HIGHEST
     ).astype(jnp.bfloat16)
@@ -97,17 +110,9 @@
     grad_down_w = rounded(
         jnp.einsum("jecf,jecd->efd", hidden_all, cotangent, preferred_element_type=jnp.float32)
     )
-    summed_gate, summed_up = (
-        lax.psum_scatter(
-            grad_gate_w.astype(jnp.bfloat16), "dp", scatter_dimension=2, tiled=True
-        ).astype(jnp.float32),
-        lax.psum_scatter(
-            grad_up_w.astype(jnp.bfloat16), "dp", scatter_dimension=2, tiled=True
-        ).astype(jnp.float32),
-    )
-    summed_down = lax.psum_scatter(
-        grad_down_w.astype(jnp.bfloat16), "dp", scatter_dimension=1, tiled=True
-    )
+    summed_gate = dp_reduce(grad_gate_w.astype(jnp.bfloat16), 2).astype(jnp.float32)
+    summed_up = dp_reduce(grad_up_w.astype(jnp.bfloat16), 2).astype(jnp.float32)
+    summed_down = dp_reduce(grad_down_w.astype(jnp.bfloat16), 1)
     return (
         mixed,
         grad_tokens,

time: 339 us -> 280 us (0.83)
  waiting for transfers between devices: 172 us -> 75.6 us
  blocking collectives: 75.9 us -> 99.2 us
  other arithmetic: 1.69 us -> 9.23 us
  matrix products: 9.2 us -> 14.1 us
  starting transfers between devices: 30.4 us -> 25.7 us
  local copies, waits for them, and re-layouts: 33.6 us -> 37.7 us
    reduce_scatter x3 -> x0, waiting for transfers between devices: 97.9 us -> none  [the longest x1 40.3 us: body(): lax.psum_scatter(grad_up_w.astype(jnp.bfloat16), 'dp', scatter_dimension=...]
    all_to_all x1, blocking collectives: 18.7 us -> 40.7 us  [body(): lax.all_to_all(jnp.concatenate([outgoing, scaled_grad], axis=1), 'expert'...]
    all_to_all x3 -> x1, starting transfers between devices: 30.2 us -> 9.25 us  [body(): lax.all_to_all(jnp.concatenate([expert_out.reshape(slot_count, -1), input...]
    ppermute x0 -> x3, starting transfers between devices: none -> 16.3 us  [dp_reduce(): got = lax.ppermute(send, 'dp', perm=[(0, 1), (1, 0)])]
    convert_element_type x0 -> x3, other arithmetic: none -> 4.86 us  [dp_reduce(): (keep.astype(jnp.float32) + got.astype(jnp.float32)).astype(jnp.bfloat16)]
    unnamed x18 -> x46, local copies, waits for them, and re-layouts: 26.5 us -> 29.3 us
    unnamed x7 -> x4, waiting for transfers between devices: 65.1 us -> 66.7 us
    all_to_all x3 -> x1, waiting for transfers between devices: 8.59 us -> 8.93 us  [body(): lax.all_to_all(jnp.concatenate([expert_out.reshape(slot_count, -1), input...]
  transfers between devices with their start and end apart: 8 -> 6, of which waited for: 6 -> 3; matrix products, arithmetic and copies ran while one was open for 7% -> 12% of each run, Pallas kernels for 0% -> 0%
where the time goes in v1:
time: 280 us; the launch traced here: 276 us
  blocking collectives  99.2 us (35%)
  waiting for transfers between devices  75.6 us (27%)
  local copies, waits for them, and re-layouts  37.7 us (13%)
  starting transfers between devices  25.7 us (9%)
  between operations  14.5 us (5%)
  matrix products  14.1 us (5%)
  other arithmetic  9.23 us (3%)
    unnamed x4, waiting for transfers between devices  66.7 us
    all_to_all x1, blocking collectives, body(): lax.all_to_all(jnp.concatenate([outgoing, scaled_grad], axis=1), 'expert'...  40.7 us
    all_gather x1, blocking collectives, body(): full_rows = lax.all_gather(tokens, 'fsdp', axis=1, tiled=True)  31.4 us
    unnamed x46, local copies, waits for them, and re-layouts  29.3 us
    all_gather x1, blocking collectives, body(): hidden_all = lax.all_gather(hidden, 'fsdp', axis=3, tiled=True)  27.1 us
    ppermute x3, starting transfers between devices, dp_reduce(): got = lax.ppermute(send, 'dp', perm=[(0, 1), (1, 0)])  16.3 us
    all_to_all x1, starting transfers between devices, body(): lax.all_to_all(jnp.concatenate([expert_out.reshape(slot_count, -1), input...  9.25 us
    all_to_all x1, waiting for transfers between devices, body(): lax.all_to_all(jnp.concatenate([expert_out.reshape(slot_count, -1), input...  8.93 us
  transfers between devices with their start and end apart: 6, of which 3 were waited for; matrix products, arithmetic and copies ran while one was open for 12% of the time, Pallas kernels for 0%

profile of v1, /device:TPU:1, one launch (start us, length us, event | category | flops | bytes accessed | tf_op | source)
XLA Modules:
  0.0 276.0 jit_solution(3474357881058562684)
XLA Ops:
  7.2 0.0 reduce-scatter.7.cloned.1.call-start
  7.2 0.8 copy.56
  8.1 0.1 eq.35
  8.2 0.6 reduce-window.6
  8.8 0.2 slice_reduce_fusion
  9.0 0.1 bitcast_bitcast_fusion
  9.2 0.1 reduce_sum.21
  9.3 0.1 copy.59
  9.4 0.7 multiply_add_fusion
  10.1 0.1 convert_reduce_fusion
  10.2 0.1 iota_compare_fusion
  10.3 0.8 copy.72
  11.0 31.4 %all_gather.6 = bf16[32,2048]{1,0:T(8,128)(2,1)S(1)} all-gather(bf16[32,128]{1,0:T(8,128)(2,1)} %param.7), channel_id=1, replica_groups=mesh['dp'=2,'expert'=32,'fsdp'=16] {'fsdp'}, dimensions={1}, use_global_device_ids=true | all-gather | bytes 139264 | tf_op jit(solution)/shard_map/all_gather | solution.py:53
  42.5 0.3 fusion.28
  42.8 1.0 convolution_convert_fusion.3
  43.8 0.4 convolution_convert_fusion.1
  44.1 0.1 pad_maximum_fusion
  44.2 0.3 all_to_all.14
  44.5 40.7 %all_to_all.21 = bf16[32,6,2176]{2,1,0:T(8,128)(2,1)S(1)} all-to-all(bf16[32,6,2176]{2,1,0:T(8,128)(2,1)S(1)} %all_to_all.14), channel_id=1, replica_groups=mesh['dp'=2,'expert'=32,'fsdp'=16] {'expert'}, dimensions={0} | all-to-all | bytes 1671168 | tf_op jit(solution)/shard_map/all_to_all | solution.py:57
  85.2 0.3 all_to_all.16
  85.5 1.5 fusion.4
  87.1 3.6 %copy.80 = bf16[32,2,3,1408]{0,2,1,3:T(4,128)(2,1)} copy(bf16[32,2,3,1408]{3,0,2,1:T(8,128)(2,1)S(1)} %fusion.4) | data formatting | bytes 1081344
  90.7 6.1 %reshape.67 = bf16[1408,192]{1,0:T(8,128)(2,1)} reshape(bf16[1408,2,3,32]{3,2,1,0:T(4,128)(2,1)} %bitcast.116) | data formatting | bytes 1081344
  96.7 0.0 reduce-scatter.7.cloned.1.call-update
  96.8 0.0 reduce-scatter.9.cloned.1.call-start
  96.8 0.1 slice.30
  96.9 0.5 reshape.53
  97.4 0.5 copy-done.7
  97.9 0.8 convolution_bitcast_fusion.4
  98.7 50.4 %reduce-scatter.7.cloned.1.call-done = bf16[88,192]{1,0:T(8,128)(2,1)} async-done(((bf16[1408,192]{1,0:T(8,128)(2,1)}), bf16[88,192]{1,0:T(8,128)(2,1)}) %reduce-scatter.7.cloned.1.call-update) | async-done | bytes 33808
  149.1 0.9 reshape.68
  150.0 0.1 copy.81
  150.2 1.7 fusion.3
  151.9 1.4 multiply_convert_fusion
  153.3 0.8 fusion.2
  154.2 0.4 fusion.11
  154.5 0.4 copy-done.17
  154.9 0.1 copy.62
  155.1 0.1 slice_bitcast_fusion.4
  155.2 1.4 slice_bitcast_fusion.2
  156.6 0.9 fusion.25
  157.5 6.6 %collective-permute-start = (bf16[2,88,1024]{2,1,0:T(8,128)(2,1)}, bf16[2,88,1024]{2,1,0:T(8,128)(2,1)}, u32[]{:S(2)}, u32[]{:S(2)}) collective-permute-start(bf16[2,88,1024]{2,1,0:T(8,128)(2,1)} %fusion.25), channel_id=1, source_target_pairs={{0,512},{512,0},{1,513},{513,1},{2,514},{514,2},{3,515},{515,3},{4... | collective-permute-start | bytes 1081352 | tf_op jit(solution)/shard_map/ppermute | solution.py:24
  164.1 0.9 fusion.21
  165.0 2.6 collective-permute-start.1
  167.6 1.3 fusion.5
  168.9 6.6 %copy.82 = bf16[32,2,3,2048]{0,2,1,3:T(4,128)(2,1)} copy(bf16[32,2,3,2048]{3,0,2,1:T(8,128)(2,1)} %fusion.5) | data formatting | bytes 1572864
  175.6 8.2 %reshape.69 = bf16[2048,192]{1,0:T(8,128)(2,1)} reshape(bf16[2048,2,3,32]{3,2,1,0:T(4,128)(2,1)} %bitcast.115) | data formatting | bytes 1572864
  183.7 27.1 %all_gather.7 = bf16[32,2,3,1408]{0,1,2,3:T(2,128)(2,1)S(1)} all-gather(bf16[32,2,3,88]{0,1,2,3:T(2,128)(2,1)S(1)} %copy.62), channel_id=1, replica_groups=mesh['dp'=2,'expert'=32,'fsdp'=16] {'fsdp'}, dimensions={3}, use_global_device_ids=true | all-gather | bytes 574464 | tf_op jit(solution)/shard_map/all_gather | solution.py:68
  210.8 5.0 %copy.63 = bf16[32,2,3,1408]{3,0,2,1:T(8,128)(2,1)} copy(bf16[32,2,3,1408]{0,1,2,3:T(2,128)(2,1)S(1)} %all_gather.7) | data formatting | bytes 1081344 | tf_op jit(solution)/shard_map/all_gather | solution.py:68
  215.8 1.6 convolution_convert_fusion.2
  217.4 1.5 fusion
  219.0 0.1 fusion.17
  219.1 7.2 %collective-permute-start.2 = (bf16[2,704,128]{2,1,0:T(8,128)(2,1)S(1)}, bf16[2,704,128]{2,1,0:T(8,128)(2,1)S(1)}, u32[]{:S(2)}, u32[]{:S(2)}) collective-permute-start(bf16[2,704,128]{2,1,0:T(8,128)(2,1)S(1)} %fusion.17), channel_id=1, source_target_pairs={{0,512},{512,0},{1,513},{513,1},{2,514},{514,2},{3,515},{515,3},{4... | collective-permute-start | bytes 1081352 | tf_op jit(solution)/shard_map/ppermute | solution.py:24
  226.3 2.0 fusion.8
  228.3 2.0 fusion.7
  230.3 16.3 %reduce-scatter.9.cloned.1.call-done = bf16[128,192]{1,0:T(8,128)(2,1)} async-done(((bf16[2048,192]{1,0:T(8,128)(2,1)}), bf16[128,192]{1,0:T(8,128)(2,1)}) %reduce-scatter.9.cloned.1.call-update) | async-done | bytes 49168
  246.5 1.0 reshape.70
  247.6 0.2 copy.83
  247.8 0.7 pad_maximum_fusion.1
  248.4 9.2 %all-to-all-start.1 = ((bf16[32,6,256]{2,1,0:T(8,128)(2,1)}), bf16[32,6,256]{2,1,0:T(8,128)(2,1)S(1)}, u32[]{:S(2)}, u32[]{:S(2)}) async-start(bf16[32,6,256]{2,1,0:T(8,128)(2,1)} %pad_maximum_fusion.1), calls=%async_computation.1 | async-start | bytes 262144 | tf_op jit(solution)/shard_map/all_to_all | solution.py:91
  257.7 0.9 fusion.6
  258.6 8.9 %all-to-all-done.1 = bf16[32,6,256]{2,1,0:T(8,128)(2,1)S(1)} async-done(((bf16[32,6,256]{2,1,0:T(8,128)(2,1)}), bf16[32,6,256]{2,1,0:T(8,128)(2,1)S(1)}, u32[]{:S(2)}, u32[]{:S(2)}) %all-to-all-start.1) | async-done | bytes 98336 | tf_op jit(solution)/shard_map/all_to_all | solution.py:91
  267.6 0.8 convolution_convert_fusion.4
  268.4 0.8 convolution_convert_fusion.5
  (49 shorter events, 0.4 us)
Async XLA Ops:
  7.2 144.7 %copy-start = (bf16[2,88,2048]{2,1,0:T(8,128)(2,1)S(1)}, bf16[2,88,2048]{2,1,0:T(8,128)(2,1)}, u32[]{:S(2)}) copy-start(bf16[2,88,2048]{2,1,0:T(8,128)(2,1)} %param.12) | copy-start | bytes 2162692
  7.2 141.9 %reduce-scatter.7.cloned.1.call-start = ((), (), s32[]{:S(2)}) async-start(), calls=%async_computation.4 | async-start | bytes 765952
  42.8 1.5 copy-start.15
  85.5 5.1 %copy-start.13 = (bf16[32,2,3,128]{3,2,1,0:T(4,128)(2,1)}, bf16[32,2,3,128]{3,2,1,0:T(4,128)(2,1)S(1)}, u32[]{:S(2)}) copy-start(bf16[32,2,3,128]{3,2,1,0:T(4,128)(2,1)S(1)} %reshape.54) | copy-start | bytes 147460
  96.8 149.8 %reduce-scatter.9.cloned.1.call-start = ((), (), s32[]{:S(2)}) async-start(), calls=%async_computation.5 | async-start | bytes 1114112
  96.8 1.1 copy-start.7
  98.7 54.6 %copy-start.11 = (f32[32,2,3,88]{3,0,2,1:T(8,128)}, f32[32,2,3,88]{3,0,2,1:T(8,128)S(1)}, u32[]{:S(2)}) copy-start(f32[32,2,3,88]{3,0,2,1:T(8,128)S(1)} %convolution_bitcast_fusion.4) | copy-start | bytes 202756
  150.2 3.1 %copy-start.9 = (bf16[32,2,3,88]{3,0,2,1:T(8,128)(2,1)}, bf16[32,2,3,88]{3,0,2,1:T(8,128)(2,1)S(1)}, u32[]{:S(2)}) copy-start(bf16[32,2,3,88]{3,0,2,1:T(8,128)(2,1)S(1)} %copy.81) | copy-start | bytes 101380
  151.9 2.2 copy-start.8
  154.1 0.8 copy-start.17
  155.1 9.9 %copy-start.3 = (bf16[1,2,88,1024]{3,2,1,0:T(8,128)(2,1)}, bf16[1,2,88,1024]{3,2,1,0:T(8,128)(2,1)S(1)}, u32[]{:S(2)}) copy-start(bf16[1,2,88,1024]{3,2,1,0:T(8,128)(2,1)S(1)} %get-tuple-element.9) | copy-start | bytes 1081348
  155.2 9.9 %copy-start.5 = (bf16[1,2,88,1024]{3,2,1,0:T(8,128)(2,1)}, bf16[1,2,88,1024]{3,2,1,0:T(8,128)(2,1)S(1)}, u32[]{:S(2)}) copy-start(bf16[1,2,88,1024]{3,2,1,0:T(8,128)(2,1)S(1)} %get-tuple-element.10) | copy-start | bytes 1081348
  155.2 12.4 %copy-start.10 = (bf16[32,2,3,88]{3,0,2,1:T(8,128)(2,1)S(1)}, bf16[32,2,3,88]{3,0,2,1:T(8,128)(2,1)}, u32[]{:S(2)}) copy-start(bf16[32,2,3,88]{3,0,2,1:T(8,128)(2,1)} %copy-done.9) | copy-start | bytes 101380
  155.2 12.4 %copy-start.12 = (f32[32,2,3,88]{3,0,2,1:T(8,128)S(1)}, f32[32,2,3,88]{3,0,2,1:T(8,128)}, u32[]{:S(2)}) copy-start(f32[32,2,3,88]{3,0,2,1:T(8,128)} %copy-done.11) | copy-start | bytes 202756
  156.6 12.3 %copy-start.1 = (bf16[1,2,88,1024]{3,2,1,0:T(8,128)(2,1)}, bf16[1,2,88,1024]{3,2,1,0:T(8,128)(2,1)S(1)}, u32[]{:S(2)}) copy-start(bf16[1,2,88,1024]{3,2,1,0:T(8,128)(2,1)S(1)} %get-tuple-element.8) | copy-start | bytes 1081348
  157.5 68.8 %collective-permute-start = (bf16[2,88,1024]{2,1,0:T(8,128)(2,1)}, bf16[2,88,1024]{2,1,0:T(8,128)(2,1)}, u32[]{:S(2)}, u32[]{:S(2)}) collective-permute-start(bf16[2,88,1024]{2,1,0:T(8,128)(2,1)} %fusion.25), channel_id=1, source_target_pairs={{0,512},{512,0},{1,513},{513,1},{2,514},{514,2},{3,515},{515,3},{4... | collective-permute-start | bytes 1081352 | tf_op jit(solution)/shard_map/ppermute | solution.py:24
  165.0 63.3 %collective-permute-start.1 = (bf16[2,88,1024]{2,1,0:T(8,128)(2,1)}, bf16[2,88,1024]{2,1,0:T(8,128)(2,1)}, u32[]{:S(2)}, u32[]{:S(2)}) collective-permute-start(bf16[2,88,1024]{2,1,0:T(8,128)(2,1)} %fusion.21), channel_id=1, source_target_pairs={{0,512},{512,0},{1,513},{513,1},{2,514},{514,2},{3,515},{515,3},{4... | collective-permute-start | bytes 1081352 | tf_op jit(solution)/shard_map/ppermute | solution.py:24
  210.8 6.6 %copy-start.14 = (bf16[32,2,3,128]{3,2,1,0:T(4,128)(2,1)S(1)}, bf16[32,2,3,128]{3,2,1,0:T(4,128)(2,1)}, u32[]{:S(2)}) copy-start(bf16[32,2,3,128]{3,2,1,0:T(4,128)(2,1)} %copy-done.13) | copy-start | bytes 147460
  218.9 7.4 %copy-start.4 = (bf16[1,2,88,1024]{3,2,1,0:T(8,128)(2,1)S(1)}, bf16[1,2,88,1024]{3,2,1,0:T(8,128)(2,1)}, u32[]{:S(2)}) copy-start(bf16[1,2,88,1024]{3,2,1,0:T(8,128)(2,1)} %copy-done.3) | copy-start | bytes 1081348
  218.9 7.4 %copy-start.6 = (bf16[1,2,88,1024]{3,2,1,0:T(8,128)(2,1)S(1)}, bf16[1,2,88,1024]{3,2,1,0:T(8,128)(2,1)}, u32[]{:S(2)}) copy-start(bf16[1,2,88,1024]{3,2,1,0:T(8,128)(2,1)} %copy-done.5) | copy-start | bytes 1081348
  219.0 9.3 %copy-start.2 = (bf16[1,2,88,1024]{3,2,1,0:T(8,128)(2,1)S(1)}, bf16[1,2,88,1024]{3,2,1,0:T(8,128)(2,1)}, u32[]{:S(2)}) copy-start(bf16[1,2,88,1024]{3,2,1,0:T(8,128)(2,1)} %copy-done.1) | copy-start | bytes 1081348
  219.1 38.6 %collective-permute-start.2 = (bf16[2,704,128]{2,1,0:T(8,128)(2,1)S(1)}, bf16[2,704,128]{2,1,0:T(8,128)(2,1)S(1)}, u32[]{:S(2)}, u32[]{:S(2)}) collective-permute-start(bf16[2,704,128]{2,1,0:T(8,128)(2,1)S(1)} %fusion.17), channel_id=1, source_target_pairs={{0,512},{512,0},{1,513},{513,1},{2,514},{514,2},{3,515},{515,3},{4... | collective-permute-start | bytes 1081352 | tf_op jit(solution)/shard_map/ppermute | solution.py:24
  230.3 38.1 %copy-start.16 = (f32[32,1,192]{2,1,0:T(1,128)S(1)}, f32[32,1,192]{2,1,0:T(1,128)}, u32[]{:S(2)}) copy-start(f32[32,1,192]{2,1,0:T(1,128)} %copy-done.15) | copy-start | bytes 73732
  248.4 19.1 %all-to-all-start.1 = ((bf16[32,6,256]{2,1,0:T(8,128)(2,1)}), bf16[32,6,256]{2,1,0:T(8,128)(2,1)S(1)}, u32[]{:S(2)}, u32[]{:S(2)}) async-start(bf16[32,6,256]{2,1,0:T(8,128)(2,1)} %pad_maximum_fusion.1), calls=%async_computation.1 | async-start | bytes 262144 | tf_op jit(solution)/shard_map/all_to_all | solution.py:91
Sparse Core Ops, SparseCore 0:
  96.9 52.1 reduce-scatter.6
  183.9 62.6 reduce-scatter.8

commit v2 on v1

--- a/solution.py
+++ b/solution.py
@@ -69,24 +69,28 @@
     expert_out = jnp.einsum(
         "jecf,efd->jecd", hidden_all, w_down, preferred_element_type=jnp.float32
     ).astype(jnp.bfloat16)
-    hidden_parts = rounded(
-        jnp.einsum("jecd,efd->jecf", cotangent, w_down, preferred_element_type=jnp.float32)
+    shards = lax.axis_size("fsdp")
+    exp_n, ff_all, feat = w_down.shape
+    hidden_parts = jnp.einsum(
+        "jecd,egfd->gjecf", cotangent, w_down.reshape(exp_n, shards, ff_all // shards, feat),
+        preferred_element_type=jnp.float32,
+    ).astype(jnp.bfloat16)
+    grad_hidden = jnp.sum(
+        lax.all_to_all(hidden_parts, "fsdp", 0, 0, tiled=False).astype(jnp.float32), axis=0
     )
-    grad_hidden = lax.psum_scatter(
-        hidden_parts.astype(jnp.bfloat16), "fsdp", scatter_dimension=3, tiled=True
-    ).astype(jnp.float32)
     grad_gate_pre = (grad_hidden * up_pre * slope_term).astype(jnp.bfloat16)
     grad_up_pre = (grad_hidden * activation).astype(jnp.bfloat16)
+    w_gate_g = w_gate.reshape(exp_n, w_gate.shape[1], shards, model_width // shards)
+    w_up_g = w_up.reshape(exp_n, w_up.shape[1], shards, model_width // shards)
     input_parts = jnp.einsum(
-        "jecf,efd->jecd", grad_gate_pre, w_gate, preferred_element_type=jnp.float32
-    )
-    input_parts = rounded(
-        input_parts
-        + jnp.einsum("jecf,efd->jecd", grad_up_pre, w_up, preferred_element_type=jnp.float32)
-    )
-    input_slices = lax.psum_scatter(
-        input_parts.astype(jnp.bfloat16), "fsdp", scatter_dimension=3, tiled=True
-    )
+        "jecf,efgd->gjecd", grad_gate_pre, w_gate_g, preferred_element_type=jnp.float32
+    ) + jnp.einsum("jecf,efgd->gjecd", grad_up_pre, w_up_g, preferred_element_type=jnp.float32)
+    input_slices = jnp.sum(
+        lax.all_to_all(input_parts.astype(jnp.bfloat16), "fsdp", 0, 0, tiled=False).astype(
+            jnp.float32
+        ),
+        axis=0,
+    ).astype(jnp.bfloat16)
     feat = input_slices.shape[-1]
     both_back = lax.all_to_all(
         jnp.concatenate(

time: 280 us -> 207 us (0.74)
  waiting for transfers between devices: 75.6 us -> 26.1 us
  local copies, waits for them, and re-layouts: 37.7 us -> 16.7 us
  between operations: 14.5 us -> 1.03 us
  blocking collectives: 99.2 us -> 111 us
    unnamed x4 -> x0, waiting for transfers between devices: 66.7 us -> none
    unnamed x46 -> x26, local copies, waits for them, and re-layouts: 29.3 us -> 3.96 us
    all_to_all x0 -> x2, waiting for transfers between devices: none -> 14.1 us  [the longest x1 14.1 us: body(): lax.all_to_all(hidden_parts, 'fsdp', 0, 0, tiled=False).astype(jnp.float32)]
    all_gather x1, blocking collectives: 27.1 us -> 38.7 us  [body(): hidden_all = lax.all_gather(hidden, 'fsdp', axis=3, tiled=True)]
    ppermute x3, waiting for transfers between devices: 0.01 us -> 9.53 us  [dp_reduce(): got = lax.ppermute(send, 'dp', perm=[(0, 1), (1, 0)])]
    all_to_all x0 -> x2, starting transfers between devices: none -> 9.42 us  [the longest x1 5.25 us: body(): lax.all_to_all(hidden_parts, 'fsdp', 0, 0, tiled=False).astype(jnp.float32)]
    all_to_all x1, waiting for transfers between devices: 8.93 us -> 2.54 us  [body(): lax.all_to_all(jnp.concatenate([expert_out.reshape(slot_count, -1), input...]
    all_to_all x1, starting transfers between devices: 9.25 us -> 3.84 us  [body(): lax.all_to_all(jnp.concatenate([expert_out.reshape(slot_count, -1), input...]
  transfers between devices with their start and end apart: 6 -> 6, of which waited for: 3 -> 3; matrix products, arithmetic and copies ran while one was open for 12% -> 13% of each run, Pallas kernels for 0% -> 0%
where the time goes in v2:
time: 207 us; the launch traced here: 206 us
  blocking collectives  111 us (54%)
  starting transfers between devices  26.8 us (13%)
  waiting for transfers between devices  26.1 us (13%)
  local copies, waits for them, and re-layouts  16.7 us (8%)
  matrix products  13.3 us (6%)
  other arithmetic  10.7 us (5%)
    all_to_all x1, blocking collectives, body(): lax.all_to_all(jnp.concatenate([outgoing, scaled_grad], axis=1), 'expert'...  40.7 us
    all_gather x1, blocking collectives, body(): hidden_all = lax.all_gather(hidden, 'fsdp', axis=3, tiled=True)  38.7 us
    all_gather x1, blocking collectives, body(): full_rows = lax.all_gather(tokens, 'fsdp', axis=1, tiled=True)  31.4 us
    all_to_all x1, waiting for transfers between devices, body(): lax.all_to_all(hidden_parts, 'fsdp', 0, 0, tiled=False).astype(jnp.float32)  14.1 us
    ppermute x3, starting transfers between devices, dp_reduce(): got = lax.ppermute(send, 'dp', perm=[(0, 1), (1, 0)])  13.6 us
    ppermute x3, waiting for transfers between devices, dp_reduce(): got = lax.ppermute(send, 'dp', perm=[(0, 1), (1, 0)])  9.53 us
    all_to_all x1, starting transfers between devices, body(): lax.all_to_all(hidden_parts, 'fsdp', 0, 0, tiled=False).astype(jnp.float32)  5.25 us
    all_gather x1, local copies, waits for them, and re-layouts, body(): hidden_all = lax.all_gather(hidden, 'fsdp', axis=3, tiled=True)  4.97 us
  transfers between devices with their start and end apart: 6, of which 3 were waited for; matrix products, arithmetic and copies ran while one was open for 13% of the time, Pallas kernels for 0%

profile of v2, /device:TPU:1, one launch (start us, length us, event | category | flops | bytes accessed | tf_op | source)
XLA Modules:
  0.0 205.5 jit_solution(15840016763683468538)
XLA Ops:
  0.6 0.0 copy-start
  0.6 0.8 copy.78
  1.5 0.1 eq.35
  1.6 0.6 reduce-window.6
  2.2 0.2 slice_reduce_fusion
  2.5 0.1 bitcast_bitcast_fusion.2
  2.6 0.1 reduce_sum.42
  2.7 0.1 copy.81
  2.8 0.7 multiply_add_fusion
  3.5 0.1 convert_reduce_fusion.1
  3.6 0.1 iota_compare_fusion
  3.7 0.8 copy.97
  4.5 31.4 %all_gather.6 = bf16[32,2048]{1,0:T(8,128)(2,1)S(1)} all-gather(bf16[32,128]{1,0:T(8,128)(2,1)} %param.7), channel_id=1, replica_groups=mesh['dp'=2,'expert'=32,'fsdp'=16] {'fsdp'}, dimensions={1}, use_global_device_ids=true | all-gather | bytes 139264 | tf_op jit(solution)/shard_map/all_gather | solution.py:53
  35.9 0.3 fusion.26
  36.2 1.0 convolution_convert_fusion.3
  37.2 0.4 convolution_convert_fusion
  37.5 0.1 pad_maximum_fusion
  37.6 0.3 all_to_all.20
  37.9 40.7 %all_to_all.31 = bf16[32,6,2176]{2,1,0:T(8,128)(2,1)S(1)} all-to-all(bf16[32,6,2176]{2,1,0:T(8,128)(2,1)S(1)} %all_to_all.20), channel_id=1, replica_groups=mesh['dp'=2,'expert'=32,'fsdp'=16] {'expert'}, dimensions={0} | all-to-all | bytes 1671168 | tf_op jit(solution)/shard_map/all_to_all | solution.py:57
  78.6 0.3 all_to_all.22
  78.9 0.7 fusion.3
  79.7 0.0 copy-start.9
  79.7 1.0 copy.87
  80.7 5.2 %all-to-all-start.1 = ((bf16[16,32,2,3,88]{4,1,3,2,0:T(8,128)(2,1)}), bf16[16,32,2,3,88]{4,1,3,2,0:T(8,128)(2,1)S(1)}, u32[]{:S(2)}, u32[]{:S(2)}) async-start(bf16[16,32,2,3,88]{4,1,3,2,0:T(8,128)(2,1)} %copy.87), calls=%async_computation.1 | async-start | bytes 1572864 | tf_op jit(solution)/shard_map/all_to_all | solution.py:79
  85.9 1.0 copy.120
  86.9 1.3 copy.119
  88.2 2.1 %bitcast_bitcast_fusion = bf16[2,88,16,128,1]{3,2,1,0,4:T(8,128)(2,1)} fusion(bf16[2,88,16,128]{3,2,1,0:T(8,128)(2,1)} %bitcast.138), kind=kLoop, calls=%fused_computation.31 | loop fusion | bytes 1441792 | tf_op jit(solution)/shard_map/reshape | solution.py:84
  90.3 1.0 bitcast_bitcast_fusion.1
  91.3 0.1 slice.30
  91.4 0.5 reshape.62
  91.9 2.6 %convolution_bitcast_fusion.4 = f32[32,2,3,88]{3,0,2,1:T(8,128)} fusion(bf16[2,88,2048]{2,1,0:T(8,128)(2,1)} %param.11, bf16[32,2,3,2048]{3,2,1,0:T(4,128)(2,1)S(1)} %reshape.62), kind=kOutput, calls=%fused_computation.13 | convolution fusion | flops 69206016 | bytes 1574912 | tf_op jit(solution)/shard_map/jecd,efd->jecf/dot_general | solution.py:64
  94.5 14.1 %all-to-all-done.1 = bf16[16,32,2,3,88]{4,1,3,2,0:T(8,128)(2,1)S(1)} async-done(((bf16[16,32,2,3,88]{4,1,3,2,0:T(8,128)(2,1)}), bf16[16,32,2,3,88]{4,1,3,2,0:T(8,128)(2,1)S(1)}, u32[]{:S(2)}, u32[]{:S(2)}) %all-to-all-start.1) | async-done | bytes 540704 | tf_op jit(solution)/shard_map/all_to_all | solution.py:79
  108.6 0.2 convert_reduce_fusion
  108.8 1.7 multiply_convert_fusion.2
  110.5 0.1 copy.84
  110.6 0.8 fusion.1
  111.4 0.8 fusion.2
  112.2 0.1 slice_bitcast_fusion.4
  112.3 0.0 copy-start.3
  112.3 0.1 slice_bitcast_fusion.2
  112.4 0.9 fusion.23
  113.3 4.4 %collective-permute-start = (bf16[2,88,1024]{2,1,0:T(8,128)(2,1)}, bf16[2,88,1024]{2,1,0:T(8,128)(2,1)}, u32[]{:S(2)}, u32[]{:S(2)}) collective-permute-start(bf16[2,88,1024]{2,1,0:T(8,128)(2,1)} %fusion.23), channel_id=1, source_target_pairs={{0,512},{512,0},{1,513},{513,1},{2,514},{514,2},{3,515},{515,3},{4... | collective-permute-start | bytes 1081352 | tf_op jit(solution)/shard_map/ppermute | solution.py:24
  117.7 0.9 fusion.19
  118.6 4.8 %collective-permute-start.1 = (bf16[2,88,1024]{2,1,0:T(8,128)(2,1)}, bf16[2,88,1024]{2,1,0:T(8,128)(2,1)}, u32[]{:S(2)}, u32[]{:S(2)}) collective-permute-start(bf16[2,88,1024]{2,1,0:T(8,128)(2,1)} %fusion.19), channel_id=1, source_target_pairs={{0,512},{512,0},{1,513},{513,1},{2,514},{514,2},{3,515},{515,3},{4... | collective-permute-start | bytes 1081352 | tf_op jit(solution)/shard_map/ppermute | solution.py:24
  123.4 0.4 fusion.12
  123.8 0.4 fusion.4
  124.1 1.0 copy.90
  125.1 4.2 %all-to-all-start.2 = ((bf16[16,32,2,3,128]{4,1,3,2,0:T(8,128)(2,1)}), bf16[16,32,2,3,128]{4,1,3,2,0:T(8,128)(2,1)}, u32[]{:S(2)}, u32[]{:S(2)}) async-start(bf16[16,32,2,3,128]{4,1,3,2,0:T(8,128)(2,1)} %copy.90), calls=%async_computation.2 | async-start | bytes 1572864 | tf_op jit(solution)/shard_map/all_to_all | solution.py:89
  129.3 38.7 %all_gather.7 = bf16[32,2,3,1408]{0,1,2,3:T(2,128)(2,1)S(1)} all-gather(bf16[32,2,3,88]{0,1,2,3:T(2,128)(2,1)S(1)} %copy.84), channel_id=1, replica_groups=mesh['dp'=2,'expert'=32,'fsdp'=16] {'fsdp'}, dimensions={3}, use_global_device_ids=true | all-gather | bytes 574464 | tf_op jit(solution)/shard_map/all_gather | solution.py:68
  168.0 5.0 %copy.85 = bf16[32,2,3,1408]{3,0,2,1:T(8,128)(2,1)} copy(bf16[32,2,3,1408]{0,1,2,3:T(2,128)(2,1)S(1)} %all_gather.7) | data formatting | bytes 1081344 | tf_op jit(solution)/shard_map/all_gather | solution.py:68
  172.9 1.5 fusion
  174.4 1.4 convolution_convert_fusion.2
  175.8 0.9 fusion.15
  176.7 4.4 %collective-permute-start.2 = (bf16[2,704,128]{2,1,0:T(8,128)(2,1)}, bf16[2,704,128]{2,1,0:T(8,128)(2,1)S(1)}, u32[]{:S(2)}, u32[]{:S(2)}) collective-permute-start(bf16[2,704,128]{2,1,0:T(8,128)(2,1)} %fusion.15), channel_id=1, source_target_pairs={{0,512},{512,0},{1,513},{513,1},{2,514},{514,2},{3,515},{515,3},{4... | collective-permute-start | bytes 1081352 | tf_op jit(solution)/shard_map/ppermute | solution.py:24
  181.2 2.0 fusion.7
  183.1 2.0 fusion.6
  185.1 1.2 reduce_sum.45
  186.4 0.7 copy.91
  187.1 3.8 %all-to-all-start.3 = ((bf16[32,6,256]{2,1,0:T(8,128)(2,1)}), bf16[32,6,256]{2,1,0:T(8,128)(2,1)S(1)}, u32[]{:S(2)}, u32[]{:S(2)}) async-start(bf16[32,6,256]{2,1,0:T(8,128)(2,1)} %copy.91), calls=%async_computation.3 | async-start | bytes 262144 | tf_op jit(solution)/shard_map/all_to_all | solution.py:95
  190.9 9.5 %collective-permute-done.2 = bf16[2,704,128]{2,1,0:T(8,128)(2,1)S(1)} collective-permute-done((bf16[2,704,128]{2,1,0:T(8,128)(2,1)}, bf16[2,704,128]{2,1,0:T(8,128)(2,1)S(1)}, u32[]{:S(2)}, u32[]{:S(2)}) %collective-permute-start.2) | collective-permute-done | bytes 360480 | tf_op jit(solution)/shard_map/ppermute | solution.py:24
  200.5 0.9 fusion.5
  201.4 2.5 %all-to-all-done.3 = bf16[32,6,256]{2,1,0:T(8,128)(2,1)S(1)} async-done(((bf16[32,6,256]{2,1,0:T(8,128)(2,1)}), bf16[32,6,256]{2,1,0:T(8,128)(2,1)S(1)}, u32[]{:S(2)}, u32[]{:S(2)}) %all-to-all-start.3) | async-done | bytes 98336 | tf_op jit(solution)/shard_map/all_to_all | solution.py:95
  204.0 0.8 convolution_convert_fusion.4
  204.7 0.8 convolution_convert_fusion.5
  (32 shorter events, 0.3 us)
Async XLA Ops:
  0.6 78.3 %copy-start = (bf16[2,1408,128]{2,1,0:T(8,128)(2,1)S(1)}, bf16[2,1408,128]{2,1,0:T(8,128)(2,1)}, u32[]{:S(2)}) copy-start(bf16[2,1408,128]{2,1,0:T(8,128)(2,1)} %param.13) | copy-start | bytes 2162692
  79.7 6.3 %copy-start.9 = (bf16[2,88,2048]{2,1,0:T(8,128)(2,1)S(1)}, bf16[2,88,2048]{2,1,0:T(8,128)(2,1)}, u32[]{:S(2)}) copy-start(bf16[2,88,2048]{2,1,0:T(8,128)(2,1)} %param.12) | copy-start | bytes 2162692
  80.7 28.0 %all-to-all-start.1 = ((bf16[16,32,2,3,88]{4,1,3,2,0:T(8,128)(2,1)}), bf16[16,32,2,3,88]{4,1,3,2,0:T(8,128)(2,1)S(1)}, u32[]{:S(2)}, u32[]{:S(2)}) async-start(bf16[16,32,2,3,88]{4,1,3,2,0:T(8,128)(2,1)} %copy.87), calls=%async_computation.1 | async-start | bytes 1572864 | tf_op jit(solution)/shard_map/all_to_all | solution.py:79
  91.9 16.9 %copy-start.10 = (bf16[2,88,2048]{2,1,0:T(8,128)(2,1)S(1)}, bf16[2,88,2048]{2,1,0:T(8,128)(2,1)}, u32[]{:S(2)}) copy-start(bf16[2,88,2048]{2,1,0:T(8,128)(2,1)} %param.12) | copy-start | bytes 2162692
  112.3 6.3 %copy-start.3 = (bf16[1,2,88,1024]{3,2,1,0:T(8,128)(2,1)}, bf16[1,2,88,1024]{3,2,1,0:T(8,128)(2,1)S(1)}, u32[]{:S(2)}) copy-start(bf16[1,2,88,1024]{3,2,1,0:T(8,128)(2,1)S(1)} %get-tuple-element.9) | copy-start | bytes 1081348
  112.3 6.3 %copy-start.5 = (bf16[1,2,88,1024]{3,2,1,0:T(8,128)(2,1)}, bf16[1,2,88,1024]{3,2,1,0:T(8,128)(2,1)S(1)}, u32[]{:S(2)}) copy-start(bf16[1,2,88,1024]{3,2,1,0:T(8,128)(2,1)S(1)} %get-tuple-element.10) | copy-start | bytes 1081348
  112.3 11.1 %copy-start.8 = (bf16[2,88,16,128,1]{3,2,1,0,4:T(8,128)(2,1)S(1)}, bf16[2,88,16,128,1]{3,2,1,0,4:T(8,128)(2,1)}, u32[]{:S(2)}) copy-start(bf16[2,88,16,128,1]{3,2,1,0,4:T(8,128)(2,1)} %bitcast_bitcast_fusion.1) | copy-start | bytes 2162692
  112.4 11.4 %copy-start.1 = (bf16[1,2,88,1024]{3,2,1,0:T(8,128)(2,1)}, bf16[1,2,88,1024]{3,2,1,0:T(8,128)(2,1)S(1)}, u32[]{:S(2)}) copy-start(bf16[1,2,88,1024]{3,2,1,0:T(8,128)(2,1)S(1)} %get-tuple-element.8) | copy-start | bytes 1081348
  113.3 67.9 %collective-permute-start = (bf16[2,88,1024]{2,1,0:T(8,128)(2,1)}, bf16[2,88,1024]{2,1,0:T(8,128)(2,1)}, u32[]{:S(2)}, u32[]{:S(2)}) collective-permute-start(bf16[2,88,1024]{2,1,0:T(8,128)(2,1)} %fusion.23), channel_id=1, source_target_pairs={{0,512},{512,0},{1,513},{513,1},{2,514},{514,2},{3,515},{515,3},{4... | collective-permute-start | bytes 1081352 | tf_op jit(solution)/shard_map/ppermute | solution.py:24
  117.7 6.1 %copy-start.7 = (bf16[2,88,16,128,1]{3,2,1,0,4:T(8,128)(2,1)S(1)}, bf16[2,88,16,128,1]{3,2,1,0,4:T(8,128)(2,1)}, u32[]{:S(2)}) copy-start(bf16[2,88,16,128,1]{3,2,1,0,4:T(8,128)(2,1)} %bitcast_bitcast_fusion) | copy-start | bytes 2162692
  118.6 64.5 %collective-permute-start.1 = (bf16[2,88,1024]{2,1,0:T(8,128)(2,1)}, bf16[2,88,1024]{2,1,0:T(8,128)(2,1)}, u32[]{:S(2)}, u32[]{:S(2)}) collective-permute-start(bf16[2,88,1024]{2,1,0:T(8,128)(2,1)} %fusion.19), channel_id=1, source_target_pairs={{0,512},{512,0},{1,513},{513,1},{2,514},{514,2},{3,515},{515,3},{4... | collective-permute-start | bytes 1081352 | tf_op jit(solution)/shard_map/ppermute | solution.py:24
  125.1 60.0 %all-to-all-start.2 = ((bf16[16,32,2,3,128]{4,1,3,2,0:T(8,128)(2,1)}), bf16[16,32,2,3,128]{4,1,3,2,0:T(8,128)(2,1)}, u32[]{:S(2)}, u32[]{:S(2)}) async-start(bf16[16,32,2,3,128]{4,1,3,2,0:T(8,128)(2,1)} %copy.90), calls=%async_computation.2 | async-start | bytes 1572864 | tf_op jit(solution)/shard_map/all_to_all | solution.py:89
  175.7 5.4 %copy-start.4 = (bf16[1,2,88,1024]{3,2,1,0:T(8,128)(2,1)S(1)}, bf16[1,2,88,1024]{3,2,1,0:T(8,128)(2,1)}, u32[]{:S(2)}) copy-start(bf16[1,2,88,1024]{3,2,1,0:T(8,128)(2,1)} %copy-done.3) | copy-start | bytes 1081348
  175.8 5.4 %copy-start.6 = (bf16[1,2,88,1024]{3,2,1,0:T(8,128)(2,1)S(1)}, bf16[1,2,88,1024]{3,2,1,0:T(8,128)(2,1)}, u32[]{:S(2)}) copy-start(bf16[1,2,88,1024]{3,2,1,0:T(8,128)(2,1)} %copy-done.5) | copy-start | bytes 1081348
  175.8 7.3 %copy-start.2 = (bf16[1,2,88,1024]{3,2,1,0:T(8,128)(2,1)S(1)}, bf16[1,2,88,1024]{3,2,1,0:T(8,128)(2,1)}, u32[]{:S(2)}) copy-start(bf16[1,2,88,1024]{3,2,1,0:T(8,128)(2,1)} %copy-done.1) | copy-start | bytes 1081348
  176.7 23.7 %collective-permute-start.2 = (bf16[2,704,128]{2,1,0:T(8,128)(2,1)}, bf16[2,704,128]{2,1,0:T(8,128)(2,1)S(1)}, u32[]{:S(2)}, u32[]{:S(2)}) collective-permute-start(bf16[2,704,128]{2,1,0:T(8,128)(2,1)} %fusion.15), channel_id=1, source_target_pairs={{0,512},{512,0},{1,513},{513,1},{2,514},{514,2},{3,515},{515,3},{4... | collective-permute-start | bytes 1081352 | tf_op jit(solution)/shard_map/ppermute | solution.py:24
  187.1 16.8 %all-to-all-start.3 = ((bf16[32,6,256]{2,1,0:T(8,128)(2,1)}), bf16[32,6,256]{2,1,0:T(8,128)(2,1)S(1)}, u32[]{:S(2)}, u32[]{:S(2)}) async-start(bf16[32,6,256]{2,1,0:T(8,128)(2,1)} %copy.91), calls=%async_computation.3 | async-start | bytes 262144 | tf_op jit(solution)/shard_map/all_to_all | solution.py:95

commit v3 on v2

--- a/solution.py
+++ b/solution.py
@@ -54,11 +54,8 @@
     outgoing = jnp.dot(picker_half, full_rows, preferred_element_type=jnp.float32).astype(
         jnp.bfloat16
     )
-    both_in = lax.all_to_all(
-        jnp.concatenate([outgoing, scaled_grad], axis=1),
-        "expert", split_axis=0, concat_axis=0, tiled=True,
-    )
-    rows_in, grads_in = both_in[:, :model_width], both_in[:, model_width:]
+    grads_in = lax.all_to_all(scaled_grad, "expert", split_axis=0, concat_axis=0, tiled=True)
+    rows_in = lax.all_to_all(outgoing, "expert", split_axis=0, concat_axis=0, tiled=True)
     received = rows_in.reshape(owners, exp_local, capacity, model_width)
     cotangent = grads_in.reshape(owners, exp_local, capacity, -1)
     gate_pre = jnp.einsum("jecd,efd->jecf", received, w_gate, preferred_element_type=jnp.float32)
@@ -91,14 +88,12 @@
         ),
         axis=0,
     ).astype(jnp.bfloat16)
-    feat = input_slices.shape[-1]
-    both_back = lax.all_to_all(
-        jnp.concatenate(
-            [expert_out.reshape(slot_count, -1), input_slices.reshape(slot_count, -1)], axis=1
-        ),
-        "expert", split_axis=0, concat_axis=0, tiled=True,
+    mixed_slots = lax.all_to_all(
+        expert_out.reshape(slot_count, -1), "expert", split_axis=0, concat_axis=0, tiled=True
     )
-    mixed_slots, input_slots = both_back[:, :feat], both_back[:, feat:]
+    input_slots = lax.all_to_all(
+        input_slices.reshape(slot_count, -1), "expert", split_axis=0, concat_axis=0, tiled=True
+    )
     mixed = jnp.dot(
         weighted.T, mixed_slots.astype(jnp.float32), precision=lax.Precision.HIGHEST
     ).astype(jnp.bfloat16)

time: 207 us -> 238 us (1.15)
  waiting for transfers between devices: 26.1 us -> 65.7 us
  blocking collectives: 111 us -> 76.5 us
  starting transfers between devices: 26.8 us -> 52.4 us
    all_to_all x1 -> x3, waiting for transfers between devices: 2.54 us -> 37.1 us  [the longest x1 22.3 us: body(): lax.all_to_all(outgoing, 'expert', split_axis=0, concat_axis=0, tiled=True)]
    all_to_all x1, blocking collectives: 40.7 us -> 20.4 us  [body(): lax.all_to_all(scaled_grad, 'expert', split_axis=0, concat_axis=0, tiled=...]
    ppermute x3, waiting for transfers between devices: 9.53 us -> 28.5 us  [dp_reduce(): got = lax.ppermute(send, 'dp', perm=[(0, 1), (1, 0)])]
    all_gather x1, blocking collectives: 38.7 us -> 24.6 us  [body(): hidden_all = lax.all_gather(hidden, 'fsdp', axis=3, tiled=True)]
    all_to_all x1, waiting for transfers between devices: 14.1 us -> 0.01 us  [body(): lax.all_to_all(hidden_parts, 'fsdp', 0, 0, tiled=False).astype(jnp.float32)]
    all_to_all x1, starting transfers between devices: 5.25 us -> 18.8 us  [body(): lax.all_to_all(hidden_parts, 'fsdp', 0, 0, tiled=False).astype(jnp.float32)]
    all_to_all x1 -> x3, starting transfers between devices: 3.84 us -> 13 us  [the longest x1 5.23 us: body(): lax.all_to_all(expert_out.reshape(slot_count, -1), 'expert', split_axis=0...]
    all_to_all x1, starting transfers between devices: 4.18 us -> 7.05 us  [body(): lax.all_to_all(input_parts.astype(jnp.bfloat16), 'fsdp', 0, 0, tiled=False)]
  transfers between devices with their start and end apart: 6 -> 8, of which waited for: 3 -> 5; matrix products, arithmetic and copies ran while one was open for 13% -> 8% of each run, Pallas kernels for 0% -> 0%
where the time goes in v3:
time: 238 us; the launch traced here: 236 us
  blocking collectives  76.5 us (32%)
  waiting for transfers between devices  65.7 us (28%)
  starting transfers between devices  52.4 us (22%)
  local copies, waits for them, and re-layouts  18.8 us (8%)
  matrix products  11.5 us (5%)
  other arithmetic  10.6 us (4%)
    all_gather x1, blocking collectives, body(): full_rows = lax.all_gather(tokens, 'fsdp', axis=1, tiled=True)  31.5 us
    ppermute x3, waiting for transfers between devices, dp_reduce(): got = lax.ppermute(send, 'dp', perm=[(0, 1), (1, 0)])  28.5 us
    all_gather x1, blocking collectives, body(): hidden_all = lax.all_gather(hidden, 'fsdp', axis=3, tiled=True)  24.6 us
    all_to_all x1, waiting for transfers between devices, body(): lax.all_to_all(outgoing, 'expert', split_axis=0, concat_axis=0, tiled=True)  22.3 us
    all_to_all x1, blocking collectives, body(): lax.all_to_all(scaled_grad, 'expert', split_axis=0, concat_axis=0, tiled=...  20.4 us
    all_to_all x1, starting transfers between devices, body(): lax.all_to_all(hidden_parts, 'fsdp', 0, 0, tiled=False).astype(jnp.float32)  18.8 us
    ppermute x3, starting transfers between devices, dp_reduce(): got = lax.ppermute(send, 'dp', perm=[(0, 1), (1, 0)])  13.5 us
    all_to_all x1, waiting for transfers between devices, body(): lax.all_to_all(input_slices.reshape(slot_count, -1), 'expert', split_axis...  8.4 us
  transfers between devices with their start and end apart: 8, of which 5 were waited for; matrix products, arithmetic and copies ran while one was open for 8% of the time, Pallas kernels for 0%

profile of v3, /device:TPU:1, one launch (start us, length us, event | category | flops | bytes accessed | tf_op | source)
XLA Modules:
  0.0 236.5 jit_solution(13957223976176130927)
XLA Ops:
  0.6 0.8 copy.74
  1.5 0.8 copy.58
  2.3 0.1 eq.35
  2.4 0.6 reduce-window.6
  3.0 0.2 slice_reduce_fusion
  3.2 0.1 bitcast_bitcast_fusion.2
  3.4 0.1 reduce_sum.42
  3.5 0.1 copy.61
  3.5 0.7 multiply_add_fusion
  4.3 0.1 iota_compare_fusion
  4.4 0.3 fusion.26
  4.6 1.0 convolution_convert_fusion.2
  5.7 20.4 %all_to_all.52 = bf16[32,6,128]{2,1,0:T(8,128)(2,1)S(1)} all-to-all(bf16[32,6,128]{2,1,0:T(8,128)(2,1)S(1)} %all_to_all.39), channel_id=1, replica_groups=mesh['dp'=2,'expert'=32,'fsdp'=16] {'expert'}, dimensions={0} | all-to-all | bytes 98304 | tf_op jit(solution)/shard_map/all_to_all | solution.py:57
  26.1 0.7 fusion.3
  26.8 1.0 copy.67
  27.8 18.8 %all-to-all-start.3 = ((bf16[16,32,2,3,88]{4,1,3,2,0:T(8,128)(2,1)}), bf16[16,32,2,3,88]{4,1,3,2,0:T(8,128)(2,1)S(1)}, u32[]{:S(2)}, u32[]{:S(2)}) async-start(bf16[16,32,2,3,88]{4,1,3,2,0:T(8,128)(2,1)} %copy.67), calls=%async_computation.3 | async-start | bytes 1572864 | tf_op jit(solution)/shard_map/all_to_all | solution.py:76
  46.6 31.5 %all_gather.6 = bf16[32,2048]{1,0:T(8,128)(2,1)S(1)} all-gather(bf16[32,128]{1,0:T(8,128)(2,1)S(1)} %copy-done.10), channel_id=1, replica_groups=mesh['dp'=2,'expert'=32,'fsdp'=16] {'fsdp'}, dimensions={1}, use_global_device_ids=true | all-gather | bytes 139264 | tf_op jit(solution)/shard_map/all_gather | solution.py:53
  78.1 0.1 convert_reduce_fusion.1
  78.2 0.4 convolution_convert_fusion
  78.6 1.2 all_to_all.34
  79.9 3.9 %all-to-all-start = ((bf16[32,6,2048]{2,1,0:T(8,128)(2,1)}), bf16[32,6,2048]{2,1,0:T(8,128)(2,1)S(1)}, u32[]{:S(2)}, u32[]{:S(2)}) async-start(bf16[32,6,2048]{2,1,0:T(8,128)(2,1)} %all_to_all.34), calls=%async_computation | async-start | bytes 2097152 | tf_op jit(solution)/shard_map/all_to_all | solution.py:58
  83.8 1.0 copy.95
  84.9 0.1 copy-done.8
  85.0 1.0 copy.94
  86.0 2.2 bitcast_bitcast_fusion
  88.2 1.0 bitcast_bitcast_fusion.1
  89.2 0.2 convert_reduce_fusion
  89.3 22.3 %all-to-all-done = bf16[32,6,2048]{2,1,0:T(8,128)(2,1)S(1)} async-done(((bf16[32,6,2048]{2,1,0:T(8,128)(2,1)}), bf16[32,6,2048]{2,1,0:T(8,128)(2,1)S(1)}, u32[]{:S(2)}, u32[]{:S(2)}) %all-to-all-start) | async-done | bytes 786464 | tf_op jit(solution)/shard_map/all_to_all | solution.py:58
  111.7 0.4 copy.62
  112.1 0.4 convolution_bitcast_fusion.3
  112.5 0.3 copy-done.9
  112.8 0.4 multiply_convert_fusion
  113.2 0.1 copy.63
  113.3 0.4 fusion.2
  113.7 1.3 fusion.1
  115.0 0.8 slice_bitcast_fusion.2
  115.8 1.5 fusion.12
  117.3 24.6 %all_gather.7 = bf16[32,2,3,1408]{0,1,2,3:T(2,128)(2,1)S(1)} all-gather(bf16[32,2,3,88]{0,1,2,3:T(2,128)(2,1)S(1)} %copy.63), channel_id=1, replica_groups=mesh['dp'=2,'expert'=32,'fsdp'=16] {'fsdp'}, dimensions={3}, use_global_device_ids=true | all-gather | bytes 574464 | tf_op jit(solution)/shard_map/all_gather | solution.py:65
  141.9 5.0 %copy.64 = bf16[32,2,3,1408]{3,0,2,1:T(8,128)(2,1)} copy(bf16[32,2,3,1408]{0,1,2,3:T(2,128)(2,1)S(1)} %all_gather.7) | data formatting | bytes 1081344 | tf_op jit(solution)/shard_map/all_gather | solution.py:65
  146.9 1.4 convolution_convert_fusion.3
  148.3 0.7 copy.65
  149.0 5.2 %all-to-all-start.1 = ((bf16[32,6,128]{2,1,0:T(8,128)(2,1)}), bf16[32,6,128]{2,1,0:T(8,128)(2,1)S(1)}, u32[]{:S(2)}, u32[]{:S(2)}) async-start(bf16[32,6,128]{2,1,0:T(8,128)(2,1)} %copy.65), calls=%async_computation.1 | async-start | bytes 131072 | tf_op jit(solution)/shard_map/all_to_all | solution.py:91
  154.2 1.9 fusion.4
  156.2 1.0 copy.70
  157.2 6.4 %all-to-all-done.1 = bf16[32,6,128]{2,1,0:T(8,128)(2,1)S(1)} async-done(((bf16[32,6,128]{2,1,0:T(8,128)(2,1)}), bf16[32,6,128]{2,1,0:T(8,128)(2,1)S(1)}, u32[]{:S(2)}, u32[]{:S(2)}) %all-to-all-start.1) | async-done | bytes 49184 | tf_op jit(solution)/shard_map/all_to_all | solution.py:91
  163.6 7.1 %all-to-all-start.4 = ((bf16[16,32,2,3,128]{4,1,3,2,0:T(8,128)(2,1)}), bf16[16,32,2,3,128]{4,1,3,2,0:T(8,128)(2,1)}, u32[]{:S(2)}, u32[]{:S(2)}) async-start(bf16[16,32,2,3,128]{4,1,3,2,0:T(8,128)(2,1)} %copy.70), calls=%async_computation.4 | async-start | bytes 1572864 | tf_op jit(solution)/shard_map/all_to_all | solution.py:86
  170.6 0.9 fusion.19
  171.5 4.4 %collective-permute-start.1 = (bf16[2,88,1024]{2,1,0:T(8,128)(2,1)}, bf16[2,88,1024]{2,1,0:T(8,128)(2,1)}, u32[]{:S(2)}, u32[]{:S(2)}) collective-permute-start(bf16[2,88,1024]{2,1,0:T(8,128)(2,1)} %fusion.19), channel_id=1, source_target_pairs={{0,512},{512,0},{1,513},{513,1},{2,514},{514,2},{3,515},{515,3},{4... | collective-permute-start | bytes 1081352 | tf_op jit(solution)/shard_map/ppermute | solution.py:24
  175.9 0.9 fusion.23
  176.8 4.8 %collective-permute-start = (bf16[2,88,1024]{2,1,0:T(8,128)(2,1)}, bf16[2,88,1024]{2,1,0:T(8,128)(2,1)}, u32[]{:S(2)}, u32[]{:S(2)}) collective-permute-start(bf16[2,88,1024]{2,1,0:T(8,128)(2,1)} %fusion.23), channel_id=1, source_target_pairs={{0,512},{512,0},{1,513},{513,1},{2,514},{514,2},{3,515},{515,3},{4... | collective-permute-start | bytes 1081352 | tf_op jit(solution)/shard_map/ppermute | solution.py:24
  181.6 0.4 fusion
  182.1 0.9 fusion.15
  182.9 4.4 %collective-permute-start.2 = (bf16[2,704,128]{2,1,0:T(8,128)(2,1)}, bf16[2,704,128]{2,1,0:T(8,128)(2,1)S(1)}, u32[]{:S(2)}, u32[]{:S(2)}) collective-permute-start(bf16[2,704,128]{2,1,0:T(8,128)(2,1)} %fusion.15), channel_id=1, source_target_pairs={{0,512},{512,0},{1,513},{513,1},{2,514},{514,2},{3,515},{515,3},{4... | collective-permute-start | bytes 1081352 | tf_op jit(solution)/shard_map/ppermute | solution.py:24
  187.3 0.8 convolution_convert_fusion.5
  188.1 22.8 %collective-permute-done.1 = bf16[2,88,1024]{2,1,0:T(8,128)(2,1)} collective-permute-done((bf16[2,88,1024]{2,1,0:T(8,128)(2,1)}, bf16[2,88,1024]{2,1,0:T(8,128)(2,1)}, u32[]{:S(2)}, u32[]{:S(2)}) %collective-permute-start.1) | collective-permute-done | bytes 360480 | tf_op jit(solution)/shard_map/ppermute | solution.py:24
  210.9 2.0 fusion.6
  212.9 5.8 %collective-permute-done = bf16[2,88,1024]{2,1,0:T(8,128)(2,1)} collective-permute-done((bf16[2,88,1024]{2,1,0:T(8,128)(2,1)}, bf16[2,88,1024]{2,1,0:T(8,128)(2,1)}, u32[]{:S(2)}, u32[]{:S(2)}) %collective-permute-start) | collective-permute-done | bytes 360480 | tf_op jit(solution)/shard_map/ppermute | solution.py:24
  218.6 2.0 fusion.7
  220.6 1.2 reduce_sum.45
  221.8 0.6 copy.71
  222.5 3.8 %all-to-all-start.5 = ((bf16[32,6,128]{2,1,0:T(8,128)(2,1)}), bf16[32,6,128]{2,1,0:T(8,128)(2,1)S(1)}, u32[]{:S(2)}, u32[]{:S(2)}) async-start(bf16[32,6,128]{2,1,0:T(8,128)(2,1)} %copy.71), calls=%async_computation.5 | async-start | bytes 131072 | tf_op jit(solution)/shard_map/all_to_all | solution.py:94
  226.3 0.9 fusion.5
  227.3 8.4 %all-to-all-done.5 = bf16[32,6,128]{2,1,0:T(8,128)(2,1)S(1)} async-done(((bf16[32,6,128]{2,1,0:T(8,128)(2,1)}), bf16[32,6,128]{2,1,0:T(8,128)(2,1)S(1)}, u32[]{:S(2)}, u32[]{:S(2)}) %all-to-all-start.5) | async-done | bytes 49184 | tf_op jit(solution)/shard_map/all_to_all | solution.py:94
  235.7 0.8 convolution_convert_fusion.4
  (34 shorter events, 0.3 us)
Async XLA Ops:
  0.6 25.5 %copy-start = (bf16[2,1408,128]{2,1,0:T(8,128)(2,1)S(1)}, bf16[2,1408,128]{2,1,0:T(8,128)(2,1)}, u32[]{:S(2)}) copy-start(bf16[2,1408,128]{2,1,0:T(8,128)(2,1)} %param.13) | copy-start | bytes 2162692
  26.8 19.8 %copy-start.10 = (bf16[32,128]{1,0:T(8,128)(2,1)S(1)}, bf16[32,128]{1,0:T(8,128)(2,1)}, u32[]{:S(2)}) copy-start(bf16[32,128]{1,0:T(8,128)(2,1)} %param.7) | copy-start | bytes 24580
  27.8 52.1 %all-to-all-start.3 = ((bf16[16,32,2,3,88]{4,1,3,2,0:T(8,128)(2,1)}), bf16[16,32,2,3,88]{4,1,3,2,0:T(8,128)(2,1)S(1)}, u32[]{:S(2)}, u32[]{:S(2)}) async-start(bf16[16,32,2,3,88]{4,1,3,2,0:T(8,128)(2,1)} %copy.67), calls=%async_computation.3 | async-start | bytes 1572864 | tf_op jit(solution)/shard_map/all_to_all | solution.py:76
  78.6 5.2 %copy-start.2 = (bf16[2,88,2048]{2,1,0:T(8,128)(2,1)S(1)}, bf16[2,88,2048]{2,1,0:T(8,128)(2,1)}, u32[]{:S(2)}) copy-start(bf16[2,88,2048]{2,1,0:T(8,128)(2,1)} %param.12) | copy-start | bytes 2162692
  79.9 31.8 %all-to-all-start = ((bf16[32,6,2048]{2,1,0:T(8,128)(2,1)}), bf16[32,6,2048]{2,1,0:T(8,128)(2,1)S(1)}, u32[]{:S(2)}, u32[]{:S(2)}) async-start(bf16[32,6,2048]{2,1,0:T(8,128)(2,1)} %all_to_all.34), calls=%async_computation | async-start | bytes 2097152 | tf_op jit(solution)/shard_map/all_to_all | solution.py:58
  83.8 1.2 copy-start.8
  86.0 2.2 copy-start.4
  111.7 1.1 copy-start.9
  113.7 2.1 copy-start.6
  146.9 7.3 %copy-start.5 = (bf16[2,88,16,128,1]{3,2,1,0,4:T(8,128)(2,1)S(1)}, bf16[2,88,16,128,1]{3,2,1,0,4:T(8,128)(2,1)}, u32[]{:S(2)}) copy-start(bf16[2,88,16,128,1]{3,2,1,0,4:T(8,128)(2,1)} %bitcast_bitcast_fusion) | copy-start | bytes 2162692
  149.0 14.6 %all-to-all-start.1 = ((bf16[32,6,128]{2,1,0:T(8,128)(2,1)}), bf16[32,6,128]{2,1,0:T(8,128)(2,1)S(1)}, u32[]{:S(2)}, u32[]{:S(2)}) async-start(bf16[32,6,128]{2,1,0:T(8,128)(2,1)} %copy.65), calls=%async_computation.1 | async-start | bytes 131072 | tf_op jit(solution)/shard_map/all_to_all | solution.py:91
  154.2 1.9 copy-start.3
  156.2 14.5 %copy-start.1 = (bf16[1,2,88,1024]{3,2,1,0:T(8,128)(2,1)S(1)}, bf16[1,2,88,1024]{3,2,1,0:T(8,128)(2,1)}, u32[]{:S(2)}) copy-start(bf16[1,2,88,1024]{3,2,1,0:T(8,128)(2,1)} %get-tuple-element.8) | copy-start | bytes 1081348
  157.2 24.4 %copy-start.7 = (bf16[32,2,3,1408]{3,0,2,1:T(8,128)(2,1)S(1)}, bf16[32,2,3,1408]{3,0,2,1:T(8,128)(2,1)}, u32[]{:S(2)}) copy-start(bf16[32,2,3,1408]{3,0,2,1:T(8,128)(2,1)} %copy.64) | copy-start | bytes 1622020
  163.6 57.0 %all-to-all-start.4 = ((bf16[16,32,2,3,128]{4,1,3,2,0:T(8,128)(2,1)}), bf16[16,32,2,3,128]{4,1,3,2,0:T(8,128)(2,1)}, u32[]{:S(2)}, u32[]{:S(2)}) async-start(bf16[16,32,2,3,128]{4,1,3,2,0:T(8,128)(2,1)} %copy.70), calls=%async_computation.4 | async-start | bytes 1572864 | tf_op jit(solution)/shard_map/all_to_all | solution.py:86
  171.5 39.4 %collective-permute-start.1 = (bf16[2,88,1024]{2,1,0:T(8,128)(2,1)}, bf16[2,88,1024]{2,1,0:T(8,128)(2,1)}, u32[]{:S(2)}, u32[]{:S(2)}) collective-permute-start(bf16[2,88,1024]{2,1,0:T(8,128)(2,1)} %fusion.19), channel_id=1, source_target_pairs={{0,512},{512,0},{1,513},{513,1},{2,514},{514,2},{3,515},{515,3},{4... | collective-permute-start | bytes 1081352 | tf_op jit(solution)/shard_map/ppermute | solution.py:24
  176.8 41.9 %collective-permute-start = (bf16[2,88,1024]{2,1,0:T(8,128)(2,1)}, bf16[2,88,1024]{2,1,0:T(8,128)(2,1)}, u32[]{:S(2)}, u32[]{:S(2)}) collective-permute-start(bf16[2,88,1024]{2,1,0:T(8,128)(2,1)} %fusion.23), channel_id=1, source_target_pairs={{0,512},{512,0},{1,513},{513,1},{2,514},{514,2},{3,515},{515,3},{4... | collective-permute-start | bytes 1081352 | tf_op jit(solution)/shard_map/ppermute | solution.py:24
  182.9 43.4 %collective-permute-start.2 = (bf16[2,704,128]{2,1,0:T(8,128)(2,1)}, bf16[2,704,128]{2,1,0:T(8,128)(2,1)S(1)}, u32[]{:S(2)}, u32[]{:S(2)}) collective-permute-start(bf16[2,704,128]{2,1,0:T(8,128)(2,1)} %fusion.15), channel_id=1, source_target_pairs={{0,512},{512,0},{1,513},{513,1},{2,514},{514,2},{3,515},{515,3},{4... | collective-permute-start | bytes 1081352 | tf_op jit(solution)/shard_map/ppermute | solution.py:24
  222.5 13.2 %all-to-all-start.5 = ((bf16[32,6,128]{2,1,0:T(8,128)(2,1)}), bf16[32,6,128]{2,1,0:T(8,128)(2,1)S(1)}, u32[]{:S(2)}, u32[]{:S(2)}) async-start(bf16[32,6,128]{2,1,0:T(8,128)(2,1)} %copy.71), calls=%async_computation.5 | async-start | bytes 131072 | tf_op jit(solution)/shard_map/all_to_all | solution.py:94

commit v4 on v2

--- a/solution.py
+++ b/solution.py
@@ -50,15 +50,16 @@
     scaled_grad = jnp.dot(
         weighted, grad_out.astype(jnp.float32), precision=lax.Precision.HIGHEST
     ).astype(jnp.bfloat16)
-    full_rows = lax.all_gather(tokens, "fsdp", axis=1, tiled=True)
-    outgoing = jnp.dot(picker_half, full_rows, preferred_element_type=jnp.float32).astype(
+    outgoing = jnp.dot(picker_half, tokens, preferred_element_type=jnp.float32).astype(
         jnp.bfloat16
     )
+    local_feat = tokens.shape[1]
     both_in = lax.all_to_all(
         jnp.concatenate([outgoing, scaled_grad], axis=1),
         "expert", split_axis=0, concat_axis=0, tiled=True,
     )
-    rows_in, grads_in = both_in[:, :model_width], both_in[:, model_width:]
+    rows_in = lax.all_gather(both_in[:, :local_feat], "fsdp", axis=1, tiled=True)
+    grads_in = both_in[:, local_feat:]
     received = rows_in.reshape(owners, exp_local, capacity, model_width)
     cotangent = grads_in.reshape(owners, exp_local, capacity, -1)
     gate_pre = jnp.einsum("jecd,efd->jecf", received, w_gate, preferred_element_type=jnp.float32)

time: 207 us -> 184 us (0.89)
  blocking collectives: 111 us -> 70.9 us
  starting transfers between devices: 26.8 us -> 54.3 us
  waiting for transfers between devices: 26.1 us -> 20.8 us
  local copies, waits for them, and re-layouts: 16.7 us -> 13.7 us
    all_to_all x1 -> x0, blocking collectives: 40.7 us -> none  [body(): lax.all_to_all(jnp.concatenate([outgoing, scaled_grad], axis=1), 'expert'...]
    all_to_all x1, waiting for transfers between devices: 14.1 us -> 0.01 us  [body(): lax.all_to_all(hidden_parts, 'fsdp', 0, 0, tiled=False).astype(jnp.float32)]
    all_to_all x1, starting transfers between devices: 5.25 us -> 18.9 us  [body(): lax.all_to_all(hidden_parts, 'fsdp', 0, 0, tiled=False).astype(jnp.float32)]
    all_to_all x0 -> x1, starting transfers between devices: none -> 11.3 us  [body(): lax.all_to_all(jnp.concatenate([outgoing, scaled_grad], axis=1), 'expert'...]
    all_to_all x0 -> x1, waiting for transfers between devices: none -> 9.68 us  [body(): lax.all_to_all(jnp.concatenate([outgoing, scaled_grad], axis=1), 'expert'...]
    all_to_all x1, starting transfers between devices: 4.18 us -> 6.51 us  [body(): lax.all_to_all(input_parts.astype(jnp.bfloat16), 'fsdp', 0, 0, tiled=False)]
  transfers between devices with their start and end apart: 6 -> 7, of which waited for: 3 -> 3; matrix products, arithmetic and copies ran while one was open for 13% -> 12% of each run, Pallas kernels for 0% -> 0%
where the time goes in v4:
time: 184 us; the launch traced here: 183 us
  blocking collectives  70.9 us (39%)
  starting transfers between devices  54.3 us (30%)
  waiting for transfers between devices  20.8 us (11%)
  local copies, waits for them, and re-layouts  13.7 us (7%)
  matrix products  12.3 us (7%)
  other arithmetic  9.92 us (5%)
    all_gather x1, blocking collectives, body(): hidden_all = lax.all_gather(hidden, 'fsdp', axis=3, tiled=True)  39.1 us
    all_gather x1, blocking collectives, body(): lax.all_gather(both_in[:, :local_feat], 'fsdp', axis=1, tiled=True)  31.8 us
    all_to_all x1, starting transfers between devices, body(): lax.all_to_all(hidden_parts, 'fsdp', 0, 0, tiled=False).astype(jnp.float32)  18.9 us
    ppermute x3, starting transfers between devices, dp_reduce(): got = lax.ppermute(send, 'dp', perm=[(0, 1), (1, 0)])  13.7 us
    all_to_all x1, starting transfers between devices, body(): lax.all_to_all(jnp.concatenate([outgoing, scaled_grad], axis=1), 'expert'...  11.3 us
    all_to_all x1, waiting for transfers between devices, body(): lax.all_to_all(jnp.concatenate([outgoing, scaled_grad], axis=1), 'expert'...  9.68 us
    ppermute x3, waiting for transfers between devices, dp_reduce(): got = lax.ppermute(send, 'dp', perm=[(0, 1), (1, 0)])  9.5 us
    all_to_all x1, starting transfers between devices, body(): lax.all_to_all(input_parts.astype(jnp.bfloat16), 'fsdp', 0, 0, tiled=False)  6.51 us
  transfers between devices with their start and end apart: 7, of which 3 were waited for; matrix products, arithmetic and copies ran while one was open for 12% of the time, Pallas kernels for 0%

profile of v4, /device:TPU:1, one launch (start us, length us, event | category | flops | bytes accessed | tf_op | source)
XLA Modules:
  0.0 183.0 jit_solution(1163524324093305088)
XLA Ops:
  0.6 0.0 copy-start
  0.6 0.0 copy-start.10
  0.7 0.9 copy.78
  1.5 0.1 eq.35
  1.7 0.6 reduce-window.6
  2.3 0.2 slice_reduce_fusion
  2.5 0.1 bitcast_bitcast_fusion.2
  2.7 0.1 reduce_sum.42
  2.8 0.1 copy.81
  2.8 0.7 multiply_add_fusion
  3.5 0.1 convert_reduce_fusion.1
  3.6 0.1 iota_compare_fusion
  3.7 0.8 copy.97
  4.5 0.3 fusion.26
  4.8 1.0 convolution_convert_fusion.2
  5.8 0.9 convolution_convert_fusion.3
  6.7 0.7 all_to_all.20
  7.4 11.3 %all-to-all-start = ((bf16[32,6,256]{2,1,0:T(8,128)(2,1)}), bf16[32,6,256]{2,1,0:T(8,128)(2,1)S(1)}, u32[]{:S(2)}, u32[]{:S(2)}) async-start(bf16[32,6,256]{2,1,0:T(8,128)(2,1)} %all_to_all.20), calls=%async_computation | async-start | bytes 262144 | tf_op jit(solution)/shard_map/all_to_all | solution.py:57
  18.7 0.1 copy.120
  18.9 9.7 %all-to-all-done = bf16[32,6,256]{2,1,0:T(8,128)(2,1)S(1)} async-done(((bf16[32,6,256]{2,1,0:T(8,128)(2,1)}), bf16[32,6,256]{2,1,0:T(8,128)(2,1)S(1)}, u32[]{:S(2)}, u32[]{:S(2)}) %all-to-all-start) | async-done | bytes 98336 | tf_op jit(solution)/shard_map/all_to_all | solution.py:57
  28.6 0.7 fusion.3
  29.3 1.0 copy.87
  30.3 18.9 %all-to-all-start.1 = ((bf16[16,32,2,3,88]{4,1,3,2,0:T(8,128)(2,1)}), bf16[16,32,2,3,88]{4,1,3,2,0:T(8,128)(2,1)S(1)}, u32[]{:S(2)}, u32[]{:S(2)}) async-start(bf16[16,32,2,3,88]{4,1,3,2,0:T(8,128)(2,1)} %copy.87), calls=%async_computation.1 | async-start | bytes 1572864 | tf_op jit(solution)/shard_map/all_to_all | solution.py:80
  49.3 1.0 bitcast_bitcast_fusion
  50.3 0.1 copy.119
  50.4 1.0 bitcast_bitcast_fusion.1
  51.4 31.8 %all_gather.6 = bf16[192,2048]{1,0:T(8,128)(2,1)S(1)} all-gather(bf16[192,128]{1,0:T(8,128)(2,1)S(1)} %get-tuple-element.15), channel_id=1, replica_groups=mesh['dp'=2,'expert'=32,'fsdp'=16] {'fsdp'}, dimensions={1}, use_global_device_ids=true | all-gather | bytes 835584 | tf_op jit(solution)/shard_map/all_gather | solution.py:61
  83.2 0.5 reshape.62
  83.7 0.0 copy-start.11
  83.7 2.0 %convolution_bitcast_fusion.4 = f32[32,2,3,88]{3,0,2,1:T(8,128)S(1)} fusion(bf16[2,88,2048]{2,1,0:T(8,128)(2,1)} %param.11, bf16[32,2,3,2048]{3,2,1,0:T(4,128)(2,1)S(1)} %reshape.62), kind=kOutput, calls=%fused_computation.12 | convolution fusion | flops 69206016 | bytes 1574912 | tf_op jit(solution)/shard_map/jecd,efd->jecf/dot_general | solution.py:65
  85.7 0.2 convert_reduce_fusion
  85.9 0.8 multiply_convert_fusion.2
  86.7 0.1 copy.84
  86.8 0.8 fusion.1
  87.6 0.8 fusion.2
  88.4 0.1 slice_bitcast_fusion.4
  88.5 0.0 copy-start.3
  88.5 0.0 copy-start.5
  88.5 0.1 slice_bitcast_fusion.2
  88.6 0.9 fusion.23
  89.5 4.4 %collective-permute-start = (bf16[2,88,1024]{2,1,0:T(8,128)(2,1)}, bf16[2,88,1024]{2,1,0:T(8,128)(2,1)}, u32[]{:S(2)}, u32[]{:S(2)}) collective-permute-start(bf16[2,88,1024]{2,1,0:T(8,128)(2,1)} %fusion.23), channel_id=1, source_target_pairs={{0,512},{512,0},{1,513},{513,1},{2,514},{514,2},{3,515},{515,3},{4... | collective-permute-start | bytes 1081352 | tf_op jit(solution)/shard_map/ppermute | solution.py:24
  93.9 0.9 fusion.19
  94.8 4.8 %collective-permute-start.1 = (bf16[2,88,1024]{2,1,0:T(8,128)(2,1)}, bf16[2,88,1024]{2,1,0:T(8,128)(2,1)}, u32[]{:S(2)}, u32[]{:S(2)}) collective-permute-start(bf16[2,88,1024]{2,1,0:T(8,128)(2,1)} %fusion.19), channel_id=1, source_target_pairs={{0,512},{512,0},{1,513},{513,1},{2,514},{514,2},{3,515},{515,3},{4... | collective-permute-start | bytes 1081352 | tf_op jit(solution)/shard_map/ppermute | solution.py:24
  99.6 0.4 fusion.12
  100.0 0.4 fusion.4
  100.4 1.0 copy.90
  101.3 6.5 %all-to-all-start.2 = ((bf16[16,32,2,3,128]{4,1,3,2,0:T(8,128)(2,1)}), bf16[16,32,2,3,128]{4,1,3,2,0:T(8,128)(2,1)}, u32[]{:S(2)}, u32[]{:S(2)}) async-start(bf16[16,32,2,3,128]{4,1,3,2,0:T(8,128)(2,1)} %copy.90), calls=%async_computation.2 | async-start | bytes 1572864 | tf_op jit(solution)/shard_map/all_to_all | solution.py:90
  107.9 39.1 %all_gather.7 = bf16[32,2,3,1408]{0,1,2,3:T(2,128)(2,1)S(1)} all-gather(bf16[32,2,3,88]{0,1,2,3:T(2,128)(2,1)S(1)} %copy.84), channel_id=1, replica_groups=mesh['dp'=2,'expert'=32,'fsdp'=16] {'fsdp'}, dimensions={3}, use_global_device_ids=true | all-gather | bytes 574464 | tf_op jit(solution)/shard_map/all_gather | solution.py:69
  147.0 4.9 %copy.85 = bf16[32,2,3,1408]{3,0,2,1:T(8,128)(2,1)} copy(bf16[32,2,3,1408]{0,1,2,3:T(2,128)(2,1)S(1)} %all_gather.7) | data formatting | bytes 1081344 | tf_op jit(solution)/shard_map/all_gather | solution.py:69
  151.9 1.5 fusion
  153.4 1.4 convolution_convert_fusion.1
  154.7 0.0 copy-start.4
  154.8 0.1 fusion.15
  155.0 4.6 %collective-permute-start.2 = (bf16[2,704,128]{2,1,0:T(8,128)(2,1)S(1)}, bf16[2,704,128]{2,1,0:T(8,128)(2,1)S(1)}, u32[]{:S(2)}, u32[]{:S(2)}) collective-permute-start(bf16[2,704,128]{2,1,0:T(8,128)(2,1)S(1)} %fusion.15), channel_id=1, source_target_pairs={{0,512},{512,0},{1,513},{513,1},{2,514},{514,2},{3,515},{515,3},{4... | collective-permute-start | bytes 1081352 | tf_op jit(solution)/shard_map/ppermute | solution.py:24
  159.5 2.0 %fusion.7 = bf16[2,88,1024]{2,1,0:T(8,128)(2,1)} fusion(bf16[2,88,1024]{2,1,0:T(8,128)(2,1)} %collective-permute-done, s32[]{:T(128)S(6)} %select_n.12, bf16[1,2,88,1024]{3,2,1,0:T(8,128)(2,1)S(1)} %copy-done.6, bf16[1,2,88,1024]{3,2,1,0:T(8,128)(2,1)S(1)} %copy-done.4), kind=kLoop, calls=%fused_computation.37 | loop fusion | flops 901120 | bytes 1441796 | tf_op jit(solution)/shard_map/convert_element_type | solution.py:25
  161.5 2.0 %fusion.6 = bf16[2,88,1024]{2,1,0:T(8,128)(2,1)} fusion(bf16[2,88,1024]{2,1,0:T(8,128)(2,1)} %collective-permute-done.1, s32[]{:T(128)S(6)} %select_n.12, bf16[1,2,88,1024]{3,2,1,0:T(8,128)(2,1)S(1)} %copy-done.2, bf16[1,2,88,1024]{3,2,1,0:T(8,128)(2,1)S(1)} %get-tuple-element.7), kind=kLoop, calls=%fused_computation.35 | loop fusion | flops 901120 | bytes 1441796 | tf_op jit(solution)/shard_map/convert_element_type | solution.py:25
  163.5 1.3 reduce_sum.45
  164.8 0.7 copy.91
  165.5 3.8 %all-to-all-start.3 = ((bf16[32,6,256]{2,1,0:T(8,128)(2,1)}), bf16[32,6,256]{2,1,0:T(8,128)(2,1)S(1)}, u32[]{:S(2)}, u32[]{:S(2)}) async-start(bf16[32,6,256]{2,1,0:T(8,128)(2,1)} %copy.91), calls=%async_computation.3 | async-start | bytes 262144 | tf_op jit(solution)/shard_map/all_to_all | solution.py:96
  169.3 9.5 %collective-permute-done.2 = bf16[2,704,128]{2,1,0:T(8,128)(2,1)S(1)} collective-permute-done((bf16[2,704,128]{2,1,0:T(8,128)(2,1)S(1)}, bf16[2,704,128]{2,1,0:T(8,128)(2,1)S(1)}, u32[]{:S(2)}, u32[]{:S(2)}) %collective-permute-start.2) | collective-permute-done | bytes 360480 | tf_op jit(solution)/shard_map/ppermute | solution.py:24
  178.8 0.9 fusion.5
  179.7 1.6 all-to-all-done.3
  181.4 0.8 convolution_convert_fusion.4
  182.2 0.8 convolution_convert_fusion.5
  (38 shorter events, 0.3 us)
Async XLA Ops:
  0.6 28.0 %copy-start = (bf16[2,1408,128]{2,1,0:T(8,128)(2,1)S(1)}, bf16[2,1408,128]{2,1,0:T(8,128)(2,1)}, u32[]{:S(2)}) copy-start(bf16[2,1408,128]{2,1,0:T(8,128)(2,1)} %param.13) | copy-start | bytes 2162692
  0.6 18.1 %copy-start.10 = (bf16[2,88,2048]{2,1,0:T(8,128)(2,1)S(1)}, bf16[2,88,2048]{2,1,0:T(8,128)(2,1)}, u32[]{:S(2)}) copy-start(bf16[2,88,2048]{2,1,0:T(8,128)(2,1)} %param.12) | copy-start | bytes 2162692
  4.8 1.0 copy-start.12
  7.4 21.1 %all-to-all-start = ((bf16[32,6,256]{2,1,0:T(8,128)(2,1)}), bf16[32,6,256]{2,1,0:T(8,128)(2,1)S(1)}, u32[]{:S(2)}, u32[]{:S(2)}) async-start(bf16[32,6,256]{2,1,0:T(8,128)(2,1)} %all_to_all.20), calls=%async_computation | async-start | bytes 262144 | tf_op jit(solution)/shard_map/all_to_all | solution.py:57
  30.3 19.9 %copy-start.9 = (bf16[2,88,2048]{2,1,0:T(8,128)(2,1)S(1)}, bf16[2,88,2048]{2,1,0:T(8,128)(2,1)}, u32[]{:S(2)}) copy-start(bf16[2,88,2048]{2,1,0:T(8,128)(2,1)} %param.11) | copy-start | bytes 2162692
  30.3 55.3 %all-to-all-start.1 = ((bf16[16,32,2,3,88]{4,1,3,2,0:T(8,128)(2,1)}), bf16[16,32,2,3,88]{4,1,3,2,0:T(8,128)(2,1)S(1)}, u32[]{:S(2)}, u32[]{:S(2)}) async-start(bf16[16,32,2,3,88]{4,1,3,2,0:T(8,128)(2,1)} %copy.87), calls=%async_computation.1 | async-start | bytes 1572864 | tf_op jit(solution)/shard_map/all_to_all | solution.py:80
  83.7 2.2 %copy-start.11 = (bf16[2,88,2048]{2,1,0:T(8,128)(2,1)S(1)}, bf16[2,88,2048]{2,1,0:T(8,128)(2,1)}, u32[]{:S(2)}) copy-start(bf16[2,88,2048]{2,1,0:T(8,128)(2,1)} %param.12) | copy-start | bytes 2162692
  88.5 6.3 %copy-start.3 = (bf16[1,2,88,1024]{3,2,1,0:T(8,128)(2,1)}, bf16[1,2,88,1024]{3,2,1,0:T(8,128)(2,1)S(1)}, u32[]{:S(2)}) copy-start(bf16[1,2,88,1024]{3,2,1,0:T(8,128)(2,1)S(1)} %get-tuple-element.9) | copy-start | bytes 1081348
  88.5 6.3 %copy-start.5 = (bf16[1,2,88,1024]{3,2,1,0:T(8,128)(2,1)}, bf16[1,2,88,1024]{3,2,1,0:T(8,128)(2,1)S(1)}, u32[]{:S(2)}) copy-start(bf16[1,2,88,1024]{3,2,1,0:T(8,128)(2,1)S(1)} %get-tuple-element.10) | copy-start | bytes 1081348
  88.5 11.1 %copy-start.8 = (bf16[2,88,16,128,1]{3,2,1,0,4:T(8,128)(2,1)S(1)}, bf16[2,88,16,128,1]{3,2,1,0,4:T(8,128)(2,1)}, u32[]{:S(2)}) copy-start(bf16[2,88,16,128,1]{3,2,1,0,4:T(8,128)(2,1)} %bitcast_bitcast_fusion.1) | copy-start | bytes 2162692
  88.6 11.4 %copy-start.1 = (bf16[1,2,88,1024]{3,2,1,0:T(8,128)(2,1)}, bf16[1,2,88,1024]{3,2,1,0:T(8,128)(2,1)S(1)}, u32[]{:S(2)}) copy-start(bf16[1,2,88,1024]{3,2,1,0:T(8,128)(2,1)S(1)} %get-tuple-element.8) | copy-start | bytes 1081348
  89.5 70.1 %collective-permute-start = (bf16[2,88,1024]{2,1,0:T(8,128)(2,1)}, bf16[2,88,1024]{2,1,0:T(8,128)(2,1)}, u32[]{:S(2)}, u32[]{:S(2)}) collective-permute-start(bf16[2,88,1024]{2,1,0:T(8,128)(2,1)} %fusion.23), channel_id=1, source_target_pairs={{0,512},{512,0},{1,513},{513,1},{2,514},{514,2},{3,515},{515,3},{4... | collective-permute-start | bytes 1081352 | tf_op jit(solution)/shard_map/ppermute | solution.py:24
  93.9 6.1 %copy-start.7 = (bf16[2,88,16,128,1]{3,2,1,0,4:T(8,128)(2,1)S(1)}, bf16[2,88,16,128,1]{3,2,1,0,4:T(8,128)(2,1)}, u32[]{:S(2)}) copy-start(bf16[2,88,16,128,1]{3,2,1,0,4:T(8,128)(2,1)} %bitcast_bitcast_fusion) | copy-start | bytes 2162692
  94.8 66.7 %collective-permute-start.1 = (bf16[2,88,1024]{2,1,0:T(8,128)(2,1)}, bf16[2,88,1024]{2,1,0:T(8,128)(2,1)}, u32[]{:S(2)}, u32[]{:S(2)}) collective-permute-start(bf16[2,88,1024]{2,1,0:T(8,128)(2,1)} %fusion.19), channel_id=1, source_target_pairs={{0,512},{512,0},{1,513},{513,1},{2,514},{514,2},{3,515},{515,3},{4... | collective-permute-start | bytes 1081352 | tf_op jit(solution)/shard_map/ppermute | solution.py:24
  101.3 62.1 %all-to-all-start.2 = ((bf16[16,32,2,3,128]{4,1,3,2,0:T(8,128)(2,1)}), bf16[16,32,2,3,128]{4,1,3,2,0:T(8,128)(2,1)}, u32[]{:S(2)}, u32[]{:S(2)}) async-start(bf16[16,32,2,3,128]{4,1,3,2,0:T(8,128)(2,1)} %copy.90), calls=%async_computation.2 | async-start | bytes 1572864 | tf_op jit(solution)/shard_map/all_to_all | solution.py:90
  154.7 4.8 %copy-start.4 = (bf16[1,2,88,1024]{3,2,1,0:T(8,128)(2,1)S(1)}, bf16[1,2,88,1024]{3,2,1,0:T(8,128)(2,1)}, u32[]{:S(2)}) copy-start(bf16[1,2,88,1024]{3,2,1,0:T(8,128)(2,1)} %copy-done.3) | copy-start | bytes 1081348
  154.7 4.8 %copy-start.6 = (bf16[1,2,88,1024]{3,2,1,0:T(8,128)(2,1)S(1)}, bf16[1,2,88,1024]{3,2,1,0:T(8,128)(2,1)}, u32[]{:S(2)}) copy-start(bf16[1,2,88,1024]{3,2,1,0:T(8,128)(2,1)} %copy-done.5) | copy-start | bytes 1081348
  154.8 6.7 %copy-start.2 = (bf16[1,2,88,1024]{3,2,1,0:T(8,128)(2,1)S(1)}, bf16[1,2,88,1024]{3,2,1,0:T(8,128)(2,1)}, u32[]{:S(2)}) copy-start(bf16[1,2,88,1024]{3,2,1,0:T(8,128)(2,1)} %copy-done.1) | copy-start | bytes 1081348
  155.0 23.8 %collective-permute-start.2 = (bf16[2,704,128]{2,1,0:T(8,128)(2,1)S(1)}, bf16[2,704,128]{2,1,0:T(8,128)(2,1)S(1)}, u32[]{:S(2)}, u32[]{:S(2)}) collective-permute-start(bf16[2,704,128]{2,1,0:T(8,128)(2,1)S(1)} %fusion.15), channel_id=1, source_target_pairs={{0,512},{512,0},{1,513},{513,1},{2,514},{514,2},{3,515},{515,3},{4... | collective-permute-start | bytes 1081352 | tf_op jit(solution)/shard_map/ppermute | solution.py:24
  163.5 18.7 %copy-start.13 = (f32[32,1,192]{2,1,0:T(1,128)S(1)}, f32[32,1,192]{2,1,0:T(1,128)}, u32[]{:S(2)}) copy-start(f32[32,1,192]{2,1,0:T(1,128)} %copy-done.12) | copy-start | bytes 73732
  165.5 15.9 %all-to-all-start.3 = ((bf16[32,6,256]{2,1,0:T(8,128)(2,1)}), bf16[32,6,256]{2,1,0:T(8,128)(2,1)S(1)}, u32[]{:S(2)}, u32[]{:S(2)}) async-start(bf16[32,6,256]{2,1,0:T(8,128)(2,1)} %copy.91), calls=%async_computation.3 | async-start | bytes 262144 | tf_op jit(solution)/shard_map/all_to_all | solution.py:96

commit v5 on v4

--- a/solution.py
+++ b/solution.py
@@ -23,6 +23,22 @@
     send = lax.dynamic_index_in_dim(halves, 1 - me, 0, keepdims=False)
     got = lax.ppermute(send, "dp", perm=[(0, 1), (1, 0)])
     return (keep.astype(jnp.float32) + got.astype(jnp.float32)).astype(jnp.bfloat16)
+
+
+def gather_fsdp(part, axis):
+    over_z = lax.all_gather(part, "fz", axis=axis, tiled=False)
+    both = lax.all_gather(over_z, "fc", axis=axis, tiled=False)
+    both = jnp.swapaxes(both, axis, axis + 1)
+    shape = part.shape[:axis] + (-1,) + part.shape[axis + 1:]
+    return both.reshape(shape)
+
+
+def reduce_fsdp(parts):
+    n_z, n_c = lax.axis_size("fz"), lax.axis_size("fc")
+    split = parts.reshape((n_z, n_c) + parts.shape[1:])
+    on_chip = lax.all_to_all(split, "fc", 1, 1, tiled=False)
+    paired = jnp.sum(on_chip.astype(jnp.float32), axis=1).astype(jnp.bfloat16)
+    return jnp.sum(lax.all_to_all(paired, "fz", 0, 0, tiled=False).astype(jnp.float32), axis=0)
 
 
 def body(tokens, grad_out, expert_ids, gate_weights, w_gate, w_up, w_down):
@@ -58,7 +74,7 @@
         jnp.concatenate([outgoing, scaled_grad], axis=1),
         "expert", split_axis=0, concat_axis=0, tiled=True,
     )
-    rows_in = lax.all_gather(both_in[:, :local_feat], "fsdp", axis=1, tiled=True)
+    rows_in = gather_fsdp(both_in[:, :local_feat], 1)
     grads_in = both_in[:, local_feat:]
     received = rows_in.reshape(owners, exp_local, capacity, model_width)
     cotangent = grads_in.reshape(owners, exp_local, capacity, -1)
@@ -66,19 +82,17 @@
     up_pre = jnp.einsum("jecd,efd->jecf", received, w_up, preferred_element_type=jnp.float32)
     activation, slope_term = silu_parts(gate_pre)
     hidden = (activation * up_pre).astype(jnp.bfloat16)
-    hidden_all = lax.all_gather(hidden, "fsdp", axis=3, tiled=True)
+    hidden_all = gather_fsdp(hidden, 3)
     expert_out = jnp.einsum(
         "jecf,efd->jecd", hidden_all, w_down, preferred_element_type=jnp.float32
     ).astype(jnp.bfloat16)
-    shards = lax.axis_size("fsdp")
+    shards = lax.axis_size("fz") * lax.axis_size("fc")
     exp_n, ff_all, feat = w_down.shape
     hidden_parts = jnp.einsum(
         "jecd,egfd->gjecf", cotangent, w_down.reshape(exp_n, shards, ff_all // shards, feat),
         preferred_element_type=jnp.float32,
     ).astype(jnp.bfloat16)
-    grad_hidden = jnp.sum(
-        lax.all_to_all(hidden_parts, "fsdp", 0, 0, tiled=False).astype(jnp.float32), axis=0
-    )
+    grad_hidden = reduce_fsdp(hidden_parts)
     grad_gate_pre = (grad_hidden * up_pre * slope_term).astype(jnp.bfloat16)
     grad_up_pre = (grad_hidden * activation).astype(jnp.bfloat16)
     w_gate_g = w_gate.reshape(exp_n, w_gate.shape[1], shards, model_width // shards)
@@ -86,12 +100,7 @@
     input_parts = jnp.einsum(
         "jecf,efgd->gjecd", grad_gate_pre, w_gate_g, preferred_element_type=jnp.float32
     ) + jnp.einsum("jecf,efgd->gjecd", grad_up_pre, w_up_g, preferred_element_type=jnp.float32)
-    input_slices = jnp.sum(
-        lax.all_to_all(input_parts.astype(jnp.bfloat16), "fsdp", 0, 0, tiled=False).astype(
-            jnp.float32
-        ),
-        axis=0,
-    ).astype(jnp.bfloat16)
+    input_slices = reduce_fsdp(input_parts.astype(jnp.bfloat16)).astype(jnp.bfloat16)
     feat = input_slices.shape[-1]
     both_back = lax.all_to_all(
         jnp.concatenate(
@@ -129,19 +138,24 @@
 
 def solution(mesh):
     in_specs = (
-        P(("dp", "expert"), "fsdp"),
-        P(("dp", "expert"), "fsdp"),
+        P(("dp", "expert"), ("fz", "fc")),
+        P(("dp", "expert"), ("fz", "fc")),
         P(("dp", "expert"), None),
         P(("dp", "expert"), None),
-        P("expert", "fsdp", None),
-        P("expert", "fsdp", None),
-        P("expert", None, "fsdp"),
+        P("expert", ("fz", "fc"), None),
+        P("expert", ("fz", "fc"), None),
+        P("expert", None, ("fz", "fc")),
     )
     out_specs = (
-        P(("dp", "expert"), "fsdp"),
-        P(("dp", "expert"), "fsdp"),
-        P("expert", "fsdp", "dp"),
-        P("expert", "fsdp", "dp"),
-        P("expert", "dp", "fsdp"),
+        P(("dp", "expert"), ("fz", "fc")),
+        P(("dp", "expert"), ("fz", "fc")),
+        P("expert", ("fz", "fc"), "dp"),
+        P("expert", ("fz", "fc"), "dp"),
+        P("expert", "dp", ("fz", "fc")),
     )
-    return jax.shard_map(body, mesh=mesh, in_specs=in_specs, out_specs=out_specs, check_vma=False)
+    n_fsdp = mesh.shape["fsdp"]
+    split_mesh = jax.sharding.Mesh(
+        mesh.devices.reshape(mesh.devices.shape[:-1] + (n_fsdp // 2, 2)),
+        mesh.axis_names[:-1] + ("fz", "fc"),
+    )
+    return jax.shard_map(body, mesh=split_mesh, in_specs=in_specs, out_specs=out_specs, check_vma=False)

time: 184 us -> 189 us (1.027)
  starting transfers between devices: 54.3 us -> 46.1 us
  blocking collectives: 70.9 us -> 79 us
  waiting for transfers between devices: 20.8 us -> 25 us
    all_to_all x0 -> x2, blocking collectives: none -> 16.8 us  [reduce_fsdp(): on_chip = lax.all_to_all(split, 'fc', 1, 1, tiled=False)]
    all_to_all x2, starting transfers between devices: 25.4 us -> 15.3 us  [reduce_fsdp(): lax.all_to_all(paired, 'fz', 0, 0, tiled=False).astype(jnp.float32)]
    all_gather x2 -> x4, blocking collectives: 70.9 us -> 62.2 us  [the longest x2 48 us: gather_fsdp(): over_z = lax.all_gather(part, 'fz', axis=axis, tiled=False)]
    all_to_all x1, waiting for transfers between devices: 1.61 us -> 7.92 us  [body(): lax.all_to_all(jnp.concatenate([expert_out.reshape(slot_count, -1), input...]
    all_gather x1, local copies, waits for them, and re-layouts: 4.95 us -> 1.38 us  [gather_fsdp(): over_z = lax.all_gather(part, 'fz', axis=axis, tiled=False)]
    all_to_all x1, waiting for transfers between devices: 9.68 us -> 7.54 us  [body(): lax.all_to_all(jnp.concatenate([outgoing, scaled_grad], axis=1), 'expert'...]
    convert_element_type x2 -> x0, local copies, waits for them, and re-layouts: 1.98 us -> none  [the longest x1 0.99 us: body(): input_parts.astype(jnp.bfloat16)]
  transfers between devices with their start and end apart: 7 -> 7, of which waited for: 3 -> 4; matrix products, arithmetic and copies ran while one was open for 12% -> 9% of each run, Pallas kernels for 0% -> 0%
where the time goes in v5:
time: 189 us; the launch traced here: 186 us
  blocking collectives  79 us (42%)
  starting transfers between devices  46.1 us (24%)
  waiting for transfers between devices  25 us (13%)
  local copies, waits for them, and re-layouts  13.2 us (7%)
  matrix products  11.1 us (6%)
  other arithmetic  10.8 us (6%)
    all_gather x2, blocking collectives, gather_fsdp(): over_z = lax.all_gather(part, 'fz', axis=axis, tiled=False)  48 us
    all_to_all x2, blocking collectives, reduce_fsdp(): on_chip = lax.all_to_all(split, 'fc', 1, 1, tiled=False)  16.8 us
    all_to_all x2, starting transfers between devices, reduce_fsdp(): lax.all_to_all(paired, 'fz', 0, 0, tiled=False).astype(jnp.float32)  15.3 us
    all_gather x2, blocking collectives, gather_fsdp(): both = lax.all_gather(over_z, 'fc', axis=axis, tiled=False)  14.2 us
    ppermute x3, starting transfers between devices, dp_reduce(): got = lax.ppermute(send, 'dp', perm=[(0, 1), (1, 0)])  13.7 us
    all_to_all x1, starting transfers between devices, body(): lax.all_to_all(jnp.concatenate([outgoing, scaled_grad], axis=1), 'expert'...  11.4 us
    ppermute x3, waiting for transfers between devices, dp_reduce(): got = lax.ppermute(send, 'dp', perm=[(0, 1), (1, 0)])  9.56 us
    all_to_all x1, waiting for transfers between devices, body(): lax.all_to_all(jnp.concatenate([expert_out.reshape(slot_count, -1), input...  7.92 us
  transfers between devices with their start and end apart: 7, of which 4 were waited for; matrix products, arithmetic and copies ran while one was open for 9% of the time, Pallas kernels for 0%

profile of v5, /device:TPU:1, one launch (start us, length us, event | category | flops | bytes accessed | tf_op | source)
XLA Modules:
  0.0 186.3 jit_solution(2452958943479987665)
XLA Ops:
  0.7 0.9 copy.138
  1.5 0.1 eq.35
  1.7 0.6 reduce-window.6
  2.3 0.2 slice_reduce_fusion
  2.5 0.1 bitcast_bitcast_fusion.2
  2.7 0.1 reduce_sum.66
  2.8 0.7 multiply_add_fusion
  3.5 0.1 convert_reduce_fusion.1
  3.6 0.1 iota_compare_fusion
  3.7 0.8 copy.163
  4.5 0.3 fusion.24
  4.8 1.0 convolution_convert_fusion.2
  5.8 0.9 convolution_convert_fusion.3
  6.7 0.7 all_to_all.26
  7.4 11.4 %all-to-all-start = ((bf16[32,6,256]{2,1,0:T(8,128)(2,1)}), bf16[32,6,256]{2,1,0:T(8,128)(2,1)S(1)}, u32[]{:S(2)}, u32[]{:S(2)}) async-start(bf16[32,6,256]{2,1,0:T(8,128)(2,1)} %all_to_all.26), calls=%async_computation | async-start | bytes 262144 | tf_op jit(solution)/shard_map/all_to_all | solution.py:73
  18.8 0.1 copy.191
  19.0 1.0 bitcast_bitcast_fusion
  20.0 0.1 copy.190
  20.1 1.0 bitcast_bitcast_fusion.1
  21.1 7.5 %all-to-all-done = bf16[32,6,256]{2,1,0:T(8,128)(2,1)S(1)} async-done(((bf16[32,6,256]{2,1,0:T(8,128)(2,1)}), bf16[32,6,256]{2,1,0:T(8,128)(2,1)S(1)}, u32[]{:S(2)}, u32[]{:S(2)}) %all-to-all-start) | async-done | bytes 98336 | tf_op jit(solution)/shard_map/all_to_all | solution.py:73
  28.7 0.7 convolution_convert_fusion
  29.5 11.9 %all_to_all.41 = bf16[8,2,32,2,3,88]{5,2,0,4,3,1:T(8,128)(2,1)S(1)} all-to-all(bf16[8,2,32,2,3,88]{5,2,0,4,3,1:T(8,128)(2,1)S(1)} %copy.150), channel_id=1, replica_groups=mesh['dp'=2,'expert'=32,'fz'=8,'fc'=2] {'fc'}, dimensions={1} | all-to-all | bytes 1081344 | tf_op jit(solution)/shard_map/all_to_all | solution.py:39
  41.4 0.3 reduce_sum.68
  41.7 0.8 copy.152
  42.5 10.6 %all-to-all-start.2 = ((bf16[8,32,2,3,88]{4,1,3,2,0:T(8,128)(2,1)}), bf16[8,32,2,3,88]{4,1,3,2,0:T(8,128)(2,1)S(1)}, u32[]{:S(2)}, u32[]{:S(2)}) async-start(bf16[8,32,2,3,88]{4,1,3,2,0:T(8,128)(2,1)} %copy.152), calls=%async_computation.2 | async-start | bytes 786432 | tf_op jit(solution)/shard_map/all_to_all | solution.py:41
  53.2 26.5 %all-gather = bf16[192,1024]{1,0:T(8,128)(2,1)S(1)} all-gather(bf16[192,128]{1,0:T(8,128)(2,1)S(1)} %get-tuple-element.15), channel_id=2, replica_groups=mesh['dp'=2,'expert'=32,'fz'=8,'fc'=2] {'fz'}, dimensions={1}, use_global_device_ids=true | all-gather | bytes 442368 | tf_op jit(solution)/shard_map/all_gather | solution.py:29
  79.7 6.6 %all-gather.1 = bf16[192,16,128]{2,1,0:T(8,128)(2,1)S(1)} all-gather(bf16[192,8,128]{2,1,0:T(8,128)(2,1)S(1)} %bitcast.158), channel_id=3, replica_groups=mesh['dp'=2,'expert'=32,'fz'=8,'fc'=2] {'fc'}, dimensions={1}, use_global_device_ids=true | all-gather | bytes 1179648 | tf_op jit(solution)/shard_map/all_gather | solution.py:30
  86.3 0.8 copy.142
  87.1 0.3 reshape_reshape.3
  87.4 2.0 %convolution_bitcast_fusion.4 = f32[32,2,3,88]{3,0,2,1:T(8,128)S(1)} fusion(bf16[2,88,2048]{2,1,0:T(8,128)(2,1)} %param.11, bf16[32,2,3,2048]{3,2,1,0:T(4,128)(2,1)S(1)} %reshape_reshape.3), kind=kOutput, calls=%fused_computation.9 | convolution fusion | flops 69206016 | bytes 1574912 | tf_op jit(solution)/shard_map/jecd,efd->jecf/dot_general | solution.py:81
  89.5 0.8 multiply_convert_fusion.2
  90.3 0.1 copy.145
  90.4 21.5 %all-gather.2 = bf16[32,2,3,704]{0,1,2,3:T(2,128)(2,1)S(1)} all-gather(bf16[32,2,3,88]{0,1,2,3:T(2,128)(2,1)S(1)} %copy.145), channel_id=4, replica_groups=mesh['dp'=2,'expert'=32,'fz'=8,'fc'=2] {'fz'}, dimensions={3}, use_global_device_ids=true | all-gather | bytes 304128 | tf_op jit(solution)/shard_map/all_gather | solution.py:29
  112.0 1.4 copy.177
  113.3 7.6 %all-gather.3 = bf16[32,2,3,16,88]{4,3,0,2,1:T(8,128)(2,1)S(1)} all-gather(bf16[32,2,3,8,88]{4,3,0,2,1:T(8,128)(2,1)S(1)} %copy.177), channel_id=5, replica_groups=mesh['dp'=2,'expert'=32,'fz'=8,'fc'=2] {'fc'}, dimensions={3}, use_global_device_ids=true | all-gather | bytes 811008 | tf_op jit(solution)/shard_map/all_gather | solution.py:30
  120.9 0.8 copy.148
  121.8 0.9 reshape.68
  122.7 0.3 convolution_convert_fusion.1
  123.0 1.3 fusion
  124.3 0.8 fusion.1
  125.0 0.8 fusion.2
  126.0 0.9 fusion.21
  126.9 4.4 %collective-permute-start = (bf16[2,88,1024]{2,1,0:T(8,128)(2,1)}, bf16[2,88,1024]{2,1,0:T(8,128)(2,1)}, u32[]{:S(2)}, u32[]{:S(2)}) collective-permute-start(bf16[2,88,1024]{2,1,0:T(8,128)(2,1)} %fusion.21), channel_id=1, source_target_pairs={{0,512},{512,0},{1,513},{513,1},{2,514},{514,2},{3,515},{515,3},{4... | collective-permute-start | bytes 1081352 | tf_op jit(solution)/shard_map/ppermute | solution.py:24
  131.3 0.9 fusion.17
  132.2 4.9 %collective-permute-start.1 = (bf16[2,88,1024]{2,1,0:T(8,128)(2,1)}, bf16[2,88,1024]{2,1,0:T(8,128)(2,1)}, u32[]{:S(2)}, u32[]{:S(2)}) collective-permute-start(bf16[2,88,1024]{2,1,0:T(8,128)(2,1)} %fusion.17), channel_id=1, source_target_pairs={{0,512},{512,0},{1,513},{513,1},{2,514},{514,2},{3,515},{515,3},{4... | collective-permute-start | bytes 1081352 | tf_op jit(solution)/shard_map/ppermute | solution.py:24
  137.1 0.4 fusion.10
  137.5 0.4 add_convert_fusion
  138.0 4.9 %all_to_all.42 = bf16[8,2,32,2,3,128]{5,2,0,4,3,1:T(8,128)(2,1)S(1)} all-to-all(bf16[8,2,32,2,3,128]{5,2,0,4,3,1:T(8,128)(2,1)S(1)} %copy.155), channel_id=1, replica_groups=mesh['dp'=2,'expert'=32,'fz'=8,'fc'=2] {'fc'}, dimensions={1} | all-to-all | bytes 1572864 | tf_op jit(solution)/shard_map/all_to_all | solution.py:39
  142.9 0.2 reduce_sum.70
  143.1 0.8 copy.157
  143.8 4.7 %all-to-all-start.4 = ((bf16[8,32,2,3,128]{4,1,3,2,0:T(8,128)(2,1)}), bf16[8,32,2,3,128]{4,1,3,2,0:T(8,128)(2,1)S(1)}, u32[]{:S(2)}, u32[]{:S(2)}) async-start(bf16[8,32,2,3,128]{4,1,3,2,0:T(8,128)(2,1)} %copy.157), calls=%async_computation.4 | async-start | bytes 786432 | tf_op jit(solution)/shard_map/all_to_all | solution.py:41
  148.5 1.1 slice_bitcast_fusion
  149.7 0.9 fusion.13
  150.6 4.4 %collective-permute-start.2 = (bf16[2,704,128]{2,1,0:T(8,128)(2,1)}, bf16[2,704,128]{2,1,0:T(8,128)(2,1)}, u32[]{:S(2)}, u32[]{:S(2)}) collective-permute-start(bf16[2,704,128]{2,1,0:T(8,128)(2,1)} %fusion.13), channel_id=1, source_target_pairs={{0,512},{512,0},{1,513},{513,1},{2,514},{514,2},{3,515},{515,3},{4... | collective-permute-start | bytes 1081352 | tf_op jit(solution)/shard_map/ppermute | solution.py:24
  155.0 3.6 %collective-permute-done = bf16[2,88,1024]{2,1,0:T(8,128)(2,1)} collective-permute-done((bf16[2,88,1024]{2,1,0:T(8,128)(2,1)}, bf16[2,88,1024]{2,1,0:T(8,128)(2,1)}, u32[]{:S(2)}, u32[]{:S(2)}) %collective-permute-start) | collective-permute-done | bytes 360480 | tf_op jit(solution)/shard_map/ppermute | solution.py:24
  158.6 2.0 %fusion.5 = bf16[2,88,1024]{2,1,0:T(8,128)(2,1)} fusion(bf16[2,88,1024]{2,1,0:T(8,128)(2,1)} %collective-permute-done, s32[]{:T(128)S(6)} %select_n.12, bf16[1,2,88,1024]{3,2,1,0:T(8,128)(2,1)S(1)} %get-tuple-element.10, bf16[1,2,88,1024]{3,2,1,0:T(8,128)(2,1)S(1)} %get-tuple-element.9), kind=kLoop, calls=%fused_computation.35 | loop fusion | flops 901120 | bytes 1441796 | tf_op jit(solution)/shard_map/convert_element_type | solution.py:25
  160.5 6.0 %collective-permute-done.1 = bf16[2,88,1024]{2,1,0:T(8,128)(2,1)} collective-permute-done((bf16[2,88,1024]{2,1,0:T(8,128)(2,1)}, bf16[2,88,1024]{2,1,0:T(8,128)(2,1)}, u32[]{:S(2)}, u32[]{:S(2)}) %collective-permute-start.1) | collective-permute-done | bytes 360480 | tf_op jit(solution)/shard_map/ppermute | solution.py:24
  166.5 2.0 %fusion.4 = bf16[2,88,1024]{2,1,0:T(8,128)(2,1)} fusion(bf16[2,88,1024]{2,1,0:T(8,128)(2,1)} %collective-permute-done.1, s32[]{:T(128)S(6)} %select_n.12, bf16[1,2,88,1024]{3,2,1,0:T(8,128)(2,1)S(1)} %get-tuple-element.8, bf16[1,2,88,1024]{3,2,1,0:T(8,128)(2,1)S(1)} %get-tuple-element.7), kind=kLoop, calls=%fused_computation.33 | loop fusion | flops 901120 | bytes 1441796 | tf_op jit(solution)/shard_map/convert_element_type | solution.py:25
  168.5 0.7 copy.158
  169.2 5.6 %all-to-all-start.5 = ((bf16[32,6,256]{2,1,0:T(8,128)(2,1)}), bf16[32,6,256]{2,1,0:T(8,128)(2,1)S(1)}, u32[]{:S(2)}, u32[]{:S(2)}) async-start(bf16[32,6,256]{2,1,0:T(8,128)(2,1)} %copy.158), calls=%async_computation.5 | async-start | bytes 262144 | tf_op jit(solution)/shard_map/all_to_all | solution.py:105
  174.9 1.9 %fusion.3 = bf16[2,704,128]{2,1,0:T(8,128)(2,1)} fusion(bf16[2,704,128]{2,1,0:T(8,128)(2,1)} %collective-permute-done.2, s32[]{:T(128)S(6)} %select_n.12, bf16[1,2,704,128]{3,2,1,0:T(8,128)(2,1)S(1)} %get-tuple-element.6, bf16[1,2,704,128]{3,2,1,0:T(8,128)(2,1)S(1)} %get-tuple-element.5), kind=kLoop, calls=%fused_computation.31 | loop fusion | flops 901120 | bytes 1441796 | tf_op jit(solution)/shard_map/convert_element_type | solution.py:25
  176.8 7.9 %all-to-all-done.5 = bf16[32,6,256]{2,1,0:T(8,128)(2,1)S(1)} async-done(((bf16[32,6,256]{2,1,0:T(8,128)(2,1)}), bf16[32,6,256]{2,1,0:T(8,128)(2,1)S(1)}, u32[]{:S(2)}, u32[]{:S(2)}) %all-to-all-start.5) | async-done | bytes 98336 | tf_op jit(solution)/shard_map/all_to_all | solution.py:105
  184.8 0.8 convolution_convert_fusion.4
  185.5 0.8 convolution_convert_fusion.5
  (34 shorter events, 0.8 us)
Async XLA Ops:
  0.6 28.1 %copy-start = (bf16[2,1408,128]{2,1,0:T(8,128)(2,1)S(1)}, bf16[2,1408,128]{2,1,0:T(8,128)(2,1)}, u32[]{:S(2)}) copy-start(bf16[2,1408,128]{2,1,0:T(8,128)(2,1)} %param.13) | copy-start | bytes 2162692
  0.6 18.2 %copy-start.4 = (bf16[2,88,2048]{2,1,0:T(8,128)(2,1)S(1)}, bf16[2,88,2048]{2,1,0:T(8,128)(2,1)}, u32[]{:S(2)}) copy-start(bf16[2,88,2048]{2,1,0:T(8,128)(2,1)} %param.12) | copy-start | bytes 2162692
  7.4 12.6 %copy-start.3 = (bf16[2,88,2048]{2,1,0:T(8,128)(2,1)S(1)}, bf16[2,88,2048]{2,1,0:T(8,128)(2,1)}, u32[]{:S(2)}) copy-start(bf16[2,88,2048]{2,1,0:T(8,128)(2,1)} %param.11) | copy-start | bytes 2162692
  7.4 21.3 %all-to-all-start = ((bf16[32,6,256]{2,1,0:T(8,128)(2,1)}), bf16[32,6,256]{2,1,0:T(8,128)(2,1)S(1)}, u32[]{:S(2)}, u32[]{:S(2)}) async-start(bf16[32,6,256]{2,1,0:T(8,128)(2,1)} %all_to_all.26), calls=%async_computation | async-start | bytes 262144 | tf_op jit(solution)/shard_map/all_to_all | solution.py:73
  42.5 46.9 %all-to-all-start.2 = ((bf16[8,32,2,3,88]{4,1,3,2,0:T(8,128)(2,1)}), bf16[8,32,2,3,88]{4,1,3,2,0:T(8,128)(2,1)S(1)}, u32[]{:S(2)}, u32[]{:S(2)}) async-start(bf16[8,32,2,3,88]{4,1,3,2,0:T(8,128)(2,1)} %copy.152), calls=%async_computation.2 | async-start | bytes 786432 | tf_op jit(solution)/shard_map/all_to_all | solution.py:41
  87.4 2.1 %copy-start.5 = (bf16[2,88,2048]{2,1,0:T(8,128)(2,1)S(1)}, bf16[2,88,2048]{2,1,0:T(8,128)(2,1)}, u32[]{:S(2)}) copy-start(bf16[2,88,2048]{2,1,0:T(8,128)(2,1)} %param.12) | copy-start | bytes 2162692
  125.9 11.2 %copy-start.2 = (bf16[2,88,16,128,1]{3,2,1,0,4:T(8,128)(2,1)S(1)}, bf16[2,88,16,128,1]{3,2,1,0,4:T(8,128)(2,1)}, u32[]{:S(2)}) copy-start(bf16[2,88,16,128,1]{3,2,1,0,4:T(8,128)(2,1)} %bitcast_bitcast_fusion.1) | copy-start | bytes 2162692
  126.9 31.7 %collective-permute-start = (bf16[2,88,1024]{2,1,0:T(8,128)(2,1)}, bf16[2,88,1024]{2,1,0:T(8,128)(2,1)}, u32[]{:S(2)}, u32[]{:S(2)}) collective-permute-start(bf16[2,88,1024]{2,1,0:T(8,128)(2,1)} %fusion.21), channel_id=1, source_target_pairs={{0,512},{512,0},{1,513},{513,1},{2,514},{514,2},{3,515},{515,3},{4... | collective-permute-start | bytes 1081352 | tf_op jit(solution)/shard_map/ppermute | solution.py:24
  131.3 6.2 %copy-start.1 = (bf16[2,88,16,128,1]{3,2,1,0,4:T(8,128)(2,1)S(1)}, bf16[2,88,16,128,1]{3,2,1,0,4:T(8,128)(2,1)}, u32[]{:S(2)}) copy-start(bf16[2,88,16,128,1]{3,2,1,0,4:T(8,128)(2,1)} %bitcast_bitcast_fusion) | copy-start | bytes 2162692
  132.2 34.3 %collective-permute-start.1 = (bf16[2,88,1024]{2,1,0:T(8,128)(2,1)}, bf16[2,88,1024]{2,1,0:T(8,128)(2,1)}, u32[]{:S(2)}, u32[]{:S(2)}) collective-permute-start(bf16[2,88,1024]{2,1,0:T(8,128)(2,1)} %fusion.17), channel_id=1, source_target_pairs={{0,512},{512,0},{1,513},{513,1},{2,514},{514,2},{3,515},{515,3},{4... | collective-permute-start | bytes 1081352 | tf_op jit(solution)/shard_map/ppermute | solution.py:24
  143.8 24.6 %all-to-all-start.4 = ((bf16[8,32,2,3,128]{4,1,3,2,0:T(8,128)(2,1)}), bf16[8,32,2,3,128]{4,1,3,2,0:T(8,128)(2,1)S(1)}, u32[]{:S(2)}, u32[]{:S(2)}) async-start(bf16[8,32,2,3,128]{4,1,3,2,0:T(8,128)(2,1)} %copy.157), calls=%async_computation.4 | async-start | bytes 786432 | tf_op jit(solution)/shard_map/all_to_all | solution.py:41
  150.6 24.3 %collective-permute-start.2 = (bf16[2,704,128]{2,1,0:T(8,128)(2,1)}, bf16[2,704,128]{2,1,0:T(8,128)(2,1)}, u32[]{:S(2)}, u32[]{:S(2)}) collective-permute-start(bf16[2,704,128]{2,1,0:T(8,128)(2,1)} %fusion.13), channel_id=1, source_target_pairs={{0,512},{512,0},{1,513},{513,1},{2,514},{514,2},{3,515},{515,3},{4... | collective-permute-start | bytes 1081352 | tf_op jit(solution)/shard_map/ppermute | solution.py:24
  169.2 15.5 %all-to-all-start.5 = ((bf16[32,6,256]{2,1,0:T(8,128)(2,1)}), bf16[32,6,256]{2,1,0:T(8,128)(2,1)S(1)}, u32[]{:S(2)}, u32[]{:S(2)}) async-start(bf16[32,6,256]{2,1,0:T(8,128)(2,1)} %copy.158), calls=%async_computation.5 | async-start | bytes 262144 | tf_op jit(solution)/shard_map/all_to_all | solution.py:105

commit v6 on v4

--- a/solution.py
+++ b/solution.py
@@ -23,6 +23,14 @@
     send = lax.dynamic_index_in_dim(halves, 1 - me, 0, keepdims=False)
     got = lax.ppermute(send, "dp", perm=[(0, 1), (1, 0)])
     return (keep.astype(jnp.float32) + got.astype(jnp.float32)).astype(jnp.bfloat16)
+
+
+def gather_fsdp(part, axis):
+    shards = lax.axis_size("fsdp")
+    copies = jnp.broadcast_to(part[None], (shards,) + part.shape)
+    got = lax.all_to_all(copies, "fsdp", 0, 0, tiled=False)
+    got = jnp.moveaxis(got, 0, axis)
+    return got.reshape(part.shape[:axis] + (-1,) + part.shape[axis + 1:])
 
 
 def body(tokens, grad_out, expert_ids, gate_weights, w_gate, w_up, w_down):
@@ -58,7 +66,7 @@
         jnp.concatenate([outgoing, scaled_grad], axis=1),
         "expert", split_axis=0, concat_axis=0, tiled=True,
     )
-    rows_in = lax.all_gather(both_in[:, :local_feat], "fsdp", axis=1, tiled=True)
+    rows_in = gather_fsdp(both_in[:, :local_feat], 1)
     grads_in = both_in[:, local_feat:]
     received = rows_in.reshape(owners, exp_local, capacity, model_width)
     cotangent = grads_in.reshape(owners, exp_local, capacity, -1)
@@ -66,7 +74,7 @@
     up_pre = jnp.einsum("jecd,efd->jecf", received, w_up, preferred_element_type=jnp.float32)
     activation, slope_term = silu_parts(gate_pre)
     hidden = (activation * up_pre).astype(jnp.bfloat16)
-    hidden_all = lax.all_gather(hidden, "fsdp", axis=3, tiled=True)
+    hidden_all = gather_fsdp(hidden, 3)
     expert_out = jnp.einsum(
         "jecf,efd->jecd", hidden_all, w_down, preferred_element_type=jnp.float32
     ).astype(jnp.bfloat16)

time: 184 us -> 176 us (0.957)
  waiting for transfers between devices: 20.8 us -> 48.2 us
  starting transfers between devices: 54.3 us -> 28.6 us
  blocking collectives: 70.9 us -> 62.4 us
    all_gather x2 -> x0, blocking collectives: 70.9 us -> none  [the longest x1 39.1 us: body(): hidden_all = lax.all_gather(hidden, 'fsdp', axis=3, tiled=True)]
    all_to_all x0 -> x2, blocking collectives: none -> 62.4 us  [the longest x1 41.5 us: body(): lax.all_to_all(hidden_parts, 'fsdp', 0, 0, tiled=False).astype(jnp.float32)]
    all_to_all x2, starting transfers between devices: 30.2 us -> 7.02 us  [gather_fsdp(): got = lax.all_to_all(copies, 'fsdp', 0, 0, tiled=False)]
    all_to_all x2, waiting for transfers between devices: 9.68 us -> 25.3 us  [gather_fsdp(): got = lax.all_to_all(copies, 'fsdp', 0, 0, tiled=False)]
    ppermute x3, waiting for transfers between devices: 9.5 us -> 16.9 us  [dp_reduce(): got = lax.ppermute(send, 'dp', perm=[(0, 1), (1, 0)])]
    all_gather x1 -> x0, local copies, waits for them, and re-layouts: 4.95 us -> none  [body(): hidden_all = lax.all_gather(hidden, 'fsdp', axis=3, tiled=True)]
    all_to_all x1, waiting for transfers between devices: 1.61 us -> 5.95 us  [body(): lax.all_to_all(jnp.concatenate([expert_out.reshape(slot_count, -1), input...]
    all_to_all x1, starting transfers between devices: 6.51 us -> 4.18 us  [body(): lax.all_to_all(input_parts.astype(jnp.bfloat16), 'fsdp', 0, 0, tiled=False)]
  transfers between devices with their start and end apart: 7 -> 7, of which waited for: 3 -> 6; matrix products, arithmetic and copies ran while one was open for 12% -> 10% of each run, Pallas kernels for 0% -> 0%
where the time goes in v6:
time: 176 us; the launch traced here: 175 us
  blocking collectives  62.4 us (35%)
  waiting for transfers between devices  48.2 us (27%)
  starting transfers between devices  28.6 us (16%)
  local copies, waits for them, and re-layouts  14.9 us (8%)
  matrix products  11.1 us (6%)
  other arithmetic  8.89 us (5%)
    all_to_all x1, blocking collectives, body(): lax.all_to_all(hidden_parts, 'fsdp', 0, 0, tiled=False).astype(jnp.float32)  41.5 us
    all_to_all x2, waiting for transfers between devices, gather_fsdp(): got = lax.all_to_all(copies, 'fsdp', 0, 0, tiled=False)  25.3 us
    all_to_all x1, blocking collectives, body(): lax.all_to_all(jnp.concatenate([outgoing, scaled_grad], axis=1), 'expert'...  20.9 us
    ppermute x3, waiting for transfers between devices, dp_reduce(): got = lax.ppermute(send, 'dp', perm=[(0, 1), (1, 0)])  16.9 us
    ppermute x3, starting transfers between devices, dp_reduce(): got = lax.ppermute(send, 'dp', perm=[(0, 1), (1, 0)])  13.5 us
    all_to_all x2, starting transfers between devices, gather_fsdp(): got = lax.all_to_all(copies, 'fsdp', 0, 0, tiled=False)  7.02 us
    all_to_all x1, waiting for transfers between devices, body(): lax.all_to_all(jnp.concatenate([expert_out.reshape(slot_count, -1), input...  5.95 us
    all_to_all x1, starting transfers between devices, body(): lax.all_to_all(input_parts.astype(jnp.bfloat16), 'fsdp', 0, 0, tiled=False)  4.18 us
  transfers between devices with their start and end apart: 7, of which 6 were waited for; matrix products, arithmetic and copies ran while one was open for 10% of the time, Pallas kernels for 0%

profile of v6, /device:TPU:1, one launch (start us, length us, event | category | flops | bytes accessed | tf_op | source)
XLA Modules:
  0.0 175.1 jit_solution(3909243355855226833)
XLA Ops:
  0.6 0.0 copy-start
  0.6 0.8 copy.76
  1.5 0.1 eq.35
  1.6 0.6 reduce-window.6
  2.2 0.2 slice_reduce_fusion
  2.5 0.1 bitcast_bitcast_fusion.2
  2.6 0.1 reduce_sum.42
  2.7 0.1 copy.79
  2.8 0.7 multiply_add_fusion
  3.5 0.1 convert_reduce_fusion.1
  3.6 0.1 iota_compare_fusion
  3.7 0.8 copy.94
  4.5 0.3 fusion.26
  4.7 1.0 convolution_convert_fusion.2
  5.7 0.9 convolution_convert_fusion.3
  6.7 20.9 %all_to_all.41 = bf16[32,6,256]{2,1,0:T(8,128)(2,1)S(1)} all-to-all(bf16[32,6,256]{2,1,0:T(8,128)(2,1)S(1)} %all_to_all.26), channel_id=1, replica_groups=mesh['dp'=2,'expert'=32,'fsdp'=16] {'expert'}, dimensions={0} | all-to-all | bytes 196608 | tf_op jit(solution)/shard_map/all_to_all | solution.py:65
  27.7 0.7 fusion.3
  28.4 0.1 copy.85
  28.5 41.5 %all_to_all.42 = bf16[16,32,2,3,88]{4,1,3,2,0:T(8,128)(2,1)S(1)} all-to-all(bf16[16,32,2,3,88]{4,1,3,2,0:T(8,128)(2,1)S(1)} %copy.85), channel_id=1, replica_groups=mesh['dp'=2,'expert'=32,'fsdp'=16] {'fsdp'}, dimensions={0} | all-to-all | bytes 1081344 | tf_op jit(solution)/shard_map/all_to_all | solution.py:88
  70.0 1.0 broadcast_in_dim.4
  71.1 3.5 %all-to-all-start.1 = ((bf16[16,192,128]{2,1,0:T(8,128)(2,1)}), bf16[16,192,128]{2,1,0:T(8,128)(2,1)S(1)}, u32[]{:S(2)}, u32[]{:S(2)}) async-start(bf16[16,192,128]{2,1,0:T(8,128)(2,1)} %broadcast_in_dim.4), calls=%async_computation.1 | async-start | bytes 1572864 | tf_op jit(solution)/shard_map/all_to_all | solution.py:31
  74.6 1.0 copy.117
  75.6 1.3 copy.116
  76.9 2.1 %bitcast_bitcast_fusion = bf16[2,88,16,128,1]{3,2,1,0,4:T(8,128)(2,1)} fusion(bf16[2,88,16,128]{3,2,1,0:T(8,128)(2,1)} %bitcast.146), kind=kLoop, calls=%fused_computation.30 | loop fusion | bytes 1441792 | tf_op jit(solution)/shard_map/reshape | solution.py:93
  79.0 1.0 bitcast_bitcast_fusion.1
  80.0 0.2 convert_reduce_fusion
  80.2 16.5 %all-to-all-done.1 = bf16[16,192,128]{2,1,0:T(8,128)(2,1)S(1)} async-done(((bf16[16,192,128]{2,1,0:T(8,128)(2,1)}), bf16[16,192,128]{2,1,0:T(8,128)(2,1)S(1)}, u32[]{:S(2)}, u32[]{:S(2)}) %all-to-all-start.1) | async-done | bytes 786464 | tf_op jit(solution)/shard_map/all_to_all | solution.py:31
  96.6 0.5 copy.80
  97.1 0.3 reshape_reshape.3
  97.4 2.0 %convolution_bitcast_fusion.4 = f32[32,2,3,88]{3,0,2,1:T(8,128)S(1)} fusion(bf16[2,88,2048]{2,1,0:T(8,128)(2,1)} %param.11, bf16[32,2,3,2048]{3,2,1,0:T(4,128)(2,1)S(1)} %reshape_reshape.3), kind=kOutput, calls=%fused_computation.12 | convolution fusion | flops 69206016 | bytes 1574912 | tf_op jit(solution)/shard_map/jecd,efd->jecf/dot_general | solution.py:73
  99.4 0.8 multiply_convert_fusion.2
  100.2 0.8 fusion.1
  101.0 1.7 fusion.2
  102.7 0.1 slice_bitcast_fusion.4
  102.7 1.1 broadcast_in_dim.5
  103.8 3.5 %all-to-all-start.2 = ((bf16[16,32,2,3,88]{4,1,3,2,0:T(8,128)(2,1)}), bf16[16,32,2,3,88]{4,1,3,2,0:T(8,128)(2,1)S(1)}, u32[]{:S(2)}, u32[]{:S(2)}) async-start(bf16[16,32,2,3,88]{4,1,3,2,0:T(8,128)(2,1)} %broadcast_in_dim.5), calls=%async_computation.2 | async-start | bytes 1572864 | tf_op jit(solution)/shard_map/all_to_all | solution.py:31
  107.3 0.9 fusion.23
  108.2 4.4 %collective-permute-start = (bf16[2,88,1024]{2,1,0:T(8,128)(2,1)}, bf16[2,88,1024]{2,1,0:T(8,128)(2,1)S(1)}, u32[]{:S(2)}, u32[]{:S(2)}) collective-permute-start(bf16[2,88,1024]{2,1,0:T(8,128)(2,1)} %fusion.23), channel_id=1, source_target_pairs={{0,512},{512,0},{1,513},{513,1},{2,514},{514,2},{3,515},{515,3},{4... | collective-permute-start | bytes 1081352 | tf_op jit(solution)/shard_map/ppermute | solution.py:24
  112.6 1.1 slice_bitcast_fusion.2
  113.8 0.9 fusion.19
  114.6 4.8 %collective-permute-start.1 = (bf16[2,88,1024]{2,1,0:T(8,128)(2,1)}, bf16[2,88,1024]{2,1,0:T(8,128)(2,1)}, u32[]{:S(2)}, u32[]{:S(2)}) collective-permute-start(bf16[2,88,1024]{2,1,0:T(8,128)(2,1)} %fusion.19), channel_id=1, source_target_pairs={{0,512},{512,0},{1,513},{513,1},{2,514},{514,2},{3,515},{515,3},{4... | collective-permute-start | bytes 1081352 | tf_op jit(solution)/shard_map/ppermute | solution.py:24
  119.4 0.4 fusion.12
  119.8 0.4 fusion.4
  120.2 1.0 copy.88
  121.2 8.9 %all-to-all-done.2 = bf16[16,32,2,3,88]{4,1,3,2,0:T(8,128)(2,1)S(1)} async-done(((bf16[16,32,2,3,88]{4,1,3,2,0:T(8,128)(2,1)}), bf16[16,32,2,3,88]{4,1,3,2,0:T(8,128)(2,1)S(1)}, u32[]{:S(2)}, u32[]{:S(2)}) %all-to-all-start.2) | async-done | bytes 540704 | tf_op jit(solution)/shard_map/all_to_all | solution.py:31
  130.0 4.2 %all-to-all-start.4 = ((bf16[16,32,2,3,128]{4,1,3,2,0:T(8,128)(2,1)}), bf16[16,32,2,3,128]{4,1,3,2,0:T(8,128)(2,1)}, u32[]{:S(2)}, u32[]{:S(2)}) async-start(bf16[16,32,2,3,128]{4,1,3,2,0:T(8,128)(2,1)} %copy.88), calls=%async_computation.4 | async-start | bytes 1572864 | tf_op jit(solution)/shard_map/all_to_all | solution.py:98
  134.2 5.6 %collective-permute-done = bf16[2,88,1024]{2,1,0:T(8,128)(2,1)S(1)} collective-permute-done((bf16[2,88,1024]{2,1,0:T(8,128)(2,1)}, bf16[2,88,1024]{2,1,0:T(8,128)(2,1)S(1)}, u32[]{:S(2)}, u32[]{:S(2)}) %collective-permute-start) | collective-permute-done | bytes 360480 | tf_op jit(solution)/shard_map/ppermute | solution.py:24
  139.8 1.0 fusion.7
  140.8 6.9 %collective-permute-done.1 = bf16[2,88,1024]{2,1,0:T(8,128)(2,1)} collective-permute-done((bf16[2,88,1024]{2,1,0:T(8,128)(2,1)}, bf16[2,88,1024]{2,1,0:T(8,128)(2,1)}, u32[]{:S(2)}, u32[]{:S(2)}) %collective-permute-start.1) | collective-permute-done | bytes 360480 | tf_op jit(solution)/shard_map/ppermute | solution.py:24
  147.6 2.0 %fusion.6 = bf16[2,88,1024]{2,1,0:T(8,128)(2,1)} fusion(bf16[2,88,1024]{2,1,0:T(8,128)(2,1)} %collective-permute-done.1, s32[]{:T(128)S(6)} %select_n.12, bf16[1,2,88,1024]{3,2,1,0:T(8,128)(2,1)S(1)} %get-tuple-element.8, bf16[1,2,88,1024]{3,2,1,0:T(8,128)(2,1)S(1)} %get-tuple-element.7), kind=kLoop, calls=%fused_computation.35 | loop fusion | flops 901120 | bytes 1441796 | tf_op jit(solution)/shard_map/convert_element_type | solution.py:25
  149.6 0.5 copy.83
  150.1 0.9 reshape.64
  151.0 0.4 fusion
  151.5 0.1 fusion.15
  151.6 4.3 %collective-permute-start.2 = (bf16[2,704,128]{2,1,0:T(8,128)(2,1)S(1)}, bf16[2,704,128]{2,1,0:T(8,128)(2,1)S(1)}, u32[]{:S(2)}, u32[]{:S(2)}) collective-permute-start(bf16[2,704,128]{2,1,0:T(8,128)(2,1)S(1)} %fusion.15), channel_id=1, source_target_pairs={{0,512},{512,0},{1,513},{513,1},{2,514},{514,2},{3,515},{515,3},{4... | collective-permute-start | bytes 1081352 | tf_op jit(solution)/shard_map/ppermute | solution.py:24
  156.0 0.3 convolution_convert_fusion.1
  156.3 1.3 reduce_sum.45
  157.6 0.7 copy.89
  158.3 3.8 %all-to-all-start.5 = ((bf16[32,6,256]{2,1,0:T(8,128)(2,1)}), bf16[32,6,256]{2,1,0:T(8,128)(2,1)S(1)}, u32[]{:S(2)}, u32[]{:S(2)}) async-start(bf16[32,6,256]{2,1,0:T(8,128)(2,1)} %copy.89), calls=%async_computation.5 | async-start | bytes 262144 | tf_op jit(solution)/shard_map/all_to_all | solution.py:104
  162.1 4.5 %collective-permute-done.2 = bf16[2,704,128]{2,1,0:T(8,128)(2,1)S(1)} collective-permute-done((bf16[2,704,128]{2,1,0:T(8,128)(2,1)S(1)}, bf16[2,704,128]{2,1,0:T(8,128)(2,1)S(1)}, u32[]{:S(2)}, u32[]{:S(2)}) %collective-permute-start.2) | collective-permute-done | bytes 360480 | tf_op jit(solution)/shard_map/ppermute | solution.py:24
  166.6 0.9 fusion.5
  167.5 5.9 %all-to-all-done.5 = bf16[32,6,256]{2,1,0:T(8,128)(2,1)S(1)} async-done(((bf16[32,6,256]{2,1,0:T(8,128)(2,1)}), bf16[32,6,256]{2,1,0:T(8,128)(2,1)S(1)}, u32[]{:S(2)}, u32[]{:S(2)}) %all-to-all-start.5) | async-done | bytes 98336 | tf_op jit(solution)/shard_map/all_to_all | solution.py:104
  173.5 0.8 convolution_convert_fusion.4
  174.3 0.8 convolution_convert_fusion.5
  (23 shorter events, 0.4 us)
Async XLA Ops:
  0.6 27.1 %copy-start = (bf16[2,1408,128]{2,1,0:T(8,128)(2,1)S(1)}, bf16[2,1408,128]{2,1,0:T(8,128)(2,1)}, u32[]{:S(2)}) copy-start(bf16[2,1408,128]{2,1,0:T(8,128)(2,1)} %param.13) | copy-start | bytes 2162692
  70.0 4.6 %copy-start.3 = (bf16[2,88,2048]{2,1,0:T(8,128)(2,1)S(1)}, bf16[2,88,2048]{2,1,0:T(8,128)(2,1)}, u32[]{:S(2)}) copy-start(bf16[2,88,2048]{2,1,0:T(8,128)(2,1)} %param.12) | copy-start | bytes 2162692
  71.1 25.5 %all-to-all-start.1 = ((bf16[16,192,128]{2,1,0:T(8,128)(2,1)}), bf16[16,192,128]{2,1,0:T(8,128)(2,1)S(1)}, u32[]{:S(2)}, u32[]{:S(2)}) async-start(bf16[16,192,128]{2,1,0:T(8,128)(2,1)} %broadcast_in_dim.4), calls=%async_computation.1 | async-start | bytes 1572864 | tf_op jit(solution)/shard_map/all_to_all | solution.py:31
  97.4 2.0 %copy-start.4 = (bf16[2,88,2048]{2,1,0:T(8,128)(2,1)S(1)}, bf16[2,88,2048]{2,1,0:T(8,128)(2,1)}, u32[]{:S(2)}) copy-start(bf16[2,88,2048]{2,1,0:T(8,128)(2,1)} %param.12) | copy-start | bytes 2162692
  103.8 26.3 %all-to-all-start.2 = ((bf16[16,32,2,3,88]{4,1,3,2,0:T(8,128)(2,1)}), bf16[16,32,2,3,88]{4,1,3,2,0:T(8,128)(2,1)S(1)}, u32[]{:S(2)}, u32[]{:S(2)}) async-start(bf16[16,32,2,3,88]{4,1,3,2,0:T(8,128)(2,1)} %broadcast_in_dim.5), calls=%async_computation.2 | async-start | bytes 1572864 | tf_op jit(solution)/shard_map/all_to_all | solution.py:31
  107.3 12.1 %copy-start.2 = (bf16[2,88,16,128,1]{3,2,1,0,4:T(8,128)(2,1)S(1)}, bf16[2,88,16,128,1]{3,2,1,0,4:T(8,128)(2,1)}, u32[]{:S(2)}) copy-start(bf16[2,88,16,128,1]{3,2,1,0,4:T(8,128)(2,1)} %bitcast_bitcast_fusion.1) | copy-start | bytes 2162692
  108.2 31.6 %collective-permute-start = (bf16[2,88,1024]{2,1,0:T(8,128)(2,1)}, bf16[2,88,1024]{2,1,0:T(8,128)(2,1)S(1)}, u32[]{:S(2)}, u32[]{:S(2)}) collective-permute-start(bf16[2,88,1024]{2,1,0:T(8,128)(2,1)} %fusion.23), channel_id=1, source_target_pairs={{0,512},{512,0},{1,513},{513,1},{2,514},{514,2},{3,515},{515,3},{4... | collective-permute-start | bytes 1081352 | tf_op jit(solution)/shard_map/ppermute | solution.py:24
  113.7 6.0 %copy-start.1 = (bf16[2,88,16,128,1]{3,2,1,0,4:T(8,128)(2,1)S(1)}, bf16[2,88,16,128,1]{3,2,1,0,4:T(8,128)(2,1)}, u32[]{:S(2)}) copy-start(bf16[2,88,16,128,1]{3,2,1,0,4:T(8,128)(2,1)} %bitcast_bitcast_fusion) | copy-start | bytes 2162692
  114.6 33.0 %collective-permute-start.1 = (bf16[2,88,1024]{2,1,0:T(8,128)(2,1)}, bf16[2,88,1024]{2,1,0:T(8,128)(2,1)}, u32[]{:S(2)}, u32[]{:S(2)}) collective-permute-start(bf16[2,88,1024]{2,1,0:T(8,128)(2,1)} %fusion.19), channel_id=1, source_target_pairs={{0,512},{512,0},{1,513},{513,1},{2,514},{514,2},{3,515},{515,3},{4... | collective-permute-start | bytes 1081352 | tf_op jit(solution)/shard_map/ppermute | solution.py:24
  130.0 26.2 %all-to-all-start.4 = ((bf16[16,32,2,3,128]{4,1,3,2,0:T(8,128)(2,1)}), bf16[16,32,2,3,128]{4,1,3,2,0:T(8,128)(2,1)}, u32[]{:S(2)}, u32[]{:S(2)}) async-start(bf16[16,32,2,3,128]{4,1,3,2,0:T(8,128)(2,1)} %copy.88), calls=%async_computation.4 | async-start | bytes 1572864 | tf_op jit(solution)/shard_map/all_to_all | solution.py:98
  151.6 15.0 %collective-permute-start.2 = (bf16[2,704,128]{2,1,0:T(8,128)(2,1)S(1)}, bf16[2,704,128]{2,1,0:T(8,128)(2,1)S(1)}, u32[]{:S(2)}, u32[]{:S(2)}) collective-permute-start(bf16[2,704,128]{2,1,0:T(8,128)(2,1)S(1)} %fusion.15), channel_id=1, source_target_pairs={{0,512},{512,0},{1,513},{513,1},{2,514},{514,2},{3,515},{515,3},{4... | collective-permute-start | bytes 1081352 | tf_op jit(solution)/shard_map/ppermute | solution.py:24
  158.3 15.2 %all-to-all-start.5 = ((bf16[32,6,256]{2,1,0:T(8,128)(2,1)}), bf16[32,6,256]{2,1,0:T(8,128)(2,1)S(1)}, u32[]{:S(2)}, u32[]{:S(2)}) async-start(bf16[32,6,256]{2,1,0:T(8,128)(2,1)} %copy.89), calls=%async_computation.5 | async-start | bytes 262144 | tf_op jit(solution)/shard_map/all_to_all | solution.py:104

commit v7 on v6

--- a/solution.py
+++ b/solution.py
@@ -114,18 +114,36 @@
     grad_tokens = jnp.dot(
         picker.T, input_slots.astype(jnp.float32), precision=lax.Precision.HIGHEST
     ).astype(jnp.bfloat16)
-    grad_gate_w = rounded(
-        jnp.einsum("jecf,jecd->efd", grad_gate_pre, received, preferred_element_type=jnp.float32)
+    me = lax.axis_index("dp")
+    half_feat = model_width // 2
+    half_ff = hidden_all.shape[3] // 2
+
+    def half(values, which):
+        size = values.shape[3] // 2
+        return lax.dynamic_slice_in_dim(values, which * size, size, axis=3)
+
+    first = lax.ppermute(
+        jnp.concatenate([half(received, 1 - me), cotangent], axis=3), "dp", perm=[(0, 1), (1, 0)]
     )
-    grad_up_w = rounded(
-        jnp.einsum("jecf,jecd->efd", grad_up_pre, received, preferred_element_type=jnp.float32)
+    rows_other, cot_other = first[..., :half_feat], first[..., half_feat:]
+    second = lax.ppermute(
+        jnp.concatenate([grad_gate_pre, grad_up_pre, half(hidden_all, 1 - me)], axis=3),
+        "dp", perm=[(0, 1), (1, 0)],
     )
-    grad_down_w = rounded(
-        jnp.einsum("jecf,jecd->efd", hidden_all, cotangent, preferred_element_type=jnp.float32)
-    )
-    summed_gate = dp_reduce(grad_gate_w.astype(jnp.bfloat16), 2).astype(jnp.float32)
-    summed_up = dp_reduce(grad_up_w.astype(jnp.bfloat16), 2).astype(jnp.float32)
-    summed_down = dp_reduce(grad_down_w.astype(jnp.bfloat16), 1)
+    ff_local = grad_gate_pre.shape[3]
+    gate_other = second[..., :ff_local]
+    up_other = second[..., ff_local:2 * ff_local]
+    hidden_other = second[..., 2 * ff_local:]
+    rows_mine = half(received, me)
+
+    def group_sum(left, right):
+        return rounded(jnp.einsum("jecf,jecd->efd", left, right, preferred_element_type=jnp.float32))
+
+    summed_gate = group_sum(grad_gate_pre, rows_mine) + group_sum(gate_other, rows_other)
+    summed_up = group_sum(grad_up_pre, rows_mine) + group_sum(up_other, rows_other)
+    summed_down = (
+        group_sum(half(hidden_all, me), cotangent) + group_sum(hidden_other, cot_other)
+    ).astype(jnp.bfloat16)
     return (
         mixed,
         grad_tokens,

time: 176 us -> 179 us (1.017)
  waiting for transfers between devices: 48.2 us -> 56.6 us
  starting transfers between devices: 28.6 us -> 23.3 us
  other arithmetic: 8.89 us -> 5.72 us
  matrix products: 11.1 us -> 13.8 us
    ppermute x3 -> x2, starting transfers between devices: 13.5 us -> 8.82 us  [the longest x1 4.41 us: body(): lax.ppermute(jnp.concatenate([grad_gate_pre, grad_up_pre, half(hidden_all...]
    all_to_all x2, waiting for transfers between devices: 25.3 us -> 29.8 us  [gather_fsdp(): got = lax.all_to_all(copies, 'fsdp', 0, 0, tiled=False)]
    dot_general x3 -> x6, matrix products: 2.88 us -> 6.53 us  [group_sum(): jnp.einsum('jecf,jecd->efd', left, right, preferred_element_type=jnp.floa...]
    all_to_all x1, waiting for transfers between devices: 5.95 us -> 9.09 us  [body(): lax.all_to_all(jnp.concatenate([expert_out.reshape(slot_count, -1), input...]
    squeeze x3 -> x0, other arithmetic: 1.91 us -> none  [dp_reduce(): send = lax.dynamic_index_in_dim(halves, 1 - me, 0, keepdims=False)]
    convert_element_type x3 -> x2, other arithmetic: 3.85 us -> 1.95 us  [the longest x1 1.12 us: body(): summed_up.astype(jnp.bfloat16)]
    ppermute x3 -> x2, waiting for transfers between devices: 16.9 us -> 17.6 us  [the longest x1 17.6 us: body(): lax.ppermute(jnp.concatenate([grad_gate_pre, grad_up_pre, half(hidden_all...]
    unnamed x14 -> x30, local copies, waits for them, and re-layouts: 3.91 us -> 4.01 us
  transfers between devices with their start and end apart: 7 -> 6, of which waited for: 6 -> 4; matrix products, arithmetic and copies ran while one was open for 10% -> 12% of each run, Pallas kernels for 0% -> 0%
where the time goes in v7:
time: 179 us; the launch traced here: 178 us
  blocking collectives  62.4 us (35%)
  waiting for transfers between devices  56.6 us (32%)
  starting transfers between devices  23.3 us (13%)
  local copies, waits for them, and re-layouts  14.6 us (8%)
  matrix products  13.8 us (8%)
  other arithmetic  5.72 us (3%)
    all_to_all x1, blocking collectives, body(): lax.all_to_all(hidden_parts, 'fsdp', 0, 0, tiled=False).astype(jnp.float32)  41.5 us
    all_to_all x2, waiting for transfers between devices, gather_fsdp(): got = lax.all_to_all(copies, 'fsdp', 0, 0, tiled=False)  29.8 us
    all_to_all x1, blocking collectives, body(): lax.all_to_all(jnp.concatenate([outgoing, scaled_grad], axis=1), 'expert'...  20.9 us
    ppermute x1, waiting for transfers between devices, body(): lax.ppermute(jnp.concatenate([grad_gate_pre, grad_up_pre, half(hidden_all...  17.6 us
    all_to_all x1, waiting for transfers between devices, body(): lax.all_to_all(jnp.concatenate([expert_out.reshape(slot_count, -1), input...  9.09 us
    all_to_all x2, starting transfers between devices, gather_fsdp(): got = lax.all_to_all(copies, 'fsdp', 0, 0, tiled=False)  7.15 us
    dot_general x6, matrix products, group_sum(): jnp.einsum('jecf,jecd->efd', left, right, preferred_element_type=jnp.floa...  6.53 us
    ppermute x1, starting transfers between devices, body(): lax.ppermute(jnp.concatenate([grad_gate_pre, grad_up_pre, half(hidden_all...  4.41 us
  transfers between devices with their start and end apart: 6, of which 4 were waited for; matrix products, arithmetic and copies ran while one was open for 12% of the time, Pallas kernels for 0%

profile of v7, /device:TPU:1, one launch (start us, length us, event | category | flops | bytes accessed | tf_op | source)
XLA Modules:
  0.0 177.6 jit_solution(10513920416484691244)
XLA Ops:
  0.6 0.0 copy-start
  0.6 0.8 copy.80
  1.5 0.1 eq.35
  1.6 0.6 reduce-window.6
  2.2 0.2 slice_reduce_fusion
  2.5 0.1 bitcast_bitcast_fusion.2
  2.6 0.1 reduce_sum.42
  2.7 0.1 copy.83
  2.8 0.7 multiply_add_fusion
  3.5 0.1 iota_compare_fusion
  3.6 0.1 convert_reduce_fusion.1
  3.7 0.8 copy.99
  4.5 0.3 fusion.20
  4.8 1.0 convolution_convert_fusion.2
  5.8 0.9 convolution_convert_fusion.3
  6.7 20.9 %all_to_all.41 = bf16[32,6,256]{2,1,0:T(8,128)(2,1)S(1)} all-to-all(bf16[32,6,256]{2,1,0:T(8,128)(2,1)S(1)} %all_to_all.26), channel_id=1, replica_groups=mesh['dp'=2,'expert'=32,'fsdp'=16] {'expert'}, dimensions={0} | all-to-all | bytes 196608 | tf_op jit(solution)/shard_map/all_to_all | solution.py:65
  27.8 0.7 fusion
  28.5 0.1 copy.89
  28.6 41.5 %all_to_all.42 = bf16[16,32,2,3,88]{4,1,3,2,0:T(8,128)(2,1)S(1)} all-to-all(bf16[16,32,2,3,88]{4,1,3,2,0:T(8,128)(2,1)S(1)} %copy.89), channel_id=1, replica_groups=mesh['dp'=2,'expert'=32,'fsdp'=16] {'fsdp'}, dimensions={0} | all-to-all | bytes 1081344 | tf_op jit(solution)/shard_map/all_to_all | solution.py:88
  70.1 1.0 broadcast_in_dim.4
  71.1 3.5 %all-to-all-start.1 = ((bf16[16,192,128]{2,1,0:T(8,128)(2,1)}), bf16[16,192,128]{2,1,0:T(8,128)(2,1)S(1)}, u32[]{:S(2)}, u32[]{:S(2)}) async-start(bf16[16,192,128]{2,1,0:T(8,128)(2,1)} %broadcast_in_dim.4), calls=%async_computation.1 | async-start | bytes 1572864 | tf_op jit(solution)/shard_map/all_to_all | solution.py:31
  74.7 1.0 copy.124
  75.7 0.1 copy-done.5
  75.8 1.0 copy.125
  76.9 2.2 %bitcast_bitcast_fusion.1 = bf16[2,88,16,128,1]{3,2,1,0,4:T(8,128)(2,1)} fusion(bf16[2,88,16,128]{3,2,1,0:T(8,128)(2,1)} %bitcast.131), kind=kLoop, calls=%fused_computation.25 | loop fusion | bytes 1441792 | tf_op jit(solution)/shard_map/reshape | solution.py:92
  79.0 1.0 bitcast_bitcast_fusion
  80.1 0.2 convert_reduce_fusion
  80.2 16.5 %all-to-all-done.1 = bf16[16,192,128]{2,1,0:T(8,128)(2,1)S(1)} async-done(((bf16[16,192,128]{2,1,0:T(8,128)(2,1)}), bf16[16,192,128]{2,1,0:T(8,128)(2,1)S(1)}, u32[]{:S(2)}, u32[]{:S(2)}) %all-to-all-start.1) | async-done | bytes 786464 | tf_op jit(solution)/shard_map/all_to_all | solution.py:31
  96.7 0.5 copy.84
  97.2 0.3 reshape_reshape.3
  97.5 0.6 copy.85
  98.1 0.4 convolution_bitcast_fusion.7
  98.4 0.2 copy-done.6
  98.6 0.4 multiply_convert_fusion.2
  99.0 1.1 broadcast_in_dim.5
  100.0 3.6 %all-to-all-start.2 = ((bf16[16,32,2,3,88]{4,1,3,2,0:T(8,128)(2,1)}), bf16[16,32,2,3,88]{4,1,3,2,0:T(8,128)(2,1)S(1)}, u32[]{:S(2)}, u32[]{:S(2)}) async-start(bf16[16,32,2,3,88]{4,1,3,2,0:T(8,128)(2,1)} %broadcast_in_dim.5), calls=%async_computation.2 | async-start | bytes 1572864 | tf_op jit(solution)/shard_map/all_to_all | solution.py:31
  103.7 1.5 fusion.12
  105.2 0.4 fusion.1
  105.5 1.0 copy.92
  106.6 0.8 pad_maximum_fusion
  107.4 4.4 %collective-permute-start.1 = (bf16[32,2,3,1152]{3,0,2,1:T(8,128)(2,1)}, bf16[32,2,3,1152]{3,0,2,1:T(8,128)(2,1)}, u32[]{:S(2)}, u32[]{:S(2)}) collective-permute-start(bf16[32,2,3,1152]{3,0,2,1:T(8,128)(2,1)} %pad_maximum_fusion), channel_id=1, source_target_pairs={{0,512},{512,0},{1,513},{513,1},{2,514},{514,2},{3,515},{515,3},{4... | collective-permute-start | bytes 1327112 | tf_op jit(solution)/shard_map/ppermute | solution.py:125
  111.8 0.3 fusion.4
  112.1 1.0 fusion.2
  113.1 13.4 %all-to-all-done.2 = bf16[16,32,2,3,88]{4,1,3,2,0:T(8,128)(2,1)S(1)} async-done(((bf16[16,32,2,3,88]{4,1,3,2,0:T(8,128)(2,1)}), bf16[16,32,2,3,88]{4,1,3,2,0:T(8,128)(2,1)S(1)}, u32[]{:S(2)}, u32[]{:S(2)}) %all-to-all-start.2) | async-done | bytes 540704 | tf_op jit(solution)/shard_map/all_to_all | solution.py:31
  126.5 3.5 %all-to-all-start.4 = ((bf16[16,32,2,3,128]{4,1,3,2,0:T(8,128)(2,1)}), bf16[16,32,2,3,128]{4,1,3,2,0:T(8,128)(2,1)S(1)}, u32[]{:S(2)}, u32[]{:S(2)}) async-start(bf16[16,32,2,3,128]{4,1,3,2,0:T(8,128)(2,1)} %copy.92), calls=%async_computation.4 | async-start | bytes 1572864 | tf_op jit(solution)/shard_map/all_to_all | solution.py:98
  130.0 0.5 copy.87
  130.5 0.9 reshape.58
  131.5 0.2 constant_dynamic-slice_fusion.1
  131.6 1.0 pad_maximum_fusion.1
  132.6 4.4 %collective-permute-start = (bf16[32,2,3,880]{3,0,2,1:T(8,128)(2,1)S(1)}, bf16[32,2,3,880]{3,0,2,1:T(8,128)(2,1)S(1)}, u32[]{:S(2)}, u32[]{:S(2)}) collective-permute-start(bf16[32,2,3,880]{3,0,2,1:T(8,128)(2,1)S(1)} %pad_maximum_fusion.1), channel_id=1, source_target_pairs={{0,512},{512,0},{1,513},{513,1},{2,514},{514,2},{3,515},{515,3},{4... | collective-permute-start | bytes 1013768 | tf_op jit(solution)/shard_map/ppermute | solution.py:129
  137.0 0.5 fusion.6
  137.5 0.3 convolution_convert_fusion.1
  137.9 17.6 %collective-permute-done = bf16[32,2,3,880]{3,0,2,1:T(8,128)(2,1)S(1)} collective-permute-done((bf16[32,2,3,880]{3,0,2,1:T(8,128)(2,1)S(1)}, bf16[32,2,3,880]{3,0,2,1:T(8,128)(2,1)S(1)}, u32[]{:S(2)}, u32[]{:S(2)}) %collective-permute-start) | collective-permute-done | bytes 337952 | tf_op jit(solution)/shard_map/ppermute | solution.py:129
  155.5 1.4 fusion.5
  156.9 1.3 fusion.3
  158.2 2.0 %fusion.7 = bf16[2,704,128]{2,1,0:T(8,128)(2,1)} fusion(bf16[32,2,3,880]{3,0,2,1:T(8,128)(2,1)S(1)} %collective-permute-done, bf16[32,2,3,1152]{3,0,2,1:T(8,128)(2,1)} %collective-permute-done.1), kind=kOutput, calls=%fused_computation.16 | convolution fusion | flops 34783232 | bytes 704512 | tf_op jit(solution)/shard_map/jecf,jecd->efd/dot_general | solution.py:140
  160.2 1.1 add_convert_fusion.2
  161.3 0.1 reduce_sum.45
  161.5 0.7 copy.93
  162.2 3.9 %all-to-all-start.5 = ((bf16[32,6,256]{2,1,0:T(8,128)(2,1)}), bf16[32,6,256]{2,1,0:T(8,128)(2,1)S(1)}, u32[]{:S(2)}, u32[]{:S(2)}) async-start(bf16[32,6,256]{2,1,0:T(8,128)(2,1)} %copy.93), calls=%async_computation.5 | async-start | bytes 262144 | tf_op jit(solution)/shard_map/all_to_all | solution.py:104
  166.1 0.8 add_convert_fusion.1
  166.9 9.1 %all-to-all-done.5 = bf16[32,6,256]{2,1,0:T(8,128)(2,1)S(1)} async-done(((bf16[32,6,256]{2,1,0:T(8,128)(2,1)}), bf16[32,6,256]{2,1,0:T(8,128)(2,1)S(1)}, u32[]{:S(2)}, u32[]{:S(2)}) %all-to-all-start.5) | async-done | bytes 98336 | tf_op jit(solution)/shard_map/all_to_all | solution.py:104
  176.0 0.8 convolution_convert_fusion.5
  176.8 0.8 convolution_convert_fusion.4
  (39 shorter events, 0.4 us)
Async XLA Ops:
  0.6 27.1 %copy-start = (bf16[2,1408,128]{2,1,0:T(8,128)(2,1)S(1)}, bf16[2,1408,128]{2,1,0:T(8,128)(2,1)}, u32[]{:S(2)}) copy-start(bf16[2,1408,128]{2,1,0:T(8,128)(2,1)} %param.13) | copy-start | bytes 2162692
  3.7 3.0 %copy-start.9 = (f32[32,192]{1,0:T(8,128)}, f32[32,192]{1,0:T(8,128)S(1)}, u32[]{:S(2)}) copy-start(f32[32,192]{1,0:T(8,128)S(1)} %convert_reduce_fusion.1) | copy-start | bytes 73732
  4.8 1.9 %copy-start.11 = (f32[32,1,192]{2,1,0:T(1,128)}, f32[32,1,192]{2,1,0:T(1,128)S(1)}, u32[]{:S(2)}) copy-start(f32[32,1,192]{2,1,0:T(1,128)S(1)} %fusion.20) | copy-start | bytes 73732
  70.1 4.6 %copy-start.1 = (bf16[2,88,2048]{2,1,0:T(8,128)(2,1)S(1)}, bf16[2,88,2048]{2,1,0:T(8,128)(2,1)}, u32[]{:S(2)}) copy-start(bf16[2,88,2048]{2,1,0:T(8,128)(2,1)} %param.11) | copy-start | bytes 2162692
  71.1 25.5 %all-to-all-start.1 = ((bf16[16,192,128]{2,1,0:T(8,128)(2,1)}), bf16[16,192,128]{2,1,0:T(8,128)(2,1)S(1)}, u32[]{:S(2)}, u32[]{:S(2)}) async-start(bf16[16,192,128]{2,1,0:T(8,128)(2,1)} %broadcast_in_dim.4), calls=%async_computation.1 | async-start | bytes 1572864 | tf_op jit(solution)/shard_map/all_to_all | solution.py:31
  74.7 1.2 copy-start.5
  76.9 2.2 %copy-start.2 = (bf16[22,8,16,128]{3,2,1,0:T(8,128)(2,1)S(1)}, bf16[22,8,16,128]{3,2,1,0:T(8,128)(2,1)}, u32[]{:S(2)}) copy-start(bf16[22,8,16,128]{3,2,1,0:T(8,128)(2,1)} %copy.125) | copy-start | bytes 2162692
  97.5 1.1 copy-start.6
  98.9 12.8 %copy-start.7 = (bf16[32,2,3,88]{3,0,2,1:T(8,128)(2,1)}, bf16[32,2,3,88]{3,0,2,1:T(8,128)(2,1)S(1)}, u32[]{:S(2)}) copy-start(bf16[32,2,3,88]{3,0,2,1:T(8,128)(2,1)S(1)} %get-tuple-element.7) | copy-start | bytes 101380
  100.0 5.1 %copy-start.3 = (bf16[2,88,16,128,1]{3,2,1,0,4:T(8,128)(2,1)S(1)}, bf16[2,88,16,128,1]{3,2,1,0,4:T(8,128)(2,1)}, u32[]{:S(2)}) copy-start(bf16[2,88,16,128,1]{3,2,1,0,4:T(8,128)(2,1)} %bitcast_bitcast_fusion) | copy-start | bytes 2162692
  100.0 26.5 %all-to-all-start.2 = ((bf16[16,32,2,3,88]{4,1,3,2,0:T(8,128)(2,1)}), bf16[16,32,2,3,88]{4,1,3,2,0:T(8,128)(2,1)S(1)}, u32[]{:S(2)}, u32[]{:S(2)}) async-start(bf16[16,32,2,3,88]{4,1,3,2,0:T(8,128)(2,1)} %broadcast_in_dim.5), calls=%async_computation.2 | async-start | bytes 1572864 | tf_op jit(solution)/shard_map/all_to_all | solution.py:31
  107.4 30.5 %collective-permute-start.1 = (bf16[32,2,3,1152]{3,0,2,1:T(8,128)(2,1)}, bf16[32,2,3,1152]{3,0,2,1:T(8,128)(2,1)}, u32[]{:S(2)}, u32[]{:S(2)}) collective-permute-start(bf16[32,2,3,1152]{3,0,2,1:T(8,128)(2,1)} %pad_maximum_fusion), channel_id=1, source_target_pairs={{0,512},{512,0},{1,513},{513,1},{2,514},{514,2},{3,515},{515,3},{4... | collective-permute-start | bytes 1327112 | tf_op jit(solution)/shard_map/ppermute | solution.py:125
  126.5 34.8 %all-to-all-start.4 = ((bf16[16,32,2,3,128]{4,1,3,2,0:T(8,128)(2,1)}), bf16[16,32,2,3,128]{4,1,3,2,0:T(8,128)(2,1)S(1)}, u32[]{:S(2)}, u32[]{:S(2)}) async-start(bf16[16,32,2,3,128]{4,1,3,2,0:T(8,128)(2,1)} %copy.92), calls=%async_computation.4 | async-start | bytes 1572864 | tf_op jit(solution)/shard_map/all_to_all | solution.py:98
  132.6 22.9 %collective-permute-start = (bf16[32,2,3,880]{3,0,2,1:T(8,128)(2,1)S(1)}, bf16[32,2,3,880]{3,0,2,1:T(8,128)(2,1)S(1)}, u32[]{:S(2)}, u32[]{:S(2)}) collective-permute-start(bf16[32,2,3,880]{3,0,2,1:T(8,128)(2,1)S(1)} %pad_maximum_fusion.1), channel_id=1, source_target_pairs={{0,512},{512,0},{1,513},{513,1},{2,514},{514,2},{3,515},{515,3},{4... | collective-permute-start | bytes 1013768 | tf_op jit(solution)/shard_map/ppermute | solution.py:129
  137.5 22.7 %copy-start.4 = (bf16[2,88,1024]{2,1,0:T(8,128)(2,1)S(1)}, bf16[2,88,1024]{2,1,0:T(8,128)(2,1)}, u32[]{:S(2)}) copy-start(bf16[2,88,1024]{2,1,0:T(8,128)(2,1)} %fusion.2) | copy-start | bytes 1081348
  161.3 4.7 %copy-start.8 = (bf16[2,704,128]{2,1,0:T(8,128)(2,1)S(1)}, bf16[2,704,128]{2,1,0:T(8,128)(2,1)}, u32[]{:S(2)}) copy-start(bf16[2,704,128]{2,1,0:T(8,128)(2,1)} %fusion.7) | copy-start | bytes 1081348
  161.3 14.7 %copy-start.12 = (f32[32,1,192]{2,1,0:T(1,128)S(1)}, f32[32,1,192]{2,1,0:T(1,128)}, u32[]{:S(2)}) copy-start(f32[32,1,192]{2,1,0:T(1,128)} %copy-done.11) | copy-start | bytes 73732
  161.3 15.5 %copy-start.10 = (f32[32,192]{1,0:T(8,128)S(1)}, f32[32,192]{1,0:T(8,128)}, u32[]{:S(2)}) copy-start(f32[32,192]{1,0:T(8,128)} %copy-done.9) | copy-start | bytes 73732
  162.2 13.8 %all-to-all-start.5 = ((bf16[32,6,256]{2,1,0:T(8,128)(2,1)}), bf16[32,6,256]{2,1,0:T(8,128)(2,1)S(1)}, u32[]{:S(2)}, u32[]{:S(2)}) async-start(bf16[32,6,256]{2,1,0:T(8,128)(2,1)} %copy.93), calls=%async_computation.5 | async-start | bytes 262144 | tf_op jit(solution)/shard_map/all_to_all | solution.py:104

commit v8 on v6

--- a/solution.py
+++ b/solution.py
@@ -66,27 +66,35 @@
         jnp.concatenate([outgoing, scaled_grad], axis=1),
         "expert", split_axis=0, concat_axis=0, tiled=True,
     )
-    rows_in = gather_fsdp(both_in[:, :local_feat], 1)
     grads_in = both_in[:, local_feat:]
+    cotangent = grads_in.reshape(owners, exp_local, capacity, -1)
+    shards = lax.axis_size("fsdp")
+    exp_n, ff_all, feat = w_down.shape
+    ff_local = ff_all // shards
+    hidden_parts = jnp.einsum(
+        "jecd,egfd->gjecf", cotangent, w_down.reshape(exp_n, shards, ff_local, feat),
+        preferred_element_type=jnp.float32,
+    ).astype(jnp.bfloat16)
+    rows_part = both_in[:, :local_feat]
+    first = lax.all_to_all(
+        jnp.concatenate(
+            [
+                jnp.broadcast_to(rows_part[None], (shards,) + rows_part.shape),
+                hidden_parts.reshape(shards, slot_count, ff_local),
+            ],
+            axis=2,
+        ),
+        "fsdp", 0, 0, tiled=False,
+    )
+    rows_in = jnp.moveaxis(first[..., :local_feat], 0, 1).reshape(slot_count, model_width)
+    grad_hidden = jnp.sum(first[..., local_feat:].astype(jnp.float32), axis=0).reshape(
+        owners, exp_local, capacity, ff_local
+    )
     received = rows_in.reshape(owners, exp_local, capacity, model_width)
-    cotangent = grads_in.reshape(owners, exp_local, capacity, -1)
     gate_pre = jnp.einsum("jecd,efd->jecf", received, w_gate, preferred_element_type=jnp.float32)
     up_pre = jnp.einsum("jecd,efd->jecf", received, w_up, preferred_element_type=jnp.float32)
     activation, slope_term = silu_parts(gate_pre)
     hidden = (activation * up_pre).astype(jnp.bfloat16)
-    hidden_all = gather_fsdp(hidden, 3)
-    expert_out = jnp.einsum(
-        "jecf,efd->jecd", hidden_all, w_down, preferred_element_type=jnp.float32
-    ).astype(jnp.bfloat16)
-    shards = lax.axis_size("fsdp")
-    exp_n, ff_all, feat = w_down.shape
-    hidden_parts = jnp.einsum(
-        "jecd,egfd->gjecf", cotangent, w_down.reshape(exp_n, shards, ff_all // shards, feat),
-        preferred_element_type=jnp.float32,
-    ).astype(jnp.bfloat16)
-    grad_hidden = jnp.sum(
-        lax.all_to_all(hidden_parts, "fsdp", 0, 0, tiled=False).astype(jnp.float32), axis=0
-    )
     grad_gate_pre = (grad_hidden * up_pre * slope_term).astype(jnp.bfloat16)
     grad_up_pre = (grad_hidden * activation).astype(jnp.bfloat16)
     w_gate_g = w_gate.reshape(exp_n, w_gate.shape[1], shards, model_width // shards)
@@ -94,11 +102,23 @@
     input_parts = jnp.einsum(
         "jecf,efgd->gjecd", grad_gate_pre, w_gate_g, preferred_element_type=jnp.float32
     ) + jnp.einsum("jecf,efgd->gjecd", grad_up_pre, w_up_g, preferred_element_type=jnp.float32)
-    input_slices = jnp.sum(
-        lax.all_to_all(input_parts.astype(jnp.bfloat16), "fsdp", 0, 0, tiled=False).astype(
-            jnp.float32
+    hidden_flat = hidden.reshape(slot_count, ff_local)
+    second = lax.all_to_all(
+        jnp.concatenate(
+            [
+                jnp.broadcast_to(hidden_flat[None], (shards,) + hidden_flat.shape),
+                input_parts.astype(jnp.bfloat16).reshape(shards, slot_count, feat),
+            ],
+            axis=2,
         ),
-        axis=0,
+        "fsdp", 0, 0, tiled=False,
+    )
+    hidden_all = jnp.moveaxis(second[..., :ff_local], 0, 1).reshape(
+        owners, exp_local, capacity, ff_all
+    )
+    input_slices = jnp.sum(second[..., ff_local:].astype(jnp.float32), axis=0).astype(jnp.bfloat16)
+    expert_out = jnp.einsum(
+        "jecf,efd->jecd", hidden_all, w_down, preferred_element_type=jnp.float32
     ).astype(jnp.bfloat16)
     feat = input_slices.shape[-1]
     both_back = lax.all_to_all(

time: 176 us -> 181 us (1.028)
  the two profiles are of different devices: /device:TPU:1 before, /device:TPU:5 now
where the time goes in v8:
time: 181 us; the launch traced here: 180 us
  waiting for transfers between devices  74.6 us (41%)
  starting transfers between devices  47.2 us (26%)
  blocking collectives  18 us (10%)
  local copies, waits for them, and re-layouts  16.1 us (9%)
  matrix products  12.1 us (7%)
  other arithmetic  10.9 us (6%)
    all_to_all x1, waiting for transfers between devices, body(): lax.all_to_all(jnp.concatenate([jnp.broadcast_to(rows_part[None], (shards...  35 us
    ppermute x3, waiting for transfers between devices, dp_reduce(): got = lax.ppermute(send, 'dp', perm=[(0, 1), (1, 0)])  27.4 us
    all_to_all x1, starting transfers between devices, body(): lax.all_to_all(jnp.concatenate([jnp.broadcast_to(rows_part[None], (shards...  18.9 us
    all_to_all x1, blocking collectives, body(): lax.all_to_all(jnp.concatenate([outgoing, scaled_grad], axis=1), 'expert'...  18 us
    ppermute x3, starting transfers between devices, dp_reduce(): got = lax.ppermute(send, 'dp', perm=[(0, 1), (1, 0)])  13.6 us
    all_to_all x1, starting transfers between devices, body(): lax.all_to_all(jnp.concatenate([expert_out.reshape(slot_count, -1), input...  10.4 us
    all_to_all x1, waiting for transfers between devices, body(): lax.all_to_all(jnp.concatenate([jnp.broadcast_to(hidden_flat[None], (shar...  8.56 us
    unnamed x24, local copies, waits for them, and re-layouts  4.48 us
  transfers between devices with their start and end apart: 6, of which 6 were waited for; matrix products, arithmetic and copies ran while one was open for 7% of the time, Pallas kernels for 0%

profile of v8, /device:TPU:5, one launch (start us, length us, event | category | flops | bytes accessed | tf_op | source)
XLA Modules:
  0.0 179.9 jit_solution(17607208980784208472)
XLA Ops:
  0.6 0.8 copy.84
  1.6 0.6 reduce-window.6
  2.2 0.2 slice_reduce_fusion.1
  2.8 0.7 multiply_add_fusion
  3.7 0.8 copy.109
  4.5 0.3 fusion.28
  4.7 1.0 convolution_convert_fusion.2
  5.7 0.9 convolution_convert_fusion.3
  6.7 18.0 %all_to_all.31 = bf16[32,6,256]{2,1,0:T(8,128)(2,1)S(1)} all-to-all(bf16[32,6,256]{2,1,0:T(8,128)(2,1)S(1)} %all_to_all.20), channel_id=1, replica_groups=mesh['dp'=2,'expert'=32,'fsdp'=16] {'expert'}, dimensions={0} | all-to-all | bytes 196608 | tf_op jit(solution)/shard_map/all_to_all | solution.py:65
  24.8 0.7 fusion.3
  25.5 0.3 copy.89
  25.8 0.2 copy.90
  26.0 0.1 broadcast_in_dim.6
  26.1 1.5 pad_maximum_fusion
  27.6 18.9 %all-to-all-start.1 = ((bf16[16,192,216]{2,1,0:T(8,128)(2,1)}), bf16[16,192,216]{2,1,0:T(8,128)(2,1)S(1)}, u32[]{:S(2)}, u32[]{:S(2)}) async-start(bf16[16,192,216]{2,1,0:T(8,128)(2,1)} %pad_maximum_fusion), calls=%async_computation.1 | async-start | bytes 3145728 | tf_op jit(solution)/shard_map/all_to_all | solution.py:79
  46.6 1.3 copy.131
  47.9 0.1 copy.132
  48.0 1.0 bitcast_bitcast_fusion.1
  49.0 1.0 bitcast_bitcast_fusion
  50.0 35.0 %all-to-all-done.1 = bf16[16,192,216]{2,1,0:T(8,128)(2,1)S(1)} async-done(((bf16[16,192,216]{2,1,0:T(8,128)(2,1)}), bf16[16,192,216]{2,1,0:T(8,128)(2,1)S(1)}, u32[]{:S(2)}, u32[]{:S(2)}) %all-to-all-start.1) | async-done | bytes 1327136 | tf_op jit(solution)/shard_map/all_to_all | solution.py:79
  85.0 0.2 convert_reduce_fusion
  85.2 0.7 reshape.74
  86.0 0.5 copy.91
  86.6 0.3 reshape_reshape.3
  86.8 0.3 copy-done.6
  87.1 0.8 convolution_bitcast_fusion.3
  87.9 0.3 copy-done.7
  88.3 0.8 multiply_convert_fusion
  89.1 0.2 copy-done.3
  89.4 0.4 fusion.12
  89.7 0.6 copy-done.4
  90.3 0.4 fusion.4
  90.7 0.3 copy.99
  91.0 0.7 broadcast_in_dim.7
  91.7 0.9 broadcast_in_dim.8
  92.6 0.7 pad_maximum_fusion.1
  93.3 1.7 copy.100
  95.0 4.3 %all-to-all-start.2 = ((bf16[16,192,216]{2,1,0:T(8,128)(2,1)}), bf16[16,192,216]{2,1,0:T(8,128)(2,1)S(1)}, u32[]{:S(2)}, u32[]{:S(2)}) async-start(bf16[16,192,216]{2,1,0:T(8,128)(2,1)} %copy.100), calls=%async_computation.2 | async-start | bytes 3145728 | tf_op jit(solution)/shard_map/all_to_all | solution.py:106
  99.3 1.6 fusion.1
  101.0 1.0 fusion.25
  101.9 4.4 %collective-permute-start = (bf16[2,88,1024]{2,1,0:T(8,128)(2,1)}, bf16[2,88,1024]{2,1,0:T(8,128)(2,1)}, u32[]{:S(2)}, u32[]{:S(2)}) collective-permute-start(bf16[2,88,1024]{2,1,0:T(8,128)(2,1)} %fusion.25), channel_id=1, source_target_pairs={{0,512},{512,0},{1,513},{513,1},{2,514},{514,2},{3,515},{515,3},{4... | collective-permute-start | bytes 1081352 | tf_op jit(solution)/shard_map/ppermute | solution.py:24
  106.4 0.8 fusion.2
  107.2 0.9 fusion.21
  108.1 4.9 %collective-permute-start.1 = (bf16[2,88,1024]{2,1,0:T(8,128)(2,1)}, bf16[2,88,1024]{2,1,0:T(8,128)(2,1)S(1)}, u32[]{:S(2)}, u32[]{:S(2)}) collective-permute-start(bf16[2,88,1024]{2,1,0:T(8,128)(2,1)} %fusion.21), channel_id=1, source_target_pairs={{0,512},{512,0},{1,513},{513,1},{2,514},{514,2},{3,515},{515,3},{4... | collective-permute-start | bytes 1081352 | tf_op jit(solution)/shard_map/ppermute | solution.py:24
  113.1 5.9 %collective-permute-done = bf16[2,88,1024]{2,1,0:T(8,128)(2,1)} collective-permute-done((bf16[2,88,1024]{2,1,0:T(8,128)(2,1)}, bf16[2,88,1024]{2,1,0:T(8,128)(2,1)}, u32[]{:S(2)}, u32[]{:S(2)}) %collective-permute-start) | collective-permute-done | bytes 360480 | tf_op jit(solution)/shard_map/ppermute | solution.py:24
  119.0 2.0 %fusion.7 = bf16[2,88,1024]{2,1,0:T(8,128)(2,1)} fusion(bf16[2,88,1024]{2,1,0:T(8,128)(2,1)} %collective-permute-done, s32[]{:T(128)S(6)} %select_n.12, bf16[1,2,88,1024]{3,2,1,0:T(8,128)(2,1)} %copy-done.2, bf16[1,2,88,1024]{3,2,1,0:T(8,128)(2,1)} %copy-done.1), kind=kLoop, calls=%fused_computation.42 | loop fusion | flops 901120 | bytes 1441796 | tf_op jit(solution)/shard_map/convert_element_type | solution.py:25
  121.0 7.2 %collective-permute-done.1 = bf16[2,88,1024]{2,1,0:T(8,128)(2,1)S(1)} collective-permute-done((bf16[2,88,1024]{2,1,0:T(8,128)(2,1)}, bf16[2,88,1024]{2,1,0:T(8,128)(2,1)S(1)}, u32[]{:S(2)}, u32[]{:S(2)}) %collective-permute-start.1) | collective-permute-done | bytes 360480 | tf_op jit(solution)/shard_map/ppermute | solution.py:24
  128.2 1.0 fusion.6
  129.2 8.6 %all-to-all-done.2 = bf16[16,192,216]{2,1,0:T(8,128)(2,1)S(1)} async-done(((bf16[16,192,216]{2,1,0:T(8,128)(2,1)}), bf16[16,192,216]{2,1,0:T(8,128)(2,1)S(1)}, u32[]{:S(2)}, u32[]{:S(2)}) %all-to-all-start.2) | async-done | bytes 1327136 | tf_op jit(solution)/shard_map/all_to_all | solution.py:106
  137.7 0.1 slice_bitcast_fusion
  137.9 0.5 copy.101
  138.4 2.3 %reshape.78 = bf16[32,2,3,1408]{3,2,1,0:T(4,128)(2,1)} reshape(bf16[192,16,88]{2,1,0:T(8,128)(2,1)S(1)} %copy.101) | data formatting | bytes 1081344 | tf_op jit(solution)/shard_map/reshape | solution.py:116
  140.6 1.4 convolution_convert_fusion.1
  142.1 1.5 fusion
  143.6 0.3 slice_reduce_fusion
  143.9 0.7 pad_maximum_fusion.2
  144.6 10.4 %all-to-all-start.3 = ((bf16[32,6,256]{2,1,0:T(8,128)(2,1)}), bf16[32,6,256]{2,1,0:T(8,128)(2,1)S(1)}, u32[]{:S(2)}, u32[]{:S(2)}) async-start(bf16[32,6,256]{2,1,0:T(8,128)(2,1)} %pad_maximum_fusion.2), calls=%async_computation.3 | async-start | bytes 262144 | tf_op jit(solution)/shard_map/all_to_all | solution.py:124
  155.0 0.1 fusion.17
  155.2 4.2 %collective-permute-start.2 = (bf16[2,704,128]{2,1,0:T(8,128)(2,1)S(1)}, bf16[2,704,128]{2,1,0:T(8,128)(2,1)S(1)}, u32[]{:S(2)}, u32[]{:S(2)}) collective-permute-start(bf16[2,704,128]{2,1,0:T(8,128)(2,1)S(1)} %fusion.17), channel_id=1, source_target_pairs={{0,512},{512,0},{1,513},{513,1},{2,514},{514,2},{3,515},{515,3},{4... | collective-permute-start | bytes 1081352 | tf_op jit(solution)/shard_map/ppermute | solution.py:24
  159.4 3.7 %all-to-all-done.3 = bf16[32,6,256]{2,1,0:T(8,128)(2,1)S(1)} async-done(((bf16[32,6,256]{2,1,0:T(8,128)(2,1)}), bf16[32,6,256]{2,1,0:T(8,128)(2,1)S(1)}, u32[]{:S(2)}, u32[]{:S(2)}) %all-to-all-start.3) | async-done | bytes 98336 | tf_op jit(solution)/shard_map/all_to_all | solution.py:124
  163.1 0.8 convolution_convert_fusion.5
  163.9 0.8 convolution_convert_fusion.4
  164.7 14.3 %collective-permute-done.2 = bf16[2,704,128]{2,1,0:T(8,128)(2,1)S(1)} collective-permute-done((bf16[2,704,128]{2,1,0:T(8,128)(2,1)S(1)}, bf16[2,704,128]{2,1,0:T(8,128)(2,1)S(1)}, u32[]{:S(2)}, u32[]{:S(2)}) %collective-permute-start.2) | collective-permute-done | bytes 360480 | tf_op jit(solution)/shard_map/ppermute | solution.py:24
  179.0 0.9 fusion.5
  (40 shorter events, 1.2 us)
Async XLA Ops:
  0.6 24.1 %copy-start = (bf16[2,1408,128]{2,1,0:T(8,128)(2,1)S(1)}, bf16[2,1408,128]{2,1,0:T(8,128)(2,1)}, u32[]{:S(2)}) copy-start(bf16[2,1408,128]{2,1,0:T(8,128)(2,1)} %param.13) | copy-start | bytes 2162692
  27.6 20.2 %copy-start.5 = (bf16[2,88,2048]{2,1,0:T(8,128)(2,1)S(1)}, bf16[2,88,2048]{2,1,0:T(8,128)(2,1)}, u32[]{:S(2)}) copy-start(bf16[2,88,2048]{2,1,0:T(8,128)(2,1)} %param.12) | copy-start | bytes 2162692
  27.6 57.4 %all-to-all-start.1 = ((bf16[16,192,216]{2,1,0:T(8,128)(2,1)}), bf16[16,192,216]{2,1,0:T(8,128)(2,1)S(1)}, u32[]{:S(2)}, u32[]{:S(2)}) async-start(bf16[16,192,216]{2,1,0:T(8,128)(2,1)} %pad_maximum_fusion), calls=%async_computation.1 | async-start | bytes 3145728 | tf_op jit(solution)/shard_map/all_to_all | solution.py:79
  86.0 1.1 copy-start.6
  87.1 1.1 copy-start.7
  87.1 1.1 copy-start.9
  88.3 1.1 copy-start.3
  89.1 1.6 copy-start.8
  89.1 1.2 copy-start.4
  95.0 42.7 %all-to-all-start.2 = ((bf16[16,192,216]{2,1,0:T(8,128)(2,1)}), bf16[16,192,216]{2,1,0:T(8,128)(2,1)S(1)}, u32[]{:S(2)}, u32[]{:S(2)}) async-start(bf16[16,192,216]{2,1,0:T(8,128)(2,1)} %copy.100), calls=%async_computation.2 | async-start | bytes 3145728 | tf_op jit(solution)/shard_map/all_to_all | solution.py:106
  100.9 6.3 %copy-start.1 = (bf16[1,2,88,1024]{3,2,1,0:T(8,128)(2,1)}, bf16[1,2,88,1024]{3,2,1,0:T(8,128)(2,1)S(1)}, u32[]{:S(2)}) copy-start(bf16[1,2,88,1024]{3,2,1,0:T(8,128)(2,1)S(1)} %get-tuple-element.9) | copy-start | bytes 1081348
  101.0 6.3 %copy-start.2 = (bf16[1,2,88,1024]{3,2,1,0:T(8,128)(2,1)}, bf16[1,2,88,1024]{3,2,1,0:T(8,128)(2,1)S(1)}, u32[]{:S(2)}) copy-start(bf16[1,2,88,1024]{3,2,1,0:T(8,128)(2,1)S(1)} %get-tuple-element.10) | copy-start | bytes 1081348
  101.9 17.1 %collective-permute-start = (bf16[2,88,1024]{2,1,0:T(8,128)(2,1)}, bf16[2,88,1024]{2,1,0:T(8,128)(2,1)}, u32[]{:S(2)}, u32[]{:S(2)}) collective-permute-start(bf16[2,88,1024]{2,1,0:T(8,128)(2,1)} %fusion.25), channel_id=1, source_target_pairs={{0,512},{512,0},{1,513},{513,1},{2,514},{514,2},{3,515},{515,3},{4... | collective-permute-start | bytes 1081352 | tf_op jit(solution)/shard_map/ppermute | solution.py:24
  108.1 20.1 %collective-permute-start.1 = (bf16[2,88,1024]{2,1,0:T(8,128)(2,1)}, bf16[2,88,1024]{2,1,0:T(8,128)(2,1)S(1)}, u32[]{:S(2)}, u32[]{:S(2)}) collective-permute-start(bf16[2,88,1024]{2,1,0:T(8,128)(2,1)} %fusion.21), channel_id=1, source_target_pairs={{0,512},{512,0},{1,513},{513,1},{2,514},{514,2},{3,515},{515,3},{4... | collective-permute-start | bytes 1081352 | tf_op jit(solution)/shard_map/ppermute | solution.py:24
  144.6 18.5 %all-to-all-start.3 = ((bf16[32,6,256]{2,1,0:T(8,128)(2,1)}), bf16[32,6,256]{2,1,0:T(8,128)(2,1)S(1)}, u32[]{:S(2)}, u32[]{:S(2)}) async-start(bf16[32,6,256]{2,1,0:T(8,128)(2,1)} %pad_maximum_fusion.2), calls=%async_computation.3 | async-start | bytes 262144 | tf_op jit(solution)/shard_map/all_to_all | solution.py:124
  155.2 23.8 %collective-permute-start.2 = (bf16[2,704,128]{2,1,0:T(8,128)(2,1)S(1)}, bf16[2,704,128]{2,1,0:T(8,128)(2,1)S(1)}, u32[]{:S(2)}, u32[]{:S(2)}) collective-permute-start(bf16[2,704,128]{2,1,0:T(8,128)(2,1)S(1)} %fusion.17), channel_id=1, source_target_pairs={{0,512},{512,0},{1,513},{513,1},{2,514},{514,2},{3,515},{515,3},{4... | collective-permute-start | bytes 1081352 | tf_op jit(solution)/shard_map/ppermute | solution.py:24

commit v9 on v6

--- a/solution.py
+++ b/solution.py
@@ -123,8 +123,9 @@
     grad_down_w = rounded(
         jnp.einsum("jecf,jecd->efd", hidden_all, cotangent, preferred_element_type=jnp.float32)
     )
-    summed_gate = dp_reduce(grad_gate_w.astype(jnp.bfloat16), 2).astype(jnp.float32)
-    summed_up = dp_reduce(grad_up_w.astype(jnp.bfloat16), 2).astype(jnp.float32)
+    summed_gate, summed_up = dp_reduce(
+        jnp.stack([grad_gate_w, grad_up_w]).astype(jnp.bfloat16), 3
+    ).astype(jnp.float32)
     summed_down = dp_reduce(grad_down_w.astype(jnp.bfloat16), 1)
     return (
         mixed,

time: 176 us -> 175 us (level)
  waiting for transfers between devices: 48.2 us -> 57.8 us
  starting transfers between devices: 28.6 us -> 23.8 us
  matrix products: 11.1 us -> 9.04 us
  other arithmetic: 8.89 us -> 7.08 us
    all_to_all x2, waiting for transfers between devices: 25.3 us -> 32.1 us  [gather_fsdp(): got = lax.all_to_all(copies, 'fsdp', 0, 0, tiled=False)]
    ppermute x3 -> x2, starting transfers between devices: 13.5 us -> 8.76 us  [dp_reduce(): got = lax.ppermute(send, 'dp', perm=[(0, 1), (1, 0)])]
    ppermute x3 -> x2, waiting for transfers between devices: 16.9 us -> 19.8 us  [dp_reduce(): got = lax.ppermute(send, 'dp', perm=[(0, 1), (1, 0)])]
    reshape x1, local copies, waits for them, and re-layouts: 2.12 us -> 0.13 us  [body(): w_up_g = w_up.reshape(exp_n, w_up.shape[1], shards, model_width // shards)]
    convert_element_type x3 -> x2, other arithmetic: 3.85 us -> 2.53 us  [dp_reduce(): (keep.astype(jnp.float32) + got.astype(jnp.float32)).astype(jnp.bfloat16)]
    unnamed x14 -> x16, local copies, waits for them, and re-layouts: 3.91 us -> 4.62 us
  transfers between devices with their start and end apart: 7 -> 6, of which waited for: 6 -> 5; matrix products, arithmetic and copies ran while one was open for 10% -> 9% of each run, Pallas kernels for 0% -> 0%
where the time goes in v9:
time: 175 us
  blocking collectives  62.4 us (36%)
  waiting for transfers between devices  57.8 us (33%)
  starting transfers between devices  23.8 us (14%)
  local copies, waits for them, and re-layouts  13.4 us (8%)
  matrix products  9.04 us (5%)
  other arithmetic  7.08 us (4%)
    all_to_all x1, blocking collectives, body(): lax.all_to_all(hidden_parts, 'fsdp', 0, 0, tiled=False).astype(jnp.float32)  41.5 us
    all_to_all x2, waiting for transfers between devices, gather_fsdp(): got = lax.all_to_all(copies, 'fsdp', 0, 0, tiled=False)  32.1 us
    all_to_all x1, blocking collectives, body(): lax.all_to_all(jnp.concatenate([outgoing, scaled_grad], axis=1), 'expert'...  20.9 us
    ppermute x2, waiting for transfers between devices, dp_reduce(): got = lax.ppermute(send, 'dp', perm=[(0, 1), (1, 0)])  19.8 us
    ppermute x2, starting transfers between devices, dp_reduce(): got = lax.ppermute(send, 'dp', perm=[(0, 1), (1, 0)])  8.76 us
    all_to_all x2, starting transfers between devices, gather_fsdp(): got = lax.all_to_all(copies, 'fsdp', 0, 0, tiled=False)  7.02 us
    all_to_all x1, waiting for transfers between devices, body(): lax.all_to_all(jnp.concatenate([expert_out.reshape(slot_count, -1), input...  5.95 us
    unnamed x16, local copies, waits for them, and re-layouts  4.62 us
  transfers between devices with their start and end apart: 6, of which 5 were waited for; matrix products, arithmetic and copies ran while one was open for 9% of the time, Pallas kernels for 0%

profile of v9, /device:TPU:1, one launch (start us, length us, event | category | flops | bytes accessed | tf_op | source)
XLA Modules:
  0.0 174.5 jit_solution(2022572356020686296)
XLA Ops:
  0.6 0.0 copy-start
  0.6 0.8 copy.76
  1.5 0.1 eq.35
  1.6 0.6 reduce-window.6
  2.2 0.2 slice_reduce_fusion
  2.5 0.1 bitcast_bitcast_fusion.2
  2.6 0.1 reduce_sum.42
  2.7 0.1 copy.79
  2.8 0.7 multiply_add_fusion
  3.5 0.1 iota_compare_fusion
  3.6 0.1 convert_reduce_fusion.1
  3.7 0.8 copy.94
  4.5 0.3 fusion.24
  4.7 1.0 convolution_convert_fusion.2
  5.7 0.9 convolution_convert_fusion.3
  6.7 20.9 %all_to_all.41 = bf16[32,6,256]{2,1,0:T(8,128)(2,1)S(1)} all-to-all(bf16[32,6,256]{2,1,0:T(8,128)(2,1)S(1)} %all_to_all.26), channel_id=1, replica_groups=mesh['dp'=2,'expert'=32,'fsdp'=16] {'expert'}, dimensions={0} | all-to-all | bytes 196608 | tf_op jit(solution)/shard_map/all_to_all | solution.py:65
  27.7 0.7 fusion.4
  28.4 0.1 copy.85
  28.5 41.5 %all_to_all.42 = bf16[16,32,2,3,88]{4,1,3,2,0:T(8,128)(2,1)S(1)} all-to-all(bf16[16,32,2,3,88]{4,1,3,2,0:T(8,128)(2,1)S(1)} %copy.85), channel_id=1, replica_groups=mesh['dp'=2,'expert'=32,'fsdp'=16] {'fsdp'}, dimensions={0} | all-to-all | bytes 1081344 | tf_op jit(solution)/shard_map/all_to_all | solution.py:88
  70.0 1.0 broadcast_in_dim.4
  71.1 3.5 %all-to-all-start.1 = ((bf16[16,192,128]{2,1,0:T(8,128)(2,1)}), bf16[16,192,128]{2,1,0:T(8,128)(2,1)S(1)}, u32[]{:S(2)}, u32[]{:S(2)}) async-start(bf16[16,192,128]{2,1,0:T(8,128)(2,1)} %broadcast_in_dim.4), calls=%async_computation.1 | async-start | bytes 1572864 | tf_op jit(solution)/shard_map/all_to_all | solution.py:31
  74.6 0.0 copy-start.4
  74.6 1.3 copy.116
  75.9 1.0 copy.117
  77.0 1.0 bitcast_bitcast_fusion.1
  78.0 0.2 convert_reduce_fusion
  78.1 18.5 %all-to-all-done.1 = bf16[16,192,128]{2,1,0:T(8,128)(2,1)S(1)} async-done(((bf16[16,192,128]{2,1,0:T(8,128)(2,1)}), bf16[16,192,128]{2,1,0:T(8,128)(2,1)S(1)}, u32[]{:S(2)}, u32[]{:S(2)}) %all-to-all-start.1) | async-done | bytes 786464 | tf_op jit(solution)/shard_map/all_to_all | solution.py:31
  96.6 0.5 copy.80
  97.1 0.3 reshape_reshape.3
  97.4 0.3 copy-done.3
  97.7 0.8 convolution_bitcast_fusion.4
  98.5 0.3 copy-done.5
  98.8 0.8 multiply_convert_fusion.2
  99.6 1.1 broadcast_in_dim.5
  100.7 3.5 %all-to-all-start.2 = ((bf16[16,32,2,3,88]{4,1,3,2,0:T(8,128)(2,1)}), bf16[16,32,2,3,88]{4,1,3,2,0:T(8,128)(2,1)S(1)}, u32[]{:S(2)}, u32[]{:S(2)}) async-start(bf16[16,32,2,3,88]{4,1,3,2,0:T(8,128)(2,1)} %broadcast_in_dim.5), calls=%async_computation.2 | async-start | bytes 1572864 | tf_op jit(solution)/shard_map/all_to_all | solution.py:31
  104.2 0.8 fusion.2
  105.0 0.8 fusion.1
  105.8 0.1 fusion.12
  106.0 1.1 fusion.9
  107.1 4.4 %collective-permute-start = (bf16[2,2,88,1024]{3,2,1,0:T(8,128)(2,1)}, bf16[2,2,88,1024]{3,2,1,0:T(8,128)(2,1)}, u32[]{:S(2)}, u32[]{:S(2)}) collective-permute-start(bf16[2,2,88,1024]{3,2,1,0:T(8,128)(2,1)} %fusion.9), channel_id=1, source_target_pairs={{0,512},{512,0},{1,513},{513,1},{2,514},{514,2},{3,515},{515,3},{4... | collective-permute-start | bytes 2162696 | tf_op jit(solution)/shard_map/ppermute | solution.py:24
  111.5 0.1 bitcast_bitcast_fusion
  111.7 0.4 fusion.18
  112.1 0.4 fusion.5
  112.4 1.0 copy.88
  113.4 13.6 %all-to-all-done.2 = bf16[16,32,2,3,88]{4,1,3,2,0:T(8,128)(2,1)S(1)} async-done(((bf16[16,32,2,3,88]{4,1,3,2,0:T(8,128)(2,1)}), bf16[16,32,2,3,88]{4,1,3,2,0:T(8,128)(2,1)S(1)}, u32[]{:S(2)}, u32[]{:S(2)}) %all-to-all-start.2) | async-done | bytes 540704 | tf_op jit(solution)/shard_map/all_to_all | solution.py:31
  127.1 4.2 %all-to-all-start.4 = ((bf16[16,32,2,3,128]{4,1,3,2,0:T(8,128)(2,1)}), bf16[16,32,2,3,128]{4,1,3,2,0:T(8,128)(2,1)}, u32[]{:S(2)}, u32[]{:S(2)}) async-start(bf16[16,32,2,3,128]{4,1,3,2,0:T(8,128)(2,1)} %copy.88), calls=%async_computation.4 | async-start | bytes 1572864 | tf_op jit(solution)/shard_map/all_to_all | solution.py:98
  131.3 15.3 %collective-permute-done = bf16[2,2,88,1024]{3,2,1,0:T(8,128)(2,1)} collective-permute-done((bf16[2,2,88,1024]{3,2,1,0:T(8,128)(2,1)}, bf16[2,2,88,1024]{3,2,1,0:T(8,128)(2,1)}, u32[]{:S(2)}, u32[]{:S(2)}) %collective-permute-start) | collective-permute-done | bytes 720928 | tf_op jit(solution)/shard_map/ppermute | solution.py:24
  146.6 1.6 fusion.3
  148.2 0.9 slice_bitcast_fusion.2
  149.1 0.5 copy.83
  149.6 0.9 reshape.64
  150.5 0.4 fusion
  150.9 0.1 fusion.21
  151.1 4.4 %collective-permute-start.1 = (bf16[2,704,128]{2,1,0:T(8,128)(2,1)S(1)}, bf16[2,704,128]{2,1,0:T(8,128)(2,1)S(1)}, u32[]{:S(2)}, u32[]{:S(2)}) collective-permute-start(bf16[2,704,128]{2,1,0:T(8,128)(2,1)S(1)} %fusion.21), channel_id=1, source_target_pairs={{0,512},{512,0},{1,513},{513,1},{2,514},{514,2},{3,515},{515,3},{4... | collective-permute-start | bytes 1081352 | tf_op jit(solution)/shard_map/ppermute | solution.py:24
  155.5 0.3 convolution_convert_fusion.1
  155.8 0.0 all-to-all-done.4
  155.8 1.3 reduce_sum.45
  157.1 0.7 copy.89
  157.8 3.8 %all-to-all-start.5 = ((bf16[32,6,256]{2,1,0:T(8,128)(2,1)}), bf16[32,6,256]{2,1,0:T(8,128)(2,1)S(1)}, u32[]{:S(2)}, u32[]{:S(2)}) async-start(bf16[32,6,256]{2,1,0:T(8,128)(2,1)} %copy.89), calls=%async_computation.5 | async-start | bytes 262144 | tf_op jit(solution)/shard_map/all_to_all | solution.py:104
  161.6 4.4 %collective-permute-done.1 = bf16[2,704,128]{2,1,0:T(8,128)(2,1)S(1)} collective-permute-done((bf16[2,704,128]{2,1,0:T(8,128)(2,1)S(1)}, bf16[2,704,128]{2,1,0:T(8,128)(2,1)S(1)}, u32[]{:S(2)}, u32[]{:S(2)}) %collective-permute-start.1) | collective-permute-done | bytes 360480 | tf_op jit(solution)/shard_map/ppermute | solution.py:24
  166.1 0.9 fusion.13
  167.0 5.9 %all-to-all-done.5 = bf16[32,6,256]{2,1,0:T(8,128)(2,1)S(1)} async-done(((bf16[32,6,256]{2,1,0:T(8,128)(2,1)}), bf16[32,6,256]{2,1,0:T(8,128)(2,1)S(1)}, u32[]{:S(2)}, u32[]{:S(2)}) %all-to-all-start.5) | async-done | bytes 98336 | tf_op jit(solution)/shard_map/all_to_all | solution.py:104
  173.0 0.8 convolution_convert_fusion.5
  173.8 0.8 convolution_convert_fusion.4
  (21 shorter events, 0.3 us)
Async XLA Ops:
  0.6 27.1 %copy-start = (bf16[2,1408,128]{2,1,0:T(8,128)(2,1)S(1)}, bf16[2,1408,128]{2,1,0:T(8,128)(2,1)}, u32[]{:S(2)}) copy-start(bf16[2,1408,128]{2,1,0:T(8,128)(2,1)} %param.13) | copy-start | bytes 2162692
  71.1 25.5 %all-to-all-start.1 = ((bf16[16,192,128]{2,1,0:T(8,128)(2,1)}), bf16[16,192,128]{2,1,0:T(8,128)(2,1)S(1)}, u32[]{:S(2)}, u32[]{:S(2)}) async-start(bf16[16,192,128]{2,1,0:T(8,128)(2,1)} %broadcast_in_dim.4), calls=%async_computation.1 | async-start | bytes 1572864 | tf_op jit(solution)/shard_map/all_to_all | solution.py:31
  74.6 1.3 copy-start.4
  96.6 1.1 copy-start.3
  97.7 1.1 copy-start.5
  100.7 26.4 %all-to-all-start.2 = ((bf16[16,32,2,3,88]{4,1,3,2,0:T(8,128)(2,1)}), bf16[16,32,2,3,88]{4,1,3,2,0:T(8,128)(2,1)S(1)}, u32[]{:S(2)}, u32[]{:S(2)}) async-start(bf16[16,32,2,3,88]{4,1,3,2,0:T(8,128)(2,1)} %broadcast_in_dim.5), calls=%async_computation.2 | async-start | bytes 1572864 | tf_op jit(solution)/shard_map/all_to_all | solution.py:31
  106.0 5.6 %copy-start.1 = (bf16[22,8,16,128]{3,2,1,0:T(8,128)(2,1)S(1)}, bf16[22,8,16,128]{3,2,1,0:T(8,128)(2,1)}, u32[]{:S(2)}) copy-start(bf16[22,8,16,128]{3,2,1,0:T(8,128)(2,1)} %copy.117) | copy-start | bytes 2162692
  106.0 5.7 %copy-start.2 = (bf16[2,88,16,128,1]{3,2,1,0,4:T(8,128)(2,1)S(1)}, bf16[2,88,16,128,1]{3,2,1,0,4:T(8,128)(2,1)}, u32[]{:S(2)}) copy-start(bf16[2,88,16,128,1]{3,2,1,0,4:T(8,128)(2,1)} %bitcast_bitcast_fusion.1) | copy-start | bytes 2162692
  107.1 39.4 %collective-permute-start = (bf16[2,2,88,1024]{3,2,1,0:T(8,128)(2,1)}, bf16[2,2,88,1024]{3,2,1,0:T(8,128)(2,1)}, u32[]{:S(2)}, u32[]{:S(2)}) collective-permute-start(bf16[2,2,88,1024]{3,2,1,0:T(8,128)(2,1)} %fusion.9), channel_id=1, source_target_pairs={{0,512},{512,0},{1,513},{513,1},{2,514},{514,2},{3,515},{515,3},{4... | collective-permute-start | bytes 2162696 | tf_op jit(solution)/shard_map/ppermute | solution.py:24
  127.1 28.7 %all-to-all-start.4 = ((bf16[16,32,2,3,128]{4,1,3,2,0:T(8,128)(2,1)}), bf16[16,32,2,3,128]{4,1,3,2,0:T(8,128)(2,1)}, u32[]{:S(2)}, u32[]{:S(2)}) async-start(bf16[16,32,2,3,128]{4,1,3,2,0:T(8,128)(2,1)} %copy.88), calls=%async_computation.4 | async-start | bytes 1572864 | tf_op jit(solution)/shard_map/all_to_all | solution.py:98
  151.1 15.0 %collective-permute-start.1 = (bf16[2,704,128]{2,1,0:T(8,128)(2,1)S(1)}, bf16[2,704,128]{2,1,0:T(8,128)(2,1)S(1)}, u32[]{:S(2)}, u32[]{:S(2)}) collective-permute-start(bf16[2,704,128]{2,1,0:T(8,128)(2,1)S(1)} %fusion.21), channel_id=1, source_target_pairs={{0,512},{512,0},{1,513},{513,1},{2,514},{514,2},{3,515},{515,3},{4... | collective-permute-start | bytes 1081352 | tf_op jit(solution)/shard_map/ppermute | solution.py:24
  157.8 15.2 %all-to-all-start.5 = ((bf16[32,6,256]{2,1,0:T(8,128)(2,1)}), bf16[32,6,256]{2,1,0:T(8,128)(2,1)S(1)}, u32[]{:S(2)}, u32[]{:S(2)}) async-start(bf16[32,6,256]{2,1,0:T(8,128)(2,1)} %copy.89), calls=%async_computation.5 | async-start | bytes 262144 | tf_op jit(solution)/shard_map/all_to_all | solution.py:104

commit v10 on v9

--- a/solution.py
+++ b/solution.py
@@ -123,8 +123,9 @@
     grad_down_w = rounded(
         jnp.einsum("jecf,jecd->efd", hidden_all, cotangent, preferred_element_type=jnp.float32)
     )
-    summed_gate, summed_up = dp_reduce(
-        jnp.stack([grad_gate_w, grad_up_w]).astype(jnp.bfloat16), 3
+    summed_gate, summed_up = lax.psum_scatter(
+        jnp.stack([grad_gate_w, grad_up_w]).astype(jnp.bfloat16), "dp", scatter_dimension=3,
+        tiled=True,
     ).astype(jnp.float32)
     summed_down = dp_reduce(grad_down_w.astype(jnp.bfloat16), 1)
     return (

time: 175 us -> 193 us (1.10); the launches traced: 175 us -> 190 us
  between operations: 0.97 us -> 14.3 us
  waiting for transfers between devices: 57.8 us -> 64.3 us
  starting transfers between devices: 23.8 us -> 18.8 us
    all_to_all x1, waiting for transfers between devices: 0.01 us -> 14.8 us  [body(): lax.all_to_all(input_parts.astype(jnp.bfloat16), 'fsdp', 0, 0, tiled=False)]
    ppermute x2 -> x1, waiting for transfers between devices: 19.8 us -> 8.09 us  [dp_reduce(): got = lax.ppermute(send, 'dp', perm=[(0, 1), (1, 0)])]
    ppermute x2 -> x1, starting transfers between devices: 8.76 us -> 4.4 us  [dp_reduce(): got = lax.ppermute(send, 'dp', perm=[(0, 1), (1, 0)])]
    all_to_all x2, waiting for transfers between devices: 32.1 us -> 36.1 us  [gather_fsdp(): got = lax.all_to_all(copies, 'fsdp', 0, 0, tiled=False)]
  transfers between devices with their start and end apart: 6 -> 6, of which waited for: 5 -> 5; matrix products, arithmetic and copies ran while one was open for 9% -> 7% of each run, Pallas kernels for 0% -> 0%
where the time goes in v10:
time: 193 us; the launch traced here: 190 us
  waiting for transfers between devices  64.3 us (33%)
  blocking collectives  62.4 us (32%)
  starting transfers between devices  18.8 us (10%)
  between operations  14.3 us (7%)
  local copies, waits for them, and re-layouts  13.7 us (7%)
  matrix products  10.2 us (5%)
  other arithmetic  5.69 us (3%)
    all_to_all x1, blocking collectives, body(): lax.all_to_all(hidden_parts, 'fsdp', 0, 0, tiled=False).astype(jnp.float32)  41.5 us
    all_to_all x2, waiting for transfers between devices, gather_fsdp(): got = lax.all_to_all(copies, 'fsdp', 0, 0, tiled=False)  36.1 us
    all_to_all x1, blocking collectives, body(): lax.all_to_all(jnp.concatenate([outgoing, scaled_grad], axis=1), 'expert'...  20.9 us
    all_to_all x1, waiting for transfers between devices, body(): lax.all_to_all(input_parts.astype(jnp.bfloat16), 'fsdp', 0, 0, tiled=False)  14.8 us
    ppermute x1, waiting for transfers between devices, dp_reduce(): got = lax.ppermute(send, 'dp', perm=[(0, 1), (1, 0)])  8.09 us
    all_to_all x2, starting transfers between devices, gather_fsdp(): got = lax.all_to_all(copies, 'fsdp', 0, 0, tiled=False)  7.02 us
    all_to_all x1, waiting for transfers between devices, body(): lax.all_to_all(jnp.concatenate([expert_out.reshape(slot_count, -1), input...  5.32 us
    ppermute x1, starting transfers between devices, dp_reduce(): got = lax.ppermute(send, 'dp', perm=[(0, 1), (1, 0)])  4.4 us
  transfers between devices with their start and end apart: 6, of which 5 were waited for; matrix products, arithmetic and copies ran while one was open for 7% of the time, Pallas kernels for 0%

profile of v10, /device:TPU:1, one launch (start us, length us, event | category | flops | bytes accessed | tf_op | source)
XLA Modules:
  0.0 189.5 jit_solution(17622883023194673849)
XLA Ops:
  7.2 0.0 copy-start
  7.2 0.8 copy.76
  8.0 0.1 eq.35
  8.2 0.6 reduce-window.6
  8.8 0.2 slice_reduce_fusion
  9.0 0.1 bitcast_bitcast_fusion.2
  9.1 0.1 reduce_sum.42
  9.2 0.1 copy.79
  9.3 0.7 multiply_add_fusion
  10.0 0.1 iota_compare_fusion
  10.1 0.1 convert_reduce_fusion.1
  10.2 0.8 copy.94
  11.0 0.3 fusion.16
  11.3 1.0 convolution_convert_fusion.2
  12.3 0.9 convolution_convert_fusion.3
  13.2 20.9 %all_to_all.41 = bf16[32,6,256]{2,1,0:T(8,128)(2,1)S(1)} all-to-all(bf16[32,6,256]{2,1,0:T(8,128)(2,1)S(1)} %all_to_all.26), channel_id=1, replica_groups=mesh['dp'=2,'expert'=32,'fsdp'=16] {'expert'}, dimensions={0} | all-to-all | bytes 196608 | tf_op jit(solution)/shard_map/all_to_all | solution.py:65
  34.2 0.7 fusion.3
  34.9 0.1 copy.85
  35.0 41.5 %all_to_all.42 = bf16[16,32,2,3,88]{4,1,3,2,0:T(8,128)(2,1)S(1)} all-to-all(bf16[16,32,2,3,88]{4,1,3,2,0:T(8,128)(2,1)S(1)} %copy.85), channel_id=1, replica_groups=mesh['dp'=2,'expert'=32,'fsdp'=16] {'fsdp'}, dimensions={0} | all-to-all | bytes 1081344 | tf_op jit(solution)/shard_map/all_to_all | solution.py:88
  76.6 1.0 broadcast_in_dim.4
  77.6 3.5 %all-to-all-start.1 = ((bf16[16,192,128]{2,1,0:T(8,128)(2,1)}), bf16[16,192,128]{2,1,0:T(8,128)(2,1)S(1)}, u32[]{:S(2)}, u32[]{:S(2)}) async-start(bf16[16,192,128]{2,1,0:T(8,128)(2,1)} %broadcast_in_dim.4), calls=%async_computation.1 | async-start | bytes 1572864 | tf_op jit(solution)/shard_map/all_to_all | solution.py:31
  81.1 0.0 copy-start.3
  81.1 0.1 copy.116
  81.3 0.9 copy-done.3
  82.2 0.1 copy.117
  82.4 1.0 bitcast_bitcast_fusion.1
  83.4 0.8 convert_reduce_fusion
  84.2 19.0 %all-to-all-done.1 = bf16[16,192,128]{2,1,0:T(8,128)(2,1)S(1)} async-done(((bf16[16,192,128]{2,1,0:T(8,128)(2,1)}), bf16[16,192,128]{2,1,0:T(8,128)(2,1)S(1)}, u32[]{:S(2)}, u32[]{:S(2)}) %all-to-all-start.1) | async-done | bytes 786464 | tf_op jit(solution)/shard_map/all_to_all | solution.py:31
  103.1 0.5 copy.80
  103.6 0.3 reshape_reshape.3
  103.9 0.0 copy-start.4
  103.9 2.0 %convolution_bitcast_fusion.4 = f32[32,2,3,88]{3,0,2,1:T(8,128)S(1)} fusion(bf16[2,88,2048]{2,1,0:T(8,128)(2,1)} %param.11, bf16[32,2,3,2048]{3,2,1,0:T(4,128)(2,1)S(1)} %reshape_reshape.3), kind=kOutput, calls=%fused_computation.13 | convolution fusion | flops 69206016 | bytes 1574912 | tf_op jit(solution)/shard_map/jecd,efd->jecf/dot_general | solution.py:73
  105.9 0.0 copy-done.5
  105.9 0.8 multiply_convert_fusion.2
  106.7 1.1 broadcast_in_dim.5
  107.8 3.5 %all-to-all-start.2 = ((bf16[16,32,2,3,88]{4,1,3,2,0:T(8,128)(2,1)}), bf16[16,32,2,3,88]{4,1,3,2,0:T(8,128)(2,1)S(1)}, u32[]{:S(2)}, u32[]{:S(2)}) async-start(bf16[16,32,2,3,88]{4,1,3,2,0:T(8,128)(2,1)} %broadcast_in_dim.5), calls=%async_computation.2 | async-start | bytes 1572864 | tf_op jit(solution)/shard_map/all_to_all | solution.py:31
  111.3 0.0 reduce-scatter.2.cloned.1.call-start
  111.4 0.8 fusion.2
  112.2 0.8 fusion.1
  113.0 1.2 pad_maximum_fusion
  114.2 0.0 reduce-scatter.2.cloned.1.call-update
  114.3 0.1 bitcast_bitcast_fusion
  114.4 1.0 copy-done.1
  115.4 0.4 fusion.10
  115.7 0.4 fusion.4
  116.1 1.0 copy.88
  117.1 17.1 %all-to-all-done.2 = bf16[16,32,2,3,88]{4,1,3,2,0:T(8,128)(2,1)S(1)} async-done(((bf16[16,32,2,3,88]{4,1,3,2,0:T(8,128)(2,1)}), bf16[16,32,2,3,88]{4,1,3,2,0:T(8,128)(2,1)S(1)}, u32[]{:S(2)}, u32[]{:S(2)}) %all-to-all-start.2) | async-done | bytes 540704 | tf_op jit(solution)/shard_map/all_to_all | solution.py:31
  134.2 3.5 %all-to-all-start.4 = ((bf16[16,32,2,3,128]{4,1,3,2,0:T(8,128)(2,1)}), bf16[16,32,2,3,128]{4,1,3,2,0:T(8,128)(2,1)S(1)}, u32[]{:S(2)}, u32[]{:S(2)}) async-start(bf16[16,32,2,3,128]{4,1,3,2,0:T(8,128)(2,1)} %copy.88), calls=%async_computation.4 | async-start | bytes 1572864 | tf_op jit(solution)/shard_map/all_to_all | solution.py:98
  137.7 0.5 copy.83
  138.2 0.9 reshape.62
  139.1 0.4 fusion
  139.6 0.9 fusion.13
  140.5 4.4 %collective-permute-start = (bf16[2,704,128]{2,1,0:T(8,128)(2,1)}, bf16[2,704,128]{2,1,0:T(8,128)(2,1)S(1)}, u32[]{:S(2)}, u32[]{:S(2)}) collective-permute-start(bf16[2,704,128]{2,1,0:T(8,128)(2,1)} %fusion.13), channel_id=1, source_target_pairs={{0,512},{512,0},{1,513},{513,1},{2,514},{514,2},{3,515},{515,3},{4... | collective-permute-start | bytes 1081352 | tf_op jit(solution)/shard_map/ppermute | solution.py:24
  144.9 0.3 convolution_convert_fusion.1
  145.2 14.8 %all-to-all-done.4 = bf16[16,32,2,3,128]{4,1,3,2,0:T(8,128)(2,1)S(1)} async-done(((bf16[16,32,2,3,128]{4,1,3,2,0:T(8,128)(2,1)}), bf16[16,32,2,3,128]{4,1,3,2,0:T(8,128)(2,1)S(1)}, u32[]{:S(2)}, u32[]{:S(2)}) %all-to-all-start.4) | async-done | bytes 786464 | tf_op jit(solution)/shard_map/all_to_all | solution.py:98
  160.0 0.1 reduce_sum.45
  160.2 0.7 copy.89
  160.9 3.9 %all-to-all-start.5 = ((bf16[32,6,256]{2,1,0:T(8,128)(2,1)}), bf16[32,6,256]{2,1,0:T(8,128)(2,1)S(1)}, u32[]{:S(2)}, u32[]{:S(2)}) async-start(bf16[32,6,256]{2,1,0:T(8,128)(2,1)} %copy.89), calls=%async_computation.5 | async-start | bytes 262144 | tf_op jit(solution)/shard_map/all_to_all | solution.py:104
  164.8 8.1 %collective-permute-done = bf16[2,704,128]{2,1,0:T(8,128)(2,1)S(1)} collective-permute-done((bf16[2,704,128]{2,1,0:T(8,128)(2,1)}, bf16[2,704,128]{2,1,0:T(8,128)(2,1)S(1)}, u32[]{:S(2)}, u32[]{:S(2)}) %collective-permute-start) | collective-permute-done | bytes 360480 | tf_op jit(solution)/shard_map/ppermute | solution.py:24
  172.8 0.9 fusion.5
  173.8 5.3 %all-to-all-done.5 = bf16[32,6,256]{2,1,0:T(8,128)(2,1)S(1)} async-done(((bf16[32,6,256]{2,1,0:T(8,128)(2,1)}), bf16[32,6,256]{2,1,0:T(8,128)(2,1)S(1)}, u32[]{:S(2)}, u32[]{:S(2)}) %all-to-all-start.5) | async-done | bytes 98336 | tf_op jit(solution)/shard_map/all_to_all | solution.py:104
  179.1 0.8 convolution_convert_fusion.5
  179.9 0.8 convolution_convert_fusion.4
  180.7 2.0 %slice_bitcast_fusion.2 = (bf16[2,88,1024]{2,1,0:T(8,128)(2,1)}, bf16[2,88,1024]{2,1,0:T(8,128)(2,1)}) fusion(bf16[2,2,88,1024]{3,2,1,0:T(8,128)(2,1)} %reduce-scatter.2.cloned.1.call-done), kind=kLoop, calls=%fused_computation.39 | loop fusion | bytes 1441792 | tf_op jit(solution)/shard_map/convert_element_type | solution.py:135
  (20 shorter events, 0.3 us)
Async XLA Ops:
  7.2 27.1 %copy-start = (bf16[2,1408,128]{2,1,0:T(8,128)(2,1)S(1)}, bf16[2,1408,128]{2,1,0:T(8,128)(2,1)}, u32[]{:S(2)}) copy-start(bf16[2,1408,128]{2,1,0:T(8,128)(2,1)} %param.13) | copy-start | bytes 2162692
  76.6 4.6 %copy-start.2 = (bf16[2,88,2048]{2,1,0:T(8,128)(2,1)S(1)}, bf16[2,88,2048]{2,1,0:T(8,128)(2,1)}, u32[]{:S(2)}) copy-start(bf16[2,88,2048]{2,1,0:T(8,128)(2,1)} %param.11) | copy-start | bytes 2162692
  77.6 25.5 %all-to-all-start.1 = ((bf16[16,192,128]{2,1,0:T(8,128)(2,1)}), bf16[16,192,128]{2,1,0:T(8,128)(2,1)S(1)}, u32[]{:S(2)}, u32[]{:S(2)}) async-start(bf16[16,192,128]{2,1,0:T(8,128)(2,1)} %broadcast_in_dim.4), calls=%async_computation.1 | async-start | bytes 1572864 | tf_op jit(solution)/shard_map/all_to_all | solution.py:31
  81.1 1.1 copy-start.3
  103.9 2.0 %copy-start.4 = (bf16[2,88,2048]{2,1,0:T(8,128)(2,1)S(1)}, bf16[2,88,2048]{2,1,0:T(8,128)(2,1)}, u32[]{:S(2)}) copy-start(bf16[2,88,2048]{2,1,0:T(8,128)(2,1)} %param.12) | copy-start | bytes 2162692
  103.9 2.0 %copy-start.5 = (f32[32,2,3,88]{3,0,2,1:T(8,128)S(1)}, f32[32,2,3,88]{3,0,2,1:T(8,128)}, u32[]{:S(2)}) copy-start(f32[32,2,3,88]{3,0,2,1:T(8,128)} %convert_reduce_fusion) | copy-start | bytes 202756
  107.8 26.4 %all-to-all-start.2 = ((bf16[16,32,2,3,88]{4,1,3,2,0:T(8,128)(2,1)}), bf16[16,32,2,3,88]{4,1,3,2,0:T(8,128)(2,1)S(1)}, u32[]{:S(2)}, u32[]{:S(2)}) async-start(bf16[16,32,2,3,88]{4,1,3,2,0:T(8,128)(2,1)} %broadcast_in_dim.5), calls=%async_computation.2 | async-start | bytes 1572864 | tf_op jit(solution)/shard_map/all_to_all | solution.py:31
  111.3 69.4 %reduce-scatter.2.cloned.1.call-start = ((), (), s32[]{:S(2)}) async-start(), calls=%async_computation.7 | async-start | bytes 2162688 | tf_op jit(solution)/shard_map/reduce_scatter | solution.py:126
  114.2 1.1 copy-start.1
  134.2 25.8 %all-to-all-start.4 = ((bf16[16,32,2,3,128]{4,1,3,2,0:T(8,128)(2,1)}), bf16[16,32,2,3,128]{4,1,3,2,0:T(8,128)(2,1)S(1)}, u32[]{:S(2)}, u32[]{:S(2)}) async-start(bf16[16,32,2,3,128]{4,1,3,2,0:T(8,128)(2,1)} %copy.88), calls=%async_computation.4 | async-start | bytes 1572864 | tf_op jit(solution)/shard_map/all_to_all | solution.py:98
  140.5 32.4 %collective-permute-start = (bf16[2,704,128]{2,1,0:T(8,128)(2,1)}, bf16[2,704,128]{2,1,0:T(8,128)(2,1)S(1)}, u32[]{:S(2)}, u32[]{:S(2)}) collective-permute-start(bf16[2,704,128]{2,1,0:T(8,128)(2,1)} %fusion.13), channel_id=1, source_target_pairs={{0,512},{512,0},{1,513},{513,1},{2,514},{514,2},{3,515},{515,3},{4... | collective-permute-start | bytes 1081352 | tf_op jit(solution)/shard_map/ppermute | solution.py:24
  160.9 18.2 %all-to-all-start.5 = ((bf16[32,6,256]{2,1,0:T(8,128)(2,1)}), bf16[32,6,256]{2,1,0:T(8,128)(2,1)S(1)}, u32[]{:S(2)}, u32[]{:S(2)}) async-start(bf16[32,6,256]{2,1,0:T(8,128)(2,1)} %copy.89), calls=%async_computation.5 | async-start | bytes 262144 | tf_op jit(solution)/shard_map/all_to_all | solution.py:104
Sparse Core Ops, SparseCore 0:
  115.6 47.8 reduce-scatter.1

commit v11 on v9

--- a/solution.py
+++ b/solution.py
@@ -66,7 +66,7 @@
         jnp.concatenate([outgoing, scaled_grad], axis=1),
         "expert", split_axis=0, concat_axis=0, tiled=True,
     )
-    rows_in = gather_fsdp(both_in[:, :local_feat], 1)
+    rows_in = lax.all_gather(both_in[:, :local_feat], "fsdp", axis=1, tiled=True)
     grads_in = both_in[:, local_feat:]
     received = rows_in.reshape(owners, exp_local, capacity, model_width)
     cotangent = grads_in.reshape(owners, exp_local, capacity, -1)

time: 175 us -> 165 us (0.943)
  waiting for transfers between devices: 57.8 us -> 39.3 us
  starting transfers between devices: 23.8 us -> 41.4 us
  blocking collectives: 62.4 us -> 51.7 us
  matrix products: 9.04 us -> 11.8 us
    all_to_all x1 -> x0, blocking collectives: 41.5 us -> none  [body(): lax.all_to_all(hidden_parts, 'fsdp', 0, 0, tiled=False).astype(jnp.float32)]
    all_gather x0 -> x1, blocking collectives: none -> 30.8 us  [body(): lax.all_gather(both_in[:, :local_feat], 'fsdp', axis=1, tiled=True)]
    all_to_all x0 -> x1, starting transfers between devices: none -> 18.8 us  [body(): lax.all_to_all(hidden_parts, 'fsdp', 0, 0, tiled=False).astype(jnp.float32)]
    all_to_all x2 -> x1, waiting for transfers between devices: 32.1 us -> 13.8 us  [gather_fsdp(): got = lax.all_to_all(copies, 'fsdp', 0, 0, tiled=False)]
    dot_general x1, matrix products: 0.8 us -> 2.63 us  [body(): jnp.einsum('jecd,efd->jecf', received, w_gate, preferred_element_type=jnp...]
    all_to_all x2 -> x1, starting transfers between devices: 7.02 us -> 5.96 us  [gather_fsdp(): got = lax.all_to_all(copies, 'fsdp', 0, 0, tiled=False)]
  transfers between devices with their start and end apart: 6 -> 6, of which waited for: 5 -> 4; matrix products, arithmetic and copies ran while one was open for 9% -> 11% of each run, Pallas kernels for 0% -> 0%
where the time goes in v11:
time: 165 us; the launch traced here: 164 us
  blocking collectives  51.7 us (31%)
  starting transfers between devices  41.4 us (25%)
  waiting for transfers between devices  39.3 us (24%)
  local copies, waits for them, and re-layouts  12.1 us (7%)
  matrix products  11.8 us (7%)
  other arithmetic  7.08 us (4%)
    all_gather x1, blocking collectives, body(): lax.all_gather(both_in[:, :local_feat], 'fsdp', axis=1, tiled=True)  30.8 us
    all_to_all x1, blocking collectives, body(): lax.all_to_all(jnp.concatenate([outgoing, scaled_grad], axis=1), 'expert'...  20.9 us
    ppermute x2, waiting for transfers between devices, dp_reduce(): got = lax.ppermute(send, 'dp', perm=[(0, 1), (1, 0)])  19.7 us
    all_to_all x1, starting transfers between devices, body(): lax.all_to_all(hidden_parts, 'fsdp', 0, 0, tiled=False).astype(jnp.float32)  18.8 us
    all_to_all x1, waiting for transfers between devices, gather_fsdp(): got = lax.all_to_all(copies, 'fsdp', 0, 0, tiled=False)  13.8 us
    ppermute x2, starting transfers between devices, dp_reduce(): got = lax.ppermute(send, 'dp', perm=[(0, 1), (1, 0)])  8.66 us
    all_to_all x1, starting transfers between devices, gather_fsdp(): got = lax.all_to_all(copies, 'fsdp', 0, 0, tiled=False)  5.96 us
    all_to_all x1, waiting for transfers between devices, body(): lax.all_to_all(jnp.concatenate([expert_out.reshape(slot_count, -1), input...  5.8 us
  transfers between devices with their start and end apart: 6, of which 4 were waited for; matrix products, arithmetic and copies ran while one was open for 11% of the time, Pallas kernels for 0%

profile of v11, /device:TPU:1, one launch (start us, length us, event | category | flops | bytes accessed | tf_op | source)
XLA Modules:
  0.0 164.3 jit_solution(8002289692411514320)
XLA Ops:
  0.6 0.0 copy-start
  0.6 0.8 copy.74
  1.5 0.1 eq.35
  1.6 0.6 reduce-window.6
  2.2 0.2 slice_reduce_fusion
  2.5 0.1 bitcast_bitcast_fusion.2
  2.6 0.1 reduce_sum.42
  2.7 0.1 copy.77
  2.8 0.7 multiply_add_fusion
  3.5 0.1 iota_compare_fusion
  3.6 0.1 convert_reduce_fusion.1
  3.7 0.8 copy.91
  4.5 0.3 fusion.24
  4.7 1.0 convolution_convert_fusion.2
  5.7 0.9 convolution_convert_fusion.3
  6.7 20.9 %all_to_all.36 = bf16[32,6,256]{2,1,0:T(8,128)(2,1)S(1)} all-to-all(bf16[32,6,256]{2,1,0:T(8,128)(2,1)S(1)} %all_to_all.23), channel_id=1, replica_groups=mesh['dp'=2,'expert'=32,'fsdp'=16] {'expert'}, dimensions={0} | all-to-all | bytes 196608 | tf_op jit(solution)/shard_map/all_to_all | solution.py:65
  27.7 0.7 fusion.4
  28.4 0.0 copy-start.3
  28.4 1.0 copy.82
  29.4 18.8 %all-to-all-start.2 = ((bf16[16,32,2,3,88]{4,1,3,2,0:T(8,128)(2,1)}), bf16[16,32,2,3,88]{4,1,3,2,0:T(8,128)(2,1)S(1)}, u32[]{:S(2)}, u32[]{:S(2)}) async-start(bf16[16,32,2,3,88]{4,1,3,2,0:T(8,128)(2,1)} %copy.82), calls=%async_computation.2 | async-start | bytes 1572864 | tf_op jit(solution)/shard_map/all_to_all | solution.py:88
  48.2 0.0 copy-done.3
  48.2 0.1 copy.113
  48.4 0.9 copy-done.4
  49.3 1.0 copy.114
  50.3 1.0 bitcast_bitcast_fusion.1
  51.3 30.8 %all_gather.3 = bf16[192,2048]{1,0:T(8,128)(2,1)S(1)} all-gather(bf16[192,128]{1,0:T(8,128)(2,1)S(1)} %get-tuple-element.15), channel_id=1, replica_groups=mesh['dp'=2,'expert'=32,'fsdp'=16] {'fsdp'}, dimensions={1}, use_global_device_ids=true | all-gather | bytes 835584 | tf_op jit(solution)/shard_map/all_gather | solution.py:69
  82.1 0.5 reshape.66
  82.6 0.0 copy-start.5
  82.6 2.6 %convolution_bitcast_fusion.4 = f32[32,2,3,88]{3,0,2,1:T(8,128)} fusion(bf16[2,88,2048]{2,1,0:T(8,128)(2,1)} %param.11, bf16[32,2,3,2048]{3,2,1,0:T(4,128)(2,1)S(1)} %reshape.66), kind=kOutput, calls=%fused_computation.20 | convolution fusion | flops 69206016 | bytes 1574912 | tf_op jit(solution)/shard_map/jecd,efd->jecf/dot_general | solution.py:73
  85.3 0.0 all-to-all-done.2
  85.3 0.2 convert_reduce_fusion
  85.4 1.7 %multiply_convert_fusion.2 = (bf16[32,2,3,88]{3,0,2,1:T(8,128)(2,1)S(1)}, bf16[32,2,3,88]{3,0,2,1:T(8,128)(2,1)S(1)}, bf16[32,2,3,88]{3,0,2,1:T(8,128)(2,1)S(1)}) fusion(f32[32,2,3,88]{3,0,2,1:T(8,128)} %convolution_bitcast_fusion.4, f32[32,2,3,88]{3,0,2,1:T(8,128)S(1)} %convert_reduce_fusion, bf16[2,88,2048]{2,1,0:T(8,128)(2,1)S(1)} %copy-done.5, ...), kind=kOutput, calls=%fused_computation.68 | convolution fusion | flops 69459456 | bytes 1743872 | tf_op jit(solution)/shard_map/jecd,efd->jecf/dot_general | solution.py:74
  87.1 1.1 broadcast_in_dim.2
  88.2 6.0 %all-to-all-start.1 = ((bf16[16,32,2,3,88]{4,1,3,2,0:T(8,128)(2,1)}), bf16[16,32,2,3,88]{4,1,3,2,0:T(8,128)(2,1)S(1)}, u32[]{:S(2)}, u32[]{:S(2)}) async-start(bf16[16,32,2,3,88]{4,1,3,2,0:T(8,128)(2,1)} %broadcast_in_dim.2), calls=%async_computation.1 | async-start | bytes 1572864 | tf_op jit(solution)/shard_map/all_to_all | solution.py:31
  94.2 0.8 fusion.2
  95.0 0.8 fusion.1
  95.8 0.1 fusion.12
  95.9 0.0 copy-start.1
  95.9 1.1 fusion.9
  97.1 4.4 %collective-permute-start = (bf16[2,2,88,1024]{3,2,1,0:T(8,128)(2,1)}, bf16[2,2,88,1024]{3,2,1,0:T(8,128)(2,1)}, u32[]{:S(2)}, u32[]{:S(2)}) collective-permute-start(bf16[2,2,88,1024]{3,2,1,0:T(8,128)(2,1)} %fusion.9), channel_id=1, source_target_pairs={{0,512},{512,0},{1,513},{513,1},{2,514},{514,2},{3,515},{515,3},{4... | collective-permute-start | bytes 2162696 | tf_op jit(solution)/shard_map/ppermute | solution.py:24
  101.5 0.1 bitcast_bitcast_fusion
  101.7 0.4 fusion.18
  102.0 0.4 fusion.5
  102.4 1.0 copy.85
  103.4 13.8 %all-to-all-done.1 = bf16[16,32,2,3,88]{4,1,3,2,0:T(8,128)(2,1)S(1)} async-done(((bf16[16,32,2,3,88]{4,1,3,2,0:T(8,128)(2,1)}), bf16[16,32,2,3,88]{4,1,3,2,0:T(8,128)(2,1)S(1)}, u32[]{:S(2)}, u32[]{:S(2)}) %all-to-all-start.1) | async-done | bytes 540704 | tf_op jit(solution)/shard_map/all_to_all | solution.py:31
  117.2 4.2 %all-to-all-start.3 = ((bf16[16,32,2,3,128]{4,1,3,2,0:T(8,128)(2,1)}), bf16[16,32,2,3,128]{4,1,3,2,0:T(8,128)(2,1)}, u32[]{:S(2)}, u32[]{:S(2)}) async-start(bf16[16,32,2,3,128]{4,1,3,2,0:T(8,128)(2,1)} %copy.85), calls=%async_computation.3 | async-start | bytes 1572864 | tf_op jit(solution)/shard_map/all_to_all | solution.py:98
  121.4 15.1 %collective-permute-done = bf16[2,2,88,1024]{3,2,1,0:T(8,128)(2,1)} collective-permute-done((bf16[2,2,88,1024]{3,2,1,0:T(8,128)(2,1)}, bf16[2,2,88,1024]{3,2,1,0:T(8,128)(2,1)}, u32[]{:S(2)}, u32[]{:S(2)}) %collective-permute-start) | collective-permute-done | bytes 720928 | tf_op jit(solution)/shard_map/ppermute | solution.py:24
  136.5 1.6 fusion.3
  138.1 0.9 slice_bitcast_fusion.2
  139.0 0.5 copy.80
  139.5 0.9 reshape.67
  140.4 0.4 fusion
  140.9 0.1 fusion.21
  141.1 4.2 %collective-permute-start.1 = (bf16[2,704,128]{2,1,0:T(8,128)(2,1)S(1)}, bf16[2,704,128]{2,1,0:T(8,128)(2,1)S(1)}, u32[]{:S(2)}, u32[]{:S(2)}) collective-permute-start(bf16[2,704,128]{2,1,0:T(8,128)(2,1)S(1)} %fusion.21), channel_id=1, source_target_pairs={{0,512},{512,0},{1,513},{513,1},{2,514},{514,2},{3,515},{515,3},{4... | collective-permute-start | bytes 1081352 | tf_op jit(solution)/shard_map/ppermute | solution.py:24
  145.3 0.3 convolution_convert_fusion.1
  145.6 0.0 all-to-all-done.3
  145.6 1.3 reduce_sum.45
  146.9 0.7 copy.86
  147.6 3.8 %all-to-all-start.4 = ((bf16[32,6,256]{2,1,0:T(8,128)(2,1)}), bf16[32,6,256]{2,1,0:T(8,128)(2,1)S(1)}, u32[]{:S(2)}, u32[]{:S(2)}) async-start(bf16[32,6,256]{2,1,0:T(8,128)(2,1)} %copy.86), calls=%async_computation.4 | async-start | bytes 262144 | tf_op jit(solution)/shard_map/all_to_all | solution.py:104
  151.4 4.6 %collective-permute-done.1 = bf16[2,704,128]{2,1,0:T(8,128)(2,1)S(1)} collective-permute-done((bf16[2,704,128]{2,1,0:T(8,128)(2,1)S(1)}, bf16[2,704,128]{2,1,0:T(8,128)(2,1)S(1)}, u32[]{:S(2)}, u32[]{:S(2)}) %collective-permute-start.1) | collective-permute-done | bytes 360480 | tf_op jit(solution)/shard_map/ppermute | solution.py:24
  156.0 0.9 fusion.13
  157.0 5.8 %all-to-all-done.4 = bf16[32,6,256]{2,1,0:T(8,128)(2,1)S(1)} async-done(((bf16[32,6,256]{2,1,0:T(8,128)(2,1)}), bf16[32,6,256]{2,1,0:T(8,128)(2,1)S(1)}, u32[]{:S(2)}, u32[]{:S(2)}) %all-to-all-start.4) | async-done | bytes 98336 | tf_op jit(solution)/shard_map/all_to_all | solution.py:104
  162.8 0.8 convolution_convert_fusion.5
  163.6 0.8 convolution_convert_fusion.4
  (19 shorter events, 0.3 us)
Async XLA Ops:
  0.6 27.1 %copy-start = (bf16[2,1408,128]{2,1,0:T(8,128)(2,1)S(1)}, bf16[2,1408,128]{2,1,0:T(8,128)(2,1)}, u32[]{:S(2)}) copy-start(bf16[2,1408,128]{2,1,0:T(8,128)(2,1)} %param.13) | copy-start | bytes 2162692
  28.4 19.8 %copy-start.3 = (bf16[2,88,2048]{2,1,0:T(8,128)(2,1)S(1)}, bf16[2,88,2048]{2,1,0:T(8,128)(2,1)}, u32[]{:S(2)}) copy-start(bf16[2,88,2048]{2,1,0:T(8,128)(2,1)} %param.11) | copy-start | bytes 2162692
  29.4 55.9 %all-to-all-start.2 = ((bf16[16,32,2,3,88]{4,1,3,2,0:T(8,128)(2,1)}), bf16[16,32,2,3,88]{4,1,3,2,0:T(8,128)(2,1)S(1)}, u32[]{:S(2)}, u32[]{:S(2)}) async-start(bf16[16,32,2,3,88]{4,1,3,2,0:T(8,128)(2,1)} %copy.82), calls=%async_computation.2 | async-start | bytes 1572864 | tf_op jit(solution)/shard_map/all_to_all | solution.py:88
  48.2 1.1 copy-start.4
  82.6 2.8 %copy-start.5 = (bf16[2,88,2048]{2,1,0:T(8,128)(2,1)S(1)}, bf16[2,88,2048]{2,1,0:T(8,128)(2,1)}, u32[]{:S(2)}) copy-start(bf16[2,88,2048]{2,1,0:T(8,128)(2,1)} %param.12) | copy-start | bytes 2162692
  88.2 29.0 %all-to-all-start.1 = ((bf16[16,32,2,3,88]{4,1,3,2,0:T(8,128)(2,1)}), bf16[16,32,2,3,88]{4,1,3,2,0:T(8,128)(2,1)S(1)}, u32[]{:S(2)}, u32[]{:S(2)}) async-start(bf16[16,32,2,3,88]{4,1,3,2,0:T(8,128)(2,1)} %broadcast_in_dim.2), calls=%async_computation.1 | async-start | bytes 1572864 | tf_op jit(solution)/shard_map/all_to_all | solution.py:31
  95.9 5.6 %copy-start.1 = (bf16[22,8,16,128]{3,2,1,0:T(8,128)(2,1)S(1)}, bf16[22,8,16,128]{3,2,1,0:T(8,128)(2,1)}, u32[]{:S(2)}) copy-start(bf16[22,8,16,128]{3,2,1,0:T(8,128)(2,1)} %copy.114) | copy-start | bytes 2162692
  95.9 5.7 %copy-start.2 = (bf16[2,88,16,128,1]{3,2,1,0,4:T(8,128)(2,1)S(1)}, bf16[2,88,16,128,1]{3,2,1,0,4:T(8,128)(2,1)}, u32[]{:S(2)}) copy-start(bf16[2,88,16,128,1]{3,2,1,0,4:T(8,128)(2,1)} %bitcast_bitcast_fusion.1) | copy-start | bytes 2162692
  97.1 39.4 %collective-permute-start = (bf16[2,2,88,1024]{3,2,1,0:T(8,128)(2,1)}, bf16[2,2,88,1024]{3,2,1,0:T(8,128)(2,1)}, u32[]{:S(2)}, u32[]{:S(2)}) collective-permute-start(bf16[2,2,88,1024]{3,2,1,0:T(8,128)(2,1)} %fusion.9), channel_id=1, source_target_pairs={{0,512},{512,0},{1,513},{513,1},{2,514},{514,2},{3,515},{515,3},{4... | collective-permute-start | bytes 2162696 | tf_op jit(solution)/shard_map/ppermute | solution.py:24
  117.2 28.4 %all-to-all-start.3 = ((bf16[16,32,2,3,128]{4,1,3,2,0:T(8,128)(2,1)}), bf16[16,32,2,3,128]{4,1,3,2,0:T(8,128)(2,1)}, u32[]{:S(2)}, u32[]{:S(2)}) async-start(bf16[16,32,2,3,128]{4,1,3,2,0:T(8,128)(2,1)} %copy.85), calls=%async_computation.3 | async-start | bytes 1572864 | tf_op jit(solution)/shard_map/all_to_all | solution.py:98
  141.1 15.0 %collective-permute-start.1 = (bf16[2,704,128]{2,1,0:T(8,128)(2,1)S(1)}, bf16[2,704,128]{2,1,0:T(8,128)(2,1)S(1)}, u32[]{:S(2)}, u32[]{:S(2)}) collective-permute-start(bf16[2,704,128]{2,1,0:T(8,128)(2,1)S(1)} %fusion.21), channel_id=1, source_target_pairs={{0,512},{512,0},{1,513},{513,1},{2,514},{514,2},{3,515},{515,3},{4... | collective-permute-start | bytes 1081352 | tf_op jit(solution)/shard_map/ppermute | solution.py:24
  147.6 15.2 %all-to-all-start.4 = ((bf16[32,6,256]{2,1,0:T(8,128)(2,1)}), bf16[32,6,256]{2,1,0:T(8,128)(2,1)S(1)}, u32[]{:S(2)}, u32[]{:S(2)}) async-start(bf16[32,6,256]{2,1,0:T(8,128)(2,1)} %copy.86), calls=%async_computation.4 | async-start | bytes 262144 | tf_op jit(solution)/shard_map/all_to_all | solution.py:104

commit v12 on v11

--- a/solution.py
+++ b/solution.py
@@ -31,6 +31,24 @@
     got = lax.all_to_all(copies, "fsdp", 0, 0, tiled=False)
     got = jnp.moveaxis(got, 0, axis)
     return got.reshape(part.shape[:axis] + (-1,) + part.shape[axis + 1:])
+
+
+def dp_reduce_many(parts, axes):
+    me = lax.axis_index("dp")
+    keeps, sends = [], []
+    for part, axis in zip(parts, axes):
+        halves = jnp.stack(jnp.split(part, 2, axis=axis))
+        keeps.append(lax.dynamic_index_in_dim(halves, me, 0, keepdims=False))
+        sends.append(lax.dynamic_index_in_dim(halves, 1 - me, 0, keepdims=False))
+    got = lax.ppermute(
+        jnp.concatenate([x.reshape(-1) for x in sends]), "dp", perm=[(0, 1), (1, 0)]
+    )
+    outs, at = [], 0
+    for keep in keeps:
+        piece = got[at:at + keep.size].reshape(keep.shape)
+        at += keep.size
+        outs.append((keep.astype(jnp.float32) + piece.astype(jnp.float32)).astype(jnp.bfloat16))
+    return outs[0][0], outs[0][1], outs[1]
 
 
 def body(tokens, grad_out, expert_ids, gate_weights, w_gate, w_up, w_down):
@@ -123,10 +141,12 @@
     grad_down_w = rounded(
         jnp.einsum("jecf,jecd->efd", hidden_all, cotangent, preferred_element_type=jnp.float32)
     )
-    summed_gate, summed_up = dp_reduce(
-        jnp.stack([grad_gate_w, grad_up_w]).astype(jnp.bfloat16), 3
-    ).astype(jnp.float32)
-    summed_down = dp_reduce(grad_down_w.astype(jnp.bfloat16), 1)
+    summed_gate, summed_up, summed_down = dp_reduce_many(
+        [jnp.stack([grad_gate_w, grad_up_w]).astype(jnp.bfloat16), grad_down_w.astype(jnp.bfloat16)],
+        [3, 1],
+    )
+    summed_gate = summed_gate.astype(jnp.float32)
+    summed_up = summed_up.astype(jnp.float32)
     return (
         mixed,
         grad_tokens,

time: 165 us -> 195 us (1.18)
  waiting for transfers between devices: 39.3 us -> 71.2 us
  blocking collectives: 51.7 us -> 31.8 us
  local copies, waits for them, and re-layouts: 12.1 us -> 20.4 us
  starting transfers between devices: 41.4 us -> 48.6 us
    all_to_all x1, waiting for transfers between devices: 5.8 us -> 32.6 us  [body(): lax.all_to_all(jnp.concatenate([expert_out.reshape(slot_count, -1), input...]
    all_to_all x1 -> x0, blocking collectives: 20.9 us -> none  [body(): lax.all_to_all(jnp.concatenate([outgoing, scaled_grad], axis=1), 'expert'...]
    ppermute x2 -> x1, waiting for transfers between devices: 19.7 us -> 0.01 us  [dp_reduce_many(): lax.ppermute(jnp.concatenate([x.reshape(-1) for x in sends]), 'dp', perm=...]
    all_to_all x1, waiting for transfers between devices: 0.01 us -> 11.4 us  [body(): lax.all_to_all(input_parts.astype(jnp.bfloat16), 'fsdp', 0, 0, tiled=False)]
    all_to_all x0 -> x1, starting transfers between devices: none -> 11.3 us  [body(): lax.all_to_all(jnp.concatenate([outgoing, scaled_grad], axis=1), 'expert'...]
    all_to_all x0 -> x1, waiting for transfers between devices: none -> 9.68 us  [body(): lax.all_to_all(jnp.concatenate([outgoing, scaled_grad], axis=1), 'expert'...]
    ppermute x2 -> x1, starting transfers between devices: 8.66 us -> 4.4 us  [dp_reduce_many(): lax.ppermute(jnp.concatenate([x.reshape(-1) for x in sends]), 'dp', perm=...]
    all_to_all x1, waiting for transfers between devices: 13.8 us -> 17.6 us  [gather_fsdp(): got = lax.all_to_all(copies, 'fsdp', 0, 0, tiled=False)]
  transfers between devices with their start and end apart: 6 -> 6, of which waited for: 4 -> 4; matrix products, arithmetic and copies ran while one was open for 11% -> 9% of each run, Pallas kernels for 0% -> 0%
where the time goes in v12:
time: 195 us; the launch traced here: 194 us
  waiting for transfers between devices  71.2 us (37%)
  starting transfers between devices  48.6 us (25%)
  blocking collectives  31.8 us (16%)
  local copies, waits for them, and re-layouts  20.4 us (10%)
  matrix products  12.6 us (6%)
  other arithmetic  8.43 us (4%)
    all_to_all x1, waiting for transfers between devices, body(): lax.all_to_all(jnp.concatenate([expert_out.reshape(slot_count, -1), input...  32.6 us
    all_gather x1, blocking collectives, body(): lax.all_gather(both_in[:, :local_feat], 'fsdp', axis=1, tiled=True)  31.8 us
    all_to_all x1, starting transfers between devices, body(): lax.all_to_all(hidden_parts, 'fsdp', 0, 0, tiled=False).astype(jnp.float32)  18.9 us
    all_to_all x1, waiting for transfers between devices, gather_fsdp(): got = lax.all_to_all(copies, 'fsdp', 0, 0, tiled=False)  17.6 us
    all_to_all x1, waiting for transfers between devices, body(): lax.all_to_all(input_parts.astype(jnp.bfloat16), 'fsdp', 0, 0, tiled=False)  11.4 us
    all_to_all x1, starting transfers between devices, body(): lax.all_to_all(jnp.concatenate([outgoing, scaled_grad], axis=1), 'expert'...  11.3 us
    all_to_all x1, waiting for transfers between devices, body(): lax.all_to_all(jnp.concatenate([outgoing, scaled_grad], axis=1), 'expert'...  9.68 us
    all_to_all x1, starting transfers between devices, gather_fsdp(): got = lax.all_to_all(copies, 'fsdp', 0, 0, tiled=False)  5.96 us
  transfers between devices with their start and end apart: 6, of which 4 were waited for; matrix products, arithmetic and copies ran while one was open for 9% of the time, Pallas kernels for 0%

profile of v12, /device:TPU:1, one launch (start us, length us, event | category | flops | bytes accessed | tf_op | source)
XLA Modules:
  0.0 194.0 jit_solution(5624598394385387779)
XLA Ops:
  0.7 0.9 copy.74
  1.5 0.1 eq.35
  1.7 0.6 reduce-window.6
  2.3 0.2 slice_reduce_fusion
  2.5 0.1 bitcast_bitcast_fusion.2
  2.7 0.1 reduce_sum.42
  2.8 0.1 copy.77
  2.8 0.7 multiply_add_fusion
  3.5 0.1 iota_compare_fusion
  3.6 0.1 convert_reduce_fusion.1
  3.7 0.8 copy.91
  4.5 0.3 fusion.22
  4.8 1.0 convolution_convert_fusion.2
  5.8 0.9 convolution_convert_fusion.3
  6.7 0.7 all_to_all.23
  7.4 11.3 %all-to-all-start = ((bf16[32,6,256]{2,1,0:T(8,128)(2,1)}), bf16[32,6,256]{2,1,0:T(8,128)(2,1)S(1)}, u32[]{:S(2)}, u32[]{:S(2)}) async-start(bf16[32,6,256]{2,1,0:T(8,128)(2,1)} %all_to_all.23), calls=%async_computation | async-start | bytes 262144 | tf_op jit(solution)/shard_map/all_to_all | solution.py:83
  18.7 0.1 copy.113
  18.8 9.7 %all-to-all-done = bf16[32,6,256]{2,1,0:T(8,128)(2,1)S(1)} async-done(((bf16[32,6,256]{2,1,0:T(8,128)(2,1)}), bf16[32,6,256]{2,1,0:T(8,128)(2,1)S(1)}, u32[]{:S(2)}, u32[]{:S(2)}) %all-to-all-start) | async-done | bytes 98336 | tf_op jit(solution)/shard_map/all_to_all | solution.py:83
  28.6 0.7 fusion.4
  29.3 1.0 copy.82
  30.3 18.9 %all-to-all-start.2 = ((bf16[16,32,2,3,88]{4,1,3,2,0:T(8,128)(2,1)}), bf16[16,32,2,3,88]{4,1,3,2,0:T(8,128)(2,1)S(1)}, u32[]{:S(2)}, u32[]{:S(2)}) async-start(bf16[16,32,2,3,88]{4,1,3,2,0:T(8,128)(2,1)} %copy.82), calls=%async_computation.2 | async-start | bytes 1572864 | tf_op jit(solution)/shard_map/all_to_all | solution.py:106
  49.2 1.0 bitcast_bitcast_fusion.1
  50.2 0.1 copy.114
  50.4 1.0 bitcast_bitcast_fusion
  51.4 31.8 %all_gather.3 = bf16[192,2048]{1,0:T(8,128)(2,1)S(1)} all-gather(bf16[192,128]{1,0:T(8,128)(2,1)S(1)} %get-tuple-element.15), channel_id=1, replica_groups=mesh['dp'=2,'expert'=32,'fsdp'=16] {'fsdp'}, dimensions={1}, use_global_device_ids=true | all-gather | bytes 835584 | tf_op jit(solution)/shard_map/all_gather | solution.py:87
  83.2 0.5 reshape.94
  83.7 2.6 %convolution_bitcast_fusion.4 = f32[32,2,3,88]{3,0,2,1:T(8,128)} fusion(bf16[2,88,2048]{2,1,0:T(8,128)(2,1)} %param.11, bf16[32,2,3,2048]{3,2,1,0:T(4,128)(2,1)S(1)} %reshape.94), kind=kOutput, calls=%fused_computation.20 | convolution fusion | flops 69206016 | bytes 1574912 | tf_op jit(solution)/shard_map/jecd,efd->jecf/dot_general | solution.py:91
  86.3 0.2 convert_reduce_fusion
  86.5 1.7 multiply_convert_fusion.2
  88.2 1.7 fusion.1
  89.8 1.1 broadcast_in_dim.2
  90.9 6.0 %all-to-all-start.1 = ((bf16[16,32,2,3,88]{4,1,3,2,0:T(8,128)(2,1)}), bf16[16,32,2,3,88]{4,1,3,2,0:T(8,128)(2,1)S(1)}, u32[]{:S(2)}, u32[]{:S(2)}) async-start(bf16[16,32,2,3,88]{4,1,3,2,0:T(8,128)(2,1)} %broadcast_in_dim.2), calls=%async_computation.1 | async-start | bytes 1572864 | tf_op jit(solution)/shard_map/all_to_all | solution.py:31
  96.9 0.8 fusion.2
  97.7 0.3 copy-done.5
  98.0 0.1 fusion.11
  98.1 0.3 fusion.8
  98.4 1.0 copy.115
  99.4 0.4 fusion.17
  99.8 0.7 copy-done.4
  100.5 0.4 fusion.5
  100.9 1.0 copy.85
  101.9 17.6 %all-to-all-done.1 = bf16[16,32,2,3,88]{4,1,3,2,0:T(8,128)(2,1)S(1)} async-done(((bf16[16,32,2,3,88]{4,1,3,2,0:T(8,128)(2,1)}), bf16[16,32,2,3,88]{4,1,3,2,0:T(8,128)(2,1)S(1)}, u32[]{:S(2)}, u32[]{:S(2)}) %all-to-all-start.1) | async-done | bytes 540704 | tf_op jit(solution)/shard_map/all_to_all | solution.py:31
  119.5 4.2 %all-to-all-start.3 = ((bf16[16,32,2,3,128]{4,1,3,2,0:T(8,128)(2,1)}), bf16[16,32,2,3,128]{4,1,3,2,0:T(8,128)(2,1)}, u32[]{:S(2)}, u32[]{:S(2)}) async-start(bf16[16,32,2,3,128]{4,1,3,2,0:T(8,128)(2,1)} %copy.85), calls=%async_computation.3 | async-start | bytes 1572864 | tf_op jit(solution)/shard_map/all_to_all | solution.py:116
  123.7 1.4 copy.80
  125.1 2.0 %reshape.95 = bf16[32,2,3,1408]{3,0,2,1:T(8,128)(2,1)S(1)} reshape(bf16[32,2,3,16,88]{4,3,0,2,1:T(8,128)(2,1)} %copy.80) | data formatting | bytes 1081344 | tf_op jit(solution)/shard_map/reshape | solution.py:33
  127.1 0.4 fusion
  127.6 0.1 fusion.21
  127.7 0.9 copy-done.2
  128.6 1.1 pad_maximum_fusion
  129.7 4.4 %collective-permute-start = (bf16[540672]{0:T(1024)(128)(2,1)}, bf16[540672]{0:T(1024)(128)(2,1)}, u32[]{:S(2)}, u32[]{:S(2)}) collective-permute-start(bf16[540672]{0:T(1024)(128)(2,1)} %pad_maximum_fusion), channel_id=1, source_target_pairs={{0,512},{512,0},{1,513},{513,1},{2,514},{514,2},{3,515},{515,3},{4... | collective-permute-start | bytes 3244040 | tf_op jit(solution)/shard_map/ppermute | solution.py:43
  134.1 0.3 convolution_convert_fusion.1
  134.4 11.4 %all-to-all-done.3 = bf16[16,32,2,3,128]{4,1,3,2,0:T(8,128)(2,1)} async-done(((bf16[16,32,2,3,128]{4,1,3,2,0:T(8,128)(2,1)}), bf16[16,32,2,3,128]{4,1,3,2,0:T(8,128)(2,1)}, u32[]{:S(2)}, u32[]{:S(2)}) %all-to-all-start.3) | async-done | bytes 786464 | tf_op jit(solution)/shard_map/all_to_all | solution.py:116
  145.8 1.2 reduce_sum.45
  147.0 0.7 copy.86
  147.8 3.9 %all-to-all-start.4 = ((bf16[32,6,256]{2,1,0:T(8,128)(2,1)}), bf16[32,6,256]{2,1,0:T(8,128)(2,1)S(1)}, u32[]{:S(2)}, u32[]{:S(2)}) async-start(bf16[32,6,256]{2,1,0:T(8,128)(2,1)} %copy.86), calls=%async_computation.4 | async-start | bytes 262144 | tf_op jit(solution)/shard_map/all_to_all | solution.py:122
  151.6 32.6 %all-to-all-done.4 = bf16[32,6,256]{2,1,0:T(8,128)(2,1)S(1)} async-done(((bf16[32,6,256]{2,1,0:T(8,128)(2,1)}), bf16[32,6,256]{2,1,0:T(8,128)(2,1)S(1)}, u32[]{:S(2)}, u32[]{:S(2)}) %all-to-all-start.4) | async-done | bytes 98336 | tf_op jit(solution)/shard_map/all_to_all | solution.py:122
  184.2 0.8 convolution_convert_fusion.4
  185.0 0.8 convolution_convert_fusion.5
  185.8 2.3 %slice_convert_fusion = f32[360448]{0:T(1024)} fusion(bf16[540672]{0:T(1024)(128)(2,1)} %collective-permute-done), kind=kLoop, calls=%fused_computation.38 | loop fusion | flops 360448 | bytes 2162688 | tf_op jit(solution)/shard_map/convert_element_type | solution.py:50
  188.1 2.5 %reshape.104 = f32[2,2,88,1024]{3,2,1,0:T(8,128)} reshape(f32[360448]{0:T(1024)} %slice_convert_fusion) | data formatting | bytes 2883584 | tf_op jit(solution)/shard_map/convert_element_type | solution.py:50
  190.6 1.1 slice.69
  191.7 0.9 fusion.12
  192.7 0.5 fusion.3
  193.1 0.9 slice_bitcast_fusion
  (29 shorter events, 0.3 us)
Async XLA Ops:
  0.6 28.0 %copy-start = (bf16[2,1408,128]{2,1,0:T(8,128)(2,1)S(1)}, bf16[2,1408,128]{2,1,0:T(8,128)(2,1)}, u32[]{:S(2)}) copy-start(bf16[2,1408,128]{2,1,0:T(8,128)(2,1)} %param.13) | copy-start | bytes 2162692
  0.6 18.0 %copy-start.6 = (bf16[2,88,2048]{2,1,0:T(8,128)(2,1)S(1)}, bf16[2,88,2048]{2,1,0:T(8,128)(2,1)}, u32[]{:S(2)}) copy-start(bf16[2,88,2048]{2,1,0:T(8,128)(2,1)} %param.11) | copy-start | bytes 2162692
  7.4 21.1 %all-to-all-start = ((bf16[32,6,256]{2,1,0:T(8,128)(2,1)}), bf16[32,6,256]{2,1,0:T(8,128)(2,1)S(1)}, u32[]{:S(2)}, u32[]{:S(2)}) async-start(bf16[32,6,256]{2,1,0:T(8,128)(2,1)} %all_to_all.23), calls=%async_computation | async-start | bytes 262144 | tf_op jit(solution)/shard_map/all_to_all | solution.py:83
  30.3 19.9 %copy-start.7 = (bf16[2,88,2048]{2,1,0:T(8,128)(2,1)S(1)}, bf16[2,88,2048]{2,1,0:T(8,128)(2,1)}, u32[]{:S(2)}) copy-start(bf16[2,88,2048]{2,1,0:T(8,128)(2,1)} %param.12) | copy-start | bytes 2162692
  30.3 56.0 %all-to-all-start.2 = ((bf16[16,32,2,3,88]{4,1,3,2,0:T(8,128)(2,1)}), bf16[16,32,2,3,88]{4,1,3,2,0:T(8,128)(2,1)S(1)}, u32[]{:S(2)}, u32[]{:S(2)}) async-start(bf16[16,32,2,3,88]{4,1,3,2,0:T(8,128)(2,1)} %copy.82), calls=%async_computation.2 | async-start | bytes 1572864 | tf_op jit(solution)/shard_map/all_to_all | solution.py:106
  83.7 2.8 %copy-start.8 = (bf16[2,88,2048]{2,1,0:T(8,128)(2,1)S(1)}, bf16[2,88,2048]{2,1,0:T(8,128)(2,1)}, u32[]{:S(2)}) copy-start(bf16[2,88,2048]{2,1,0:T(8,128)(2,1)} %param.12) | copy-start | bytes 2162692
  90.9 28.6 %all-to-all-start.1 = ((bf16[16,32,2,3,88]{4,1,3,2,0:T(8,128)(2,1)}), bf16[16,32,2,3,88]{4,1,3,2,0:T(8,128)(2,1)S(1)}, u32[]{:S(2)}, u32[]{:S(2)}) async-start(bf16[16,32,2,3,88]{4,1,3,2,0:T(8,128)(2,1)} %broadcast_in_dim.2), calls=%async_computation.1 | async-start | bytes 1572864 | tf_op jit(solution)/shard_map/all_to_all | solution.py:31
  96.9 1.1 copy-start.5
  98.1 1.3 copy-start.3
  99.4 1.1 copy-start.4
  119.5 26.2 %all-to-all-start.3 = ((bf16[16,32,2,3,128]{4,1,3,2,0:T(8,128)(2,1)}), bf16[16,32,2,3,128]{4,1,3,2,0:T(8,128)(2,1)}, u32[]{:S(2)}, u32[]{:S(2)}) async-start(bf16[16,32,2,3,128]{4,1,3,2,0:T(8,128)(2,1)} %copy.85), calls=%async_computation.3 | async-start | bytes 1572864 | tf_op jit(solution)/shard_map/all_to_all | solution.py:116
  127.5 1.1 copy-start.2
  129.7 56.1 %collective-permute-start = (bf16[540672]{0:T(1024)(128)(2,1)}, bf16[540672]{0:T(1024)(128)(2,1)}, u32[]{:S(2)}, u32[]{:S(2)}) collective-permute-start(bf16[540672]{0:T(1024)(128)(2,1)} %pad_maximum_fusion), channel_id=1, source_target_pairs={{0,512},{512,0},{1,513},{513,1},{2,514},{514,2},{3,515},{515,3},{4... | collective-permute-start | bytes 3244040 | tf_op jit(solution)/shard_map/ppermute | solution.py:43
  147.8 36.4 %all-to-all-start.4 = ((bf16[32,6,256]{2,1,0:T(8,128)(2,1)}), bf16[32,6,256]{2,1,0:T(8,128)(2,1)S(1)}, u32[]{:S(2)}, u32[]{:S(2)}) async-start(bf16[32,6,256]{2,1,0:T(8,128)(2,1)} %copy.86), calls=%async_computation.4 | async-start | bytes 262144 | tf_op jit(solution)/shard_map/all_to_all | solution.py:122
  190.6 2.1 %copy-start.1 = (f32[2,2,88,1024]{3,2,1,0:T(8,128)S(1)}, f32[2,2,88,1024]{3,2,1,0:T(8,128)}, u32[]{:S(2)}) copy-start(f32[2,2,88,1024]{3,2,1,0:T(8,128)} %reshape.104) | copy-start | bytes 4325380

commit v13 on v11

--- a/solution.py
+++ b/solution.py
@@ -100,6 +100,20 @@
         ),
         axis=0,
     ).astype(jnp.bfloat16)
+    grad_gate_w = rounded(
+        jnp.einsum("jecf,jecd->efd", grad_gate_pre, received, preferred_element_type=jnp.float32)
+    )
+    grad_up_w = rounded(
+        jnp.einsum("jecf,jecd->efd", grad_up_pre, received, preferred_element_type=jnp.float32)
+    )
+    grad_down_w = rounded(
+        jnp.einsum("jecf,jecd->efd", hidden_all, cotangent, preferred_element_type=jnp.float32)
+    )
+    gate_up_w, input_slices = lax.optimization_barrier(
+        (jnp.stack([grad_gate_w, grad_up_w]).astype(jnp.bfloat16), input_slices)
+    )
+    summed_gate, summed_up = dp_reduce(gate_up_w, 3).astype(jnp.float32)
+    summed_down = dp_reduce(grad_down_w.astype(jnp.bfloat16), 1)
     feat = input_slices.shape[-1]
     both_back = lax.all_to_all(
         jnp.concatenate(
@@ -114,19 +128,6 @@
     grad_tokens = jnp.dot(
         picker.T, input_slots.astype(jnp.float32), precision=lax.Precision.HIGHEST
     ).astype(jnp.bfloat16)
-    grad_gate_w = rounded(
-        jnp.einsum("jecf,jecd->efd", grad_gate_pre, received, preferred_element_type=jnp.float32)
-    )
-    grad_up_w = rounded(
-        jnp.einsum("jecf,jecd->efd", grad_up_pre, received, preferred_element_type=jnp.float32)
-    )
-    grad_down_w = rounded(
-        jnp.einsum("jecf,jecd->efd", hidden_all, cotangent, preferred_element_type=jnp.float32)
-    )
-    summed_gate, summed_up = dp_reduce(
-        jnp.stack([grad_gate_w, grad_up_w]).astype(jnp.bfloat16), 3
-    ).astype(jnp.float32)
-    summed_down = dp_reduce(grad_down_w.astype(jnp.bfloat16), 1)
     return (
         mixed,
         grad_tokens,

time: 165 us -> 190 us (1.15)
  waiting for transfers between devices: 39.3 us -> 59.2 us
    all_to_all x1, waiting for transfers between devices: 5.8 us -> 28.1 us  [body(): lax.all_to_all(jnp.concatenate([expert_out.reshape(slot_count, -1), input...]
    ppermute x2, waiting for transfers between devices: 19.7 us -> 0.01 us  [dp_reduce(): got = lax.ppermute(send, 'dp', perm=[(0, 1), (1, 0)])]
    all_to_all x1, waiting for transfers between devices: 0.01 us -> 11.6 us  [body(): lax.all_to_all(input_parts.astype(jnp.bfloat16), 'fsdp', 0, 0, tiled=False)]
    all_to_all x1, waiting for transfers between devices: 13.8 us -> 19.5 us  [gather_fsdp(): got = lax.all_to_all(copies, 'fsdp', 0, 0, tiled=False)]
  transfers between devices with their start and end apart: 6 -> 6, of which waited for: 4 -> 3; matrix products, arithmetic and copies ran while one was open for 11% -> 11% of each run, Pallas kernels for 0% -> 0%
where the time goes in v13:
time: 190 us; the launch traced here: 189 us
  waiting for transfers between devices  59.2 us (31%)
  blocking collectives  52.8 us (28%)
  starting transfers between devices  41.9 us (22%)
  local copies, waits for them, and re-layouts  13.8 us (7%)
  matrix products  11.8 us (6%)
  other arithmetic  8.92 us (5%)
    all_gather x1, blocking collectives, body(): lax.all_gather(both_in[:, :local_feat], 'fsdp', axis=1, tiled=True)  31.8 us
    all_to_all x1, waiting for transfers between devices, body(): lax.all_to_all(jnp.concatenate([expert_out.reshape(slot_count, -1), input...  28.1 us
    all_to_all x1, blocking collectives, body(): lax.all_to_all(jnp.concatenate([outgoing, scaled_grad], axis=1), 'expert'...  20.9 us
    all_to_all x1, waiting for transfers between devices, gather_fsdp(): got = lax.all_to_all(copies, 'fsdp', 0, 0, tiled=False)  19.5 us
    all_to_all x1, starting transfers between devices, body(): lax.all_to_all(hidden_parts, 'fsdp', 0, 0, tiled=False).astype(jnp.float32)  18.9 us
    all_to_all x1, waiting for transfers between devices, body(): lax.all_to_all(input_parts.astype(jnp.bfloat16), 'fsdp', 0, 0, tiled=False)  11.6 us
    ppermute x2, starting transfers between devices, dp_reduce(): got = lax.ppermute(send, 'dp', perm=[(0, 1), (1, 0)])  8.81 us
    all_to_all x1, starting transfers between devices, gather_fsdp(): got = lax.all_to_all(copies, 'fsdp', 0, 0, tiled=False)  6.09 us
  transfers between devices with their start and end apart: 6, of which 3 were waited for; matrix products, arithmetic and copies ran while one was open for 11% of the time, Pallas kernels for 0%

profile of v13, /device:TPU:1, one launch (start us, length us, event | category | flops | bytes accessed | tf_op | source)
XLA Modules:
  0.0 189.2 jit_solution(17199637791614816181)
XLA Ops:
  0.6 0.0 copy-start
  0.6 0.8 copy.74
  1.5 0.1 eq.35
  1.6 0.6 reduce-window.6
  2.2 0.2 slice_reduce_fusion
  2.5 0.1 bitcast_bitcast_fusion.2
  2.6 0.1 reduce_sum.42
  2.7 0.1 copy.77
  2.8 0.7 multiply_add_fusion
  3.5 0.1 iota_compare_fusion
  3.6 0.1 convert_reduce_fusion.1
  3.7 0.8 copy.91
  4.5 0.3 fusion.21
  4.7 1.0 convolution_convert_fusion.2
  5.7 0.9 convolution_convert_fusion.3
  6.7 20.9 %all_to_all.36 = bf16[32,6,256]{2,1,0:T(8,128)(2,1)S(1)} all-to-all(bf16[32,6,256]{2,1,0:T(8,128)(2,1)S(1)} %all_to_all.23), channel_id=1, replica_groups=mesh['dp'=2,'expert'=32,'fsdp'=16] {'expert'}, dimensions={0} | all-to-all | bytes 196608 | tf_op jit(solution)/shard_map/all_to_all | solution.py:65
  27.7 0.0 copy-done
  27.7 0.7 fusion.4
  28.4 0.0 copy-start.2
  28.4 1.0 copy.82
  29.4 18.9 %all-to-all-start.2 = ((bf16[16,32,2,3,88]{4,1,3,2,0:T(8,128)(2,1)}), bf16[16,32,2,3,88]{4,1,3,2,0:T(8,128)(2,1)S(1)}, u32[]{:S(2)}, u32[]{:S(2)}) async-start(bf16[16,32,2,3,88]{4,1,3,2,0:T(8,128)(2,1)} %copy.82), calls=%async_computation.2 | async-start | bytes 1572864 | tf_op jit(solution)/shard_map/all_to_all | solution.py:88
  48.3 0.0 copy-done.2
  48.3 1.0 copy.113
  49.4 1.0 copy.114
  50.4 31.8 %all_gather.3 = bf16[192,2048]{1,0:T(8,128)(2,1)S(1)} all-gather(bf16[192,128]{1,0:T(8,128)(2,1)S(1)} %get-tuple-element.18), channel_id=1, replica_groups=mesh['dp'=2,'expert'=32,'fsdp'=16] {'fsdp'}, dimensions={1}, use_global_device_ids=true | all-gather | bytes 835584 | tf_op jit(solution)/shard_map/all_gather | solution.py:69
  82.3 0.5 reshape.66
  82.8 0.0 copy-start.4
  82.8 2.6 %convolution_bitcast_fusion.4 = f32[32,2,3,88]{3,0,2,1:T(8,128)} fusion(bf16[2,88,2048]{2,1,0:T(8,128)(2,1)} %param.11, bf16[32,2,3,2048]{3,2,1,0:T(4,128)(2,1)S(1)} %reshape.66), kind=kOutput, calls=%fused_computation.19 | convolution fusion | flops 69206016 | bytes 1574912 | tf_op jit(solution)/shard_map/jecd,efd->jecf/dot_general | solution.py:73
  85.4 0.0 all-to-all-done.2
  85.4 0.2 convert_reduce_fusion
  85.6 1.7 multiply_convert_fusion.2
  87.3 1.1 broadcast_in_dim.2
  88.3 6.1 %all-to-all-start.1 = ((bf16[16,32,2,3,88]{4,1,3,2,0:T(8,128)(2,1)}), bf16[16,32,2,3,88]{4,1,3,2,0:T(8,128)(2,1)S(1)}, u32[]{:S(2)}, u32[]{:S(2)}) async-start(bf16[16,32,2,3,88]{4,1,3,2,0:T(8,128)(2,1)} %broadcast_in_dim.2), calls=%async_computation.1 | async-start | bytes 1572864 | tf_op jit(solution)/shard_map/all_to_all | solution.py:31
  94.4 1.2 bitcast_bitcast_fusion.1
  95.7 0.1 bitcast_bitcast_fusion
  95.8 0.4 fusion.15
  96.2 0.4 fusion.5
  96.5 1.0 copy.87
  97.5 19.5 %all-to-all-done.1 = bf16[16,32,2,3,88]{4,1,3,2,0:T(8,128)(2,1)S(1)} async-done(((bf16[16,32,2,3,88]{4,1,3,2,0:T(8,128)(2,1)}), bf16[16,32,2,3,88]{4,1,3,2,0:T(8,128)(2,1)S(1)}, u32[]{:S(2)}, u32[]{:S(2)}) %all-to-all-start.1) | async-done | bytes 540704 | tf_op jit(solution)/shard_map/all_to_all | solution.py:31
  117.1 4.2 %all-to-all-start.3 = ((bf16[16,32,2,3,128]{4,1,3,2,0:T(8,128)(2,1)}), bf16[16,32,2,3,128]{4,1,3,2,0:T(8,128)(2,1)}, u32[]{:S(2)}, u32[]{:S(2)}) async-start(bf16[16,32,2,3,128]{4,1,3,2,0:T(8,128)(2,1)} %copy.87), calls=%async_computation.3 | async-start | bytes 1572864 | tf_op jit(solution)/shard_map/all_to_all | solution.py:98
  121.3 0.8 fusion.2
  122.1 0.8 fusion.1
  122.9 1.2 pad_maximum_fusion
  124.1 0.5 copy.80
  124.6 0.9 reshape.67
  125.5 0.4 fusion
  126.0 0.9 fusion.18
  126.9 4.4 %collective-permute-start.1 = (bf16[2,704,128]{2,1,0:T(8,128)(2,1)}, bf16[2,704,128]{2,1,0:T(8,128)(2,1)S(1)}, u32[]{:S(2)}, u32[]{:S(2)}) collective-permute-start(bf16[2,704,128]{2,1,0:T(8,128)(2,1)} %fusion.18), channel_id=1, source_target_pairs={{0,512},{512,0},{1,513},{513,1},{2,514},{514,2},{3,515},{515,3},{4... | collective-permute-start | bytes 1081352 | tf_op jit(solution)/shard_map/ppermute | solution.py:24
  131.3 0.3 convolution_convert_fusion.1
  131.6 11.6 %all-to-all-done.3 = bf16[16,32,2,3,128]{4,1,3,2,0:T(8,128)(2,1)} async-done(((bf16[16,32,2,3,128]{4,1,3,2,0:T(8,128)(2,1)}), bf16[16,32,2,3,128]{4,1,3,2,0:T(8,128)(2,1)}, u32[]{:S(2)}, u32[]{:S(2)}) %all-to-all-start.3) | async-done | bytes 786464 | tf_op jit(solution)/shard_map/all_to_all | solution.py:98
  143.2 1.2 reduce_sum.45
  144.5 1.5 slice_bitcast_fusion
  146.0 1.1 fusion.7
  147.1 4.4 %collective-permute-start = (bf16[2,2,88,1024]{3,2,1,0:T(8,128)(2,1)}, bf16[2,2,88,1024]{3,2,1,0:T(8,128)(2,1)}, u32[]{:S(2)}, u32[]{:S(2)}) collective-permute-start(bf16[2,2,88,1024]{3,2,1,0:T(8,128)(2,1)} %fusion.7), channel_id=1, source_target_pairs={{0,512},{512,0},{1,513},{513,1},{2,514},{514,2},{3,515},{515,3},{4... | collective-permute-start | bytes 2162696 | tf_op jit(solution)/shard_map/ppermute | solution.py:24
  151.5 0.7 copy.88
  152.2 3.9 %all-to-all-start.4 = ((bf16[32,6,256]{2,1,0:T(8,128)(2,1)}), bf16[32,6,256]{2,1,0:T(8,128)(2,1)S(1)}, u32[]{:S(2)}, u32[]{:S(2)}) async-start(bf16[32,6,256]{2,1,0:T(8,128)(2,1)} %copy.88), calls=%async_computation.4 | async-start | bytes 262144 | tf_op jit(solution)/shard_map/all_to_all | solution.py:118
  156.1 0.0 collective-permute-done.1
  156.1 0.9 fusion.10
  157.1 28.1 %all-to-all-done.4 = bf16[32,6,256]{2,1,0:T(8,128)(2,1)S(1)} async-done(((bf16[32,6,256]{2,1,0:T(8,128)(2,1)}), bf16[32,6,256]{2,1,0:T(8,128)(2,1)S(1)}, u32[]{:S(2)}, u32[]{:S(2)}) %all-to-all-start.4) | async-done | bytes 98336 | tf_op jit(solution)/shard_map/all_to_all | solution.py:118
  185.2 0.8 convolution_convert_fusion.5
  186.0 0.8 convolution_convert_fusion.4
  186.7 0.0 collective-permute-done
  186.7 1.6 fusion.3
  188.3 0.9 slice_bitcast_fusion.4
  (18 shorter events, 0.3 us)
Async XLA Ops:
  0.6 27.1 %copy-start = (bf16[2,1408,128]{2,1,0:T(8,128)(2,1)S(1)}, bf16[2,1408,128]{2,1,0:T(8,128)(2,1)}, u32[]{:S(2)}) copy-start(bf16[2,1408,128]{2,1,0:T(8,128)(2,1)} %param.13) | copy-start | bytes 2162692
  28.4 19.9 %copy-start.2 = (bf16[2,88,2048]{2,1,0:T(8,128)(2,1)S(1)}, bf16[2,88,2048]{2,1,0:T(8,128)(2,1)}, u32[]{:S(2)}) copy-start(bf16[2,88,2048]{2,1,0:T(8,128)(2,1)} %param.11) | copy-start | bytes 2162692
  29.4 20.0 %copy-start.3 = (bf16[2,88,2048]{2,1,0:T(8,128)(2,1)S(1)}, bf16[2,88,2048]{2,1,0:T(8,128)(2,1)}, u32[]{:S(2)}) copy-start(bf16[2,88,2048]{2,1,0:T(8,128)(2,1)} %param.12) | copy-start | bytes 2162692
  29.4 56.0 %all-to-all-start.2 = ((bf16[16,32,2,3,88]{4,1,3,2,0:T(8,128)(2,1)}), bf16[16,32,2,3,88]{4,1,3,2,0:T(8,128)(2,1)S(1)}, u32[]{:S(2)}, u32[]{:S(2)}) async-start(bf16[16,32,2,3,88]{4,1,3,2,0:T(8,128)(2,1)} %copy.82), calls=%async_computation.2 | async-start | bytes 1572864 | tf_op jit(solution)/shard_map/all_to_all | solution.py:88
  82.8 2.8 %copy-start.4 = (bf16[2,88,2048]{2,1,0:T(8,128)(2,1)S(1)}, bf16[2,88,2048]{2,1,0:T(8,128)(2,1)}, u32[]{:S(2)}) copy-start(bf16[2,88,2048]{2,1,0:T(8,128)(2,1)} %param.12) | copy-start | bytes 2162692
  88.3 7.3 %copy-start.1 = (bf16[22,8,16,128]{3,2,1,0:T(8,128)(2,1)S(1)}, bf16[22,8,16,128]{3,2,1,0:T(8,128)(2,1)}, u32[]{:S(2)}) copy-start(bf16[22,8,16,128]{3,2,1,0:T(8,128)(2,1)} %copy.114) | copy-start | bytes 2162692
  88.3 28.8 %all-to-all-start.1 = ((bf16[16,32,2,3,88]{4,1,3,2,0:T(8,128)(2,1)}), bf16[16,32,2,3,88]{4,1,3,2,0:T(8,128)(2,1)S(1)}, u32[]{:S(2)}, u32[]{:S(2)}) async-start(bf16[16,32,2,3,88]{4,1,3,2,0:T(8,128)(2,1)} %broadcast_in_dim.2), calls=%async_computation.1 | async-start | bytes 1572864 | tf_op jit(solution)/shard_map/all_to_all | solution.py:31
  117.1 26.1 %all-to-all-start.3 = ((bf16[16,32,2,3,128]{4,1,3,2,0:T(8,128)(2,1)}), bf16[16,32,2,3,128]{4,1,3,2,0:T(8,128)(2,1)}, u32[]{:S(2)}, u32[]{:S(2)}) async-start(bf16[16,32,2,3,128]{4,1,3,2,0:T(8,128)(2,1)} %copy.87), calls=%async_computation.3 | async-start | bytes 1572864 | tf_op jit(solution)/shard_map/all_to_all | solution.py:98
  126.9 29.2 %collective-permute-start.1 = (bf16[2,704,128]{2,1,0:T(8,128)(2,1)}, bf16[2,704,128]{2,1,0:T(8,128)(2,1)S(1)}, u32[]{:S(2)}, u32[]{:S(2)}) collective-permute-start(bf16[2,704,128]{2,1,0:T(8,128)(2,1)} %fusion.18), channel_id=1, source_target_pairs={{0,512},{512,0},{1,513},{513,1},{2,514},{514,2},{3,515},{515,3},{4... | collective-permute-start | bytes 1081352 | tf_op jit(solution)/shard_map/ppermute | solution.py:24
  147.1 39.6 %collective-permute-start = (bf16[2,2,88,1024]{3,2,1,0:T(8,128)(2,1)}, bf16[2,2,88,1024]{3,2,1,0:T(8,128)(2,1)}, u32[]{:S(2)}, u32[]{:S(2)}) collective-permute-start(bf16[2,2,88,1024]{3,2,1,0:T(8,128)(2,1)} %fusion.7), channel_id=1, source_target_pairs={{0,512},{512,0},{1,513},{513,1},{2,514},{514,2},{3,515},{515,3},{4... | collective-permute-start | bytes 2162696 | tf_op jit(solution)/shard_map/ppermute | solution.py:24
  152.2 32.9 %all-to-all-start.4 = ((bf16[32,6,256]{2,1,0:T(8,128)(2,1)}), bf16[32,6,256]{2,1,0:T(8,128)(2,1)S(1)}, u32[]{:S(2)}, u32[]{:S(2)}) async-start(bf16[32,6,256]{2,1,0:T(8,128)(2,1)} %copy.88), calls=%async_computation.4 | async-start | bytes 262144 | tf_op jit(solution)/shard_map/all_to_all | solution.py:118

commit v14 on v11

--- a/solution.py
+++ b/solution.py
@@ -94,6 +94,10 @@
     input_parts = jnp.einsum(
         "jecf,efgd->gjecd", grad_gate_pre, w_gate_g, preferred_element_type=jnp.float32
     ) + jnp.einsum("jecf,efgd->gjecd", grad_up_pre, w_up_g, preferred_element_type=jnp.float32)
+    grad_down_w = rounded(
+        jnp.einsum("jecf,jecd->efd", hidden_all, cotangent, preferred_element_type=jnp.float32)
+    )
+    grad_down_w, input_parts = lax.optimization_barrier((grad_down_w, input_parts))
     input_slices = jnp.sum(
         lax.all_to_all(input_parts.astype(jnp.bfloat16), "fsdp", 0, 0, tiled=False).astype(
             jnp.float32
@@ -119,9 +123,6 @@
     )
     grad_up_w = rounded(
         jnp.einsum("jecf,jecd->efd", grad_up_pre, received, preferred_element_type=jnp.float32)
-    )
-    grad_down_w = rounded(
-        jnp.einsum("jecf,jecd->efd", hidden_all, cotangent, preferred_element_type=jnp.float32)
     )
     summed_gate, summed_up = dp_reduce(
         jnp.stack([grad_gate_w, grad_up_w]).astype(jnp.bfloat16), 3

time: 165 us -> 167 us (1.012)
  blocking collectives: 51.7 us -> 31.8 us
  starting transfers between devices: 41.4 us -> 52.3 us
  waiting for transfers between devices: 39.3 us -> 46 us
  matrix products: 11.8 us -> 14.4 us
  local copies, waits for them, and re-layouts: 12.1 us -> 14.3 us
    all_to_all x1 -> x0, blocking collectives: 20.9 us -> none  [body(): lax.all_to_all(jnp.concatenate([outgoing, scaled_grad], axis=1), 'expert'...]
    all_to_all x0 -> x1, starting transfers between devices: none -> 11.3 us  [body(): lax.all_to_all(jnp.concatenate([outgoing, scaled_grad], axis=1), 'expert'...]
    all_to_all x0 -> x1, waiting for transfers between devices: none -> 9.68 us  [body(): lax.all_to_all(jnp.concatenate([outgoing, scaled_grad], axis=1), 'expert'...]
    ppermute x2, waiting for transfers between devices: 19.7 us -> 11.3 us  [dp_reduce(): got = lax.ppermute(send, 'dp', perm=[(0, 1), (1, 0)])]
    all_to_all x1, waiting for transfers between devices: 0.01 us -> 4.14 us  [body(): lax.all_to_all(input_parts.astype(jnp.bfloat16), 'fsdp', 0, 0, tiled=False)]
    dot_general x1, matrix products: 0.41 us -> 2.11 us  [body(): jnp.einsum('jecf,jecd->efd', hidden_all, cotangent, preferred_element_typ...]
    unnamed x16 -> x22, local copies, waits for them, and re-layouts: 3.75 us -> 2.44 us
  transfers between devices with their start and end apart: 6 -> 7, of which waited for: 4 -> 6; matrix products, arithmetic and copies ran while one was open for 11% -> 13% of each run, Pallas kernels for 0% -> 0%
where the time goes in v14:
time: 167 us; the launch traced here: 166 us
  starting transfers between devices  52.3 us (31%)
  waiting for transfers between devices  46 us (28%)
  blocking collectives  31.8 us (19%)
  matrix products  14.4 us (9%)
  local copies, waits for them, and re-layouts  14.3 us (9%)
  other arithmetic  6.67 us (4%)
    all_gather x1, blocking collectives, body(): lax.all_gather(both_in[:, :local_feat], 'fsdp', axis=1, tiled=True)  31.8 us
    all_to_all x1, starting transfers between devices, body(): lax.all_to_all(hidden_parts, 'fsdp', 0, 0, tiled=False).astype(jnp.float32)  18.9 us
    all_to_all x1, waiting for transfers between devices, gather_fsdp(): got = lax.all_to_all(copies, 'fsdp', 0, 0, tiled=False)  13.9 us
    all_to_all x1, starting transfers between devices, body(): lax.all_to_all(jnp.concatenate([outgoing, scaled_grad], axis=1), 'expert'...  11.3 us
    ppermute x2, waiting for transfers between devices, dp_reduce(): got = lax.ppermute(send, 'dp', perm=[(0, 1), (1, 0)])  11.3 us
    all_to_all x1, waiting for transfers between devices, body(): lax.all_to_all(jnp.concatenate([outgoing, scaled_grad], axis=1), 'expert'...  9.68 us
    ppermute x2, starting transfers between devices, dp_reduce(): got = lax.ppermute(send, 'dp', perm=[(0, 1), (1, 0)])  8.76 us
    all_to_all x1, waiting for transfers between devices, body(): lax.all_to_all(jnp.concatenate([expert_out.reshape(slot_count, -1), input...  6.97 us
  transfers between devices with their start and end apart: 7, of which 6 were waited for; matrix products, arithmetic and copies ran while one was open for 13% of the time, Pallas kernels for 0%

profile of v14, /device:TPU:1, one launch (start us, length us, event | category | flops | bytes accessed | tf_op | source)
XLA Modules:
  0.0 166.4 jit_solution(10704130104497215234)
XLA Ops:
  0.6 0.0 copy-start
  0.6 0.0 copy-start.5
  0.7 0.9 copy.74
  1.5 0.1 eq.35
  1.7 0.6 reduce-window.6
  2.3 0.2 slice_reduce_fusion
  2.5 0.1 bitcast_bitcast_fusion.2
  2.7 0.1 reduce_sum.42
  2.8 0.1 copy.77
  2.8 0.7 multiply_add_fusion
  3.5 0.1 iota_compare_fusion
  3.6 0.1 convert_reduce_fusion.1
  3.7 0.8 copy.91
  4.5 0.3 fusion.23
  4.8 1.0 convolution_convert_fusion.2
  5.8 0.9 convolution_convert_fusion.3
  6.7 0.7 all_to_all.23
  7.4 11.3 %all-to-all-start = ((bf16[32,6,256]{2,1,0:T(8,128)(2,1)}), bf16[32,6,256]{2,1,0:T(8,128)(2,1)S(1)}, u32[]{:S(2)}, u32[]{:S(2)}) async-start(bf16[32,6,256]{2,1,0:T(8,128)(2,1)} %all_to_all.23), calls=%async_computation | async-start | bytes 262144 | tf_op jit(solution)/shard_map/all_to_all | solution.py:65
  18.7 0.1 copy.113
  18.8 9.7 %all-to-all-done = bf16[32,6,256]{2,1,0:T(8,128)(2,1)S(1)} async-done(((bf16[32,6,256]{2,1,0:T(8,128)(2,1)}), bf16[32,6,256]{2,1,0:T(8,128)(2,1)S(1)}, u32[]{:S(2)}, u32[]{:S(2)}) %all-to-all-start) | async-done | bytes 98336 | tf_op jit(solution)/shard_map/all_to_all | solution.py:65
  28.6 0.0 copy-start.8
  28.6 0.7 fusion.4
  29.3 1.0 copy.83
  30.3 18.9 %all-to-all-start.2 = ((bf16[16,32,2,3,88]{4,1,3,2,0:T(8,128)(2,1)}), bf16[16,32,2,3,88]{4,1,3,2,0:T(8,128)(2,1)S(1)}, u32[]{:S(2)}, u32[]{:S(2)}) async-start(bf16[16,32,2,3,88]{4,1,3,2,0:T(8,128)(2,1)} %copy.83), calls=%async_computation.2 | async-start | bytes 1572864 | tf_op jit(solution)/shard_map/all_to_all | solution.py:88
  49.3 1.0 bitcast_bitcast_fusion.1
  50.2 0.1 copy.114
  50.4 1.0 bitcast_bitcast_fusion
  51.4 31.8 %all_gather.3 = bf16[192,2048]{1,0:T(8,128)(2,1)S(1)} all-gather(bf16[192,128]{1,0:T(8,128)(2,1)S(1)} %get-tuple-element.19), channel_id=1, replica_groups=mesh['dp'=2,'expert'=32,'fsdp'=16] {'fsdp'}, dimensions={1}, use_global_device_ids=true | all-gather | bytes 835584 | tf_op jit(solution)/shard_map/all_gather | solution.py:69
  83.2 0.5 reshape.66
  83.7 0.0 copy-start.6
  83.7 2.6 %convolution_bitcast_fusion.3 = f32[32,2,3,88]{3,0,2,1:T(8,128)} fusion(bf16[2,88,2048]{2,1,0:T(8,128)(2,1)} %param.12, bf16[32,2,3,2048]{3,2,1,0:T(4,128)(2,1)S(1)} %reshape.66), kind=kOutput, calls=%fused_computation.18 | convolution fusion | flops 69206016 | bytes 1574912 | tf_op jit(solution)/shard_map/jecd,efd->jecf/dot_general | solution.py:74
  86.3 0.2 convert_reduce_fusion
  86.5 1.7 %multiply_convert_fusion = (bf16[32,2,3,88]{3,0,2,1:T(8,128)(2,1)S(1)}, bf16[32,2,3,88]{3,0,2,1:T(8,128)(2,1)S(1)}, bf16[32,2,3,88]{3,0,2,1:T(8,128)(2,1)S(1)}) fusion(f32[32,2,3,88]{3,0,2,1:T(8,128)S(1)} %convert_reduce_fusion, f32[32,2,3,88]{3,0,2,1:T(8,128)} %convolution_bitcast_fusion.3, bf16[2,88,2048]{2,1,0:T(8,128)(2,1)S(1)} %copy-done.6, ...), kind=kOutput, calls=%fused_computation.65 | convolution fusion | flops 69459456 | bytes 1743872 | tf_op jit(solution)/shard_map/jecd,efd->jecf/dot_general | solution.py:73
  88.2 1.1 broadcast_in_dim.2
  89.3 6.0 %all-to-all-start.1 = ((bf16[16,32,2,3,88]{4,1,3,2,0:T(8,128)(2,1)}), bf16[16,32,2,3,88]{4,1,3,2,0:T(8,128)(2,1)S(1)}, u32[]{:S(2)}, u32[]{:S(2)}) async-start(bf16[16,32,2,3,88]{4,1,3,2,0:T(8,128)(2,1)} %broadcast_in_dim.2), calls=%async_computation.1 | async-start | bytes 1572864 | tf_op jit(solution)/shard_map/all_to_all | solution.py:31
  95.2 0.8 fusion.1
  96.0 0.8 fusion.2
  96.8 0.1 fusion.11
  97.0 1.1 fusion.8
  98.1 4.6 %collective-permute-start = (bf16[2,2,88,1024]{3,2,1,0:T(8,128)(2,1)}, bf16[2,2,88,1024]{3,2,1,0:T(8,128)(2,1)}, u32[]{:S(2)}, u32[]{:S(2)}) collective-permute-start(bf16[2,2,88,1024]{3,2,1,0:T(8,128)(2,1)} %fusion.8), channel_id=1, source_target_pairs={{0,512},{512,0},{1,513},{513,1},{2,514},{514,2},{3,515},{515,3},{4... | collective-permute-start | bytes 2162696 | tf_op jit(solution)/shard_map/ppermute | solution.py:24
  102.7 0.4 fusion.17
  103.1 1.3 add_bitcast_fusion
  104.4 13.9 %all-to-all-done.1 = bf16[16,32,2,3,88]{4,1,3,2,0:T(8,128)(2,1)S(1)} async-done(((bf16[16,32,2,3,88]{4,1,3,2,0:T(8,128)(2,1)}), bf16[16,32,2,3,88]{4,1,3,2,0:T(8,128)(2,1)S(1)}, u32[]{:S(2)}, u32[]{:S(2)}) %all-to-all-start.1) | async-done | bytes 540704 | tf_op jit(solution)/shard_map/all_to_all | solution.py:31
  118.3 1.4 copy.80
  119.7 2.0 %reshape.67 = bf16[32,2,3,1408]{3,0,2,1:T(8,128)(2,1)S(1)} reshape(bf16[32,2,3,16,88]{4,3,0,2,1:T(8,128)(2,1)} %copy.80) | data formatting | bytes 1081344 | tf_op jit(solution)/shard_map/reshape | solution.py:33
  121.7 2.1 %fusion = bf16[2,1408,128]{2,1,0:T(8,128)(2,1)} fusion(bf16[32,2,3,1408]{3,0,2,1:T(8,128)(2,1)S(1)} %reshape.67, bf16[32,2,3,128]{3,2,1,0:T(4,128)(2,1)} %copy-done.8), kind=kOutput, calls=%fused_computation.1 | convolution fusion | flops 69566464 | bytes 1310720 | tf_op jit(solution)/shard_map/jecf,jecd->efd/dot_general | solution.py:98
  123.9 1.0 copy.86
  124.8 3.5 %all-to-all-start.3 = ((bf16[16,32,2,3,128]{4,1,3,2,0:T(8,128)(2,1)}), bf16[16,32,2,3,128]{4,1,3,2,0:T(8,128)(2,1)S(1)}, u32[]{:S(2)}, u32[]{:S(2)}) async-start(bf16[16,32,2,3,128]{4,1,3,2,0:T(8,128)(2,1)} %copy.86), calls=%async_computation.3 | async-start | bytes 1572864 | tf_op jit(solution)/shard_map/all_to_all | solution.py:102
  128.3 9.4 %collective-permute-done = bf16[2,2,88,1024]{3,2,1,0:T(8,128)(2,1)} collective-permute-done((bf16[2,2,88,1024]{3,2,1,0:T(8,128)(2,1)}, bf16[2,2,88,1024]{3,2,1,0:T(8,128)(2,1)}, u32[]{:S(2)}, u32[]{:S(2)}) %collective-permute-start) | collective-permute-done | bytes 720928 | tf_op jit(solution)/shard_map/ppermute | solution.py:24
  137.7 1.6 fusion.3
  139.3 0.9 slice_bitcast_fusion.2
  140.2 0.5 copy-done.7
  140.7 0.9 fusion.20
  141.6 4.2 %collective-permute-start.1 = (bf16[2,704,128]{2,1,0:T(8,128)(2,1)}, bf16[2,704,128]{2,1,0:T(8,128)(2,1)S(1)}, u32[]{:S(2)}, u32[]{:S(2)}) collective-permute-start(bf16[2,704,128]{2,1,0:T(8,128)(2,1)} %fusion.20), channel_id=1, source_target_pairs={{0,512},{512,0},{1,513},{513,1},{2,514},{514,2},{3,515},{515,3},{4... | collective-permute-start | bytes 1081352 | tf_op jit(solution)/shard_map/ppermute | solution.py:24
  145.8 0.3 convolution_convert_fusion.1
  146.1 4.1 %all-to-all-done.3 = bf16[16,32,2,3,128]{4,1,3,2,0:T(8,128)(2,1)S(1)} async-done(((bf16[16,32,2,3,128]{4,1,3,2,0:T(8,128)(2,1)}), bf16[16,32,2,3,128]{4,1,3,2,0:T(8,128)(2,1)S(1)}, u32[]{:S(2)}, u32[]{:S(2)}) %all-to-all-start.3) | async-done | bytes 786464 | tf_op jit(solution)/shard_map/all_to_all | solution.py:102
  150.3 0.1 reduce_sum.45
  150.4 0.7 copy.87
  151.1 3.9 %all-to-all-start.4 = ((bf16[32,6,256]{2,1,0:T(8,128)(2,1)}), bf16[32,6,256]{2,1,0:T(8,128)(2,1)S(1)}, u32[]{:S(2)}, u32[]{:S(2)}) async-start(bf16[32,6,256]{2,1,0:T(8,128)(2,1)} %copy.87), calls=%async_computation.4 | async-start | bytes 262144 | tf_op jit(solution)/shard_map/all_to_all | solution.py:108
  155.0 1.9 %collective-permute-done.1 = bf16[2,704,128]{2,1,0:T(8,128)(2,1)S(1)} collective-permute-done((bf16[2,704,128]{2,1,0:T(8,128)(2,1)}, bf16[2,704,128]{2,1,0:T(8,128)(2,1)S(1)}, u32[]{:S(2)}, u32[]{:S(2)}) %collective-permute-start.1) | collective-permute-done | bytes 360480 | tf_op jit(solution)/shard_map/ppermute | solution.py:24
  156.9 0.9 fusion.12
  157.8 7.0 %all-to-all-done.4 = bf16[32,6,256]{2,1,0:T(8,128)(2,1)S(1)} async-done(((bf16[32,6,256]{2,1,0:T(8,128)(2,1)}), bf16[32,6,256]{2,1,0:T(8,128)(2,1)S(1)}, u32[]{:S(2)}, u32[]{:S(2)}) %all-to-all-start.4) | async-done | bytes 98336 | tf_op jit(solution)/shard_map/all_to_all | solution.py:108
  164.8 0.8 convolution_convert_fusion.4
  165.6 0.8 convolution_convert_fusion.5
  (26 shorter events, 0.3 us)
Async XLA Ops:
  0.6 28.0 %copy-start = (bf16[2,1408,128]{2,1,0:T(8,128)(2,1)S(1)}, bf16[2,1408,128]{2,1,0:T(8,128)(2,1)}, u32[]{:S(2)}) copy-start(bf16[2,1408,128]{2,1,0:T(8,128)(2,1)} %param.13) | copy-start | bytes 2162692
  0.6 18.0 %copy-start.5 = (bf16[2,88,2048]{2,1,0:T(8,128)(2,1)S(1)}, bf16[2,88,2048]{2,1,0:T(8,128)(2,1)}, u32[]{:S(2)}) copy-start(bf16[2,88,2048]{2,1,0:T(8,128)(2,1)} %param.11) | copy-start | bytes 2162692
  7.4 21.1 %all-to-all-start = ((bf16[32,6,256]{2,1,0:T(8,128)(2,1)}), bf16[32,6,256]{2,1,0:T(8,128)(2,1)S(1)}, u32[]{:S(2)}, u32[]{:S(2)}) async-start(bf16[32,6,256]{2,1,0:T(8,128)(2,1)} %all_to_all.23), calls=%async_computation | async-start | bytes 262144 | tf_op jit(solution)/shard_map/all_to_all | solution.py:65
  28.6 1.7 %copy-start.8 = (bf16[32,2,3,128]{3,2,1,0:T(4,128)(2,1)}, bf16[32,2,3,128]{3,2,1,0:T(4,128)(2,1)S(1)}, u32[]{:S(2)}) copy-start(bf16[32,2,3,128]{3,2,1,0:T(4,128)(2,1)S(1)} %reshape.68) | copy-start | bytes 147460
  30.3 19.9 %copy-start.4 = (bf16[2,88,2048]{2,1,0:T(8,128)(2,1)S(1)}, bf16[2,88,2048]{2,1,0:T(8,128)(2,1)}, u32[]{:S(2)}) copy-start(bf16[2,88,2048]{2,1,0:T(8,128)(2,1)} %param.12) | copy-start | bytes 2162692
  30.3 56.0 %all-to-all-start.2 = ((bf16[16,32,2,3,88]{4,1,3,2,0:T(8,128)(2,1)}), bf16[16,32,2,3,88]{4,1,3,2,0:T(8,128)(2,1)S(1)}, u32[]{:S(2)}, u32[]{:S(2)}) async-start(bf16[16,32,2,3,88]{4,1,3,2,0:T(8,128)(2,1)} %copy.83), calls=%async_computation.2 | async-start | bytes 1572864 | tf_op jit(solution)/shard_map/all_to_all | solution.py:88
  83.7 2.8 %copy-start.6 = (bf16[2,88,2048]{2,1,0:T(8,128)(2,1)S(1)}, bf16[2,88,2048]{2,1,0:T(8,128)(2,1)}, u32[]{:S(2)}) copy-start(bf16[2,88,2048]{2,1,0:T(8,128)(2,1)} %param.11) | copy-start | bytes 2162692
  89.3 29.0 %all-to-all-start.1 = ((bf16[16,32,2,3,88]{4,1,3,2,0:T(8,128)(2,1)}), bf16[16,32,2,3,88]{4,1,3,2,0:T(8,128)(2,1)S(1)}, u32[]{:S(2)}, u32[]{:S(2)}) async-start(bf16[16,32,2,3,88]{4,1,3,2,0:T(8,128)(2,1)} %broadcast_in_dim.2), calls=%async_computation.1 | async-start | bytes 1572864 | tf_op jit(solution)/shard_map/all_to_all | solution.py:31
  97.0 5.7 %copy-start.2 = (bf16[2,88,16,128,1]{3,2,1,0,4:T(8,128)(2,1)S(1)}, bf16[2,88,16,128,1]{3,2,1,0,4:T(8,128)(2,1)}, u32[]{:S(2)}) copy-start(bf16[2,88,16,128,1]{3,2,1,0,4:T(8,128)(2,1)} %bitcast_bitcast_fusion.1) | copy-start | bytes 2162692
  98.1 4.9 %copy-start.3 = (bf16[2,88,16,128,1]{3,2,1,0,4:T(8,128)(2,1)S(1)}, bf16[2,88,16,128,1]{3,2,1,0,4:T(8,128)(2,1)}, u32[]{:S(2)}) copy-start(bf16[2,88,16,128,1]{3,2,1,0,4:T(8,128)(2,1)} %bitcast_bitcast_fusion) | copy-start | bytes 2162692
  98.1 39.6 %collective-permute-start = (bf16[2,2,88,1024]{3,2,1,0:T(8,128)(2,1)}, bf16[2,2,88,1024]{3,2,1,0:T(8,128)(2,1)}, u32[]{:S(2)}, u32[]{:S(2)}) collective-permute-start(bf16[2,2,88,1024]{3,2,1,0:T(8,128)(2,1)} %fusion.8), channel_id=1, source_target_pairs={{0,512},{512,0},{1,513},{513,1},{2,514},{514,2},{3,515},{515,3},{4... | collective-permute-start | bytes 2162696 | tf_op jit(solution)/shard_map/ppermute | solution.py:24
  119.7 4.2 %copy-start.1 = (bf16[16,32,2,3,128]{4,1,0,3,2:T(8,128)(2,1)S(1)}, bf16[16,32,2,3,128]{4,1,0,3,2:T(8,128)(2,1)}, u32[]{:S(2)}) copy-start(bf16[16,32,2,3,128]{4,1,0,3,2:T(8,128)(2,1)} %add_bitcast_fusion) | copy-start | bytes 2359300
  124.8 25.4 %all-to-all-start.3 = ((bf16[16,32,2,3,128]{4,1,3,2,0:T(8,128)(2,1)}), bf16[16,32,2,3,128]{4,1,3,2,0:T(8,128)(2,1)S(1)}, u32[]{:S(2)}, u32[]{:S(2)}) async-start(bf16[16,32,2,3,128]{4,1,3,2,0:T(8,128)(2,1)} %copy.86), calls=%async_computation.3 | async-start | bytes 1572864 | tf_op jit(solution)/shard_map/all_to_all | solution.py:102
  139.3 1.4 copy-start.7
  141.6 15.3 %collective-permute-start.1 = (bf16[2,704,128]{2,1,0:T(8,128)(2,1)}, bf16[2,704,128]{2,1,0:T(8,128)(2,1)S(1)}, u32[]{:S(2)}, u32[]{:S(2)}) collective-permute-start(bf16[2,704,128]{2,1,0:T(8,128)(2,1)} %fusion.20), channel_id=1, source_target_pairs={{0,512},{512,0},{1,513},{513,1},{2,514},{514,2},{3,515},{515,3},{4... | collective-permute-start | bytes 1081352 | tf_op jit(solution)/shard_map/ppermute | solution.py:24
  151.1 13.7 %all-to-all-start.4 = ((bf16[32,6,256]{2,1,0:T(8,128)(2,1)}), bf16[32,6,256]{2,1,0:T(8,128)(2,1)S(1)}, u32[]{:S(2)}, u32[]{:S(2)}) async-start(bf16[32,6,256]{2,1,0:T(8,128)(2,1)} %copy.87), calls=%async_computation.4 | async-start | bytes 262144 | tf_op jit(solution)/shard_map/all_to_all | solution.py:108

commit v15 on v6

--- a/solution.py
+++ b/solution.py
@@ -66,7 +66,7 @@
         jnp.concatenate([outgoing, scaled_grad], axis=1),
         "expert", split_axis=0, concat_axis=0, tiled=True,
     )
-    rows_in = gather_fsdp(both_in[:, :local_feat], 1)
+    rows_in = lax.all_gather(both_in[:, :local_feat], "fsdp", axis=1, tiled=True)
     grads_in = both_in[:, local_feat:]
     received = rows_in.reshape(owners, exp_local, capacity, model_width)
     cotangent = grads_in.reshape(owners, exp_local, capacity, -1)

time: 176 us -> 166 us (0.943)
  blocking collectives: 62.4 us -> 31.8 us
  starting transfers between devices: 28.6 us -> 57.6 us
  waiting for transfers between devices: 48.2 us -> 41.4 us
  local copies, waits for them, and re-layouts: 14.9 us -> 12.1 us
    all_to_all x2 -> x0, blocking collectives: 62.4 us -> none  [the longest x1 41.5 us: body(): lax.all_to_all(hidden_parts, 'fsdp', 0, 0, tiled=False).astype(jnp.float32)]
    all_gather x0 -> x1, blocking collectives: none -> 31.8 us  [body(): lax.all_gather(both_in[:, :local_feat], 'fsdp', axis=1, tiled=True)]
    all_to_all x0 -> x2, starting transfers between devices: none -> 30.2 us  [the longest x1 18.9 us: body(): lax.all_to_all(hidden_parts, 'fsdp', 0, 0, tiled=False).astype(jnp.float32)]
    all_to_all x2 -> x1, waiting for transfers between devices: 25.3 us -> 9.07 us  [gather_fsdp(): got = lax.all_to_all(copies, 'fsdp', 0, 0, tiled=False)]
    all_to_all x0 -> x2, waiting for transfers between devices: none -> 9.68 us  [the longest x1 9.68 us: body(): lax.all_to_all(jnp.concatenate([outgoing, scaled_grad], axis=1), 'expert'...]
    unnamed x14 -> x20, local copies, waits for them, and re-layouts: 3.91 us -> 1.98 us
    all_to_all x2 -> x1, starting transfers between devices: 7.02 us -> 5.96 us  [gather_fsdp(): got = lax.all_to_all(copies, 'fsdp', 0, 0, tiled=False)]
  transfers between devices with their start and end apart: 7 -> 8, of which waited for: 6 -> 6; matrix products, arithmetic and copies ran while one was open for 10% -> 11% of each run, Pallas kernels for 0% -> 0%
where the time goes in v15:
time: 166 us; the launch traced here: 165 us
  starting transfers between devices  57.6 us (35%)
  waiting for transfers between devices  41.4 us (25%)
  blocking collectives  31.8 us (19%)
  matrix products  12.6 us (8%)
  local copies, waits for them, and re-layouts  12.1 us (7%)
  other arithmetic  8.89 us (5%)
    all_gather x1, blocking collectives, body(): lax.all_gather(both_in[:, :local_feat], 'fsdp', axis=1, tiled=True)  31.8 us
    all_to_all x1, starting transfers between devices, body(): lax.all_to_all(hidden_parts, 'fsdp', 0, 0, tiled=False).astype(jnp.float32)  18.9 us
    ppermute x3, waiting for transfers between devices, dp_reduce(): got = lax.ppermute(send, 'dp', perm=[(0, 1), (1, 0)])  16.8 us
    ppermute x3, starting transfers between devices, dp_reduce(): got = lax.ppermute(send, 'dp', perm=[(0, 1), (1, 0)])  13.4 us
    all_to_all x1, starting transfers between devices, body(): lax.all_to_all(jnp.concatenate([outgoing, scaled_grad], axis=1), 'expert'...  11.3 us
    all_to_all x1, waiting for transfers between devices, body(): lax.all_to_all(jnp.concatenate([outgoing, scaled_grad], axis=1), 'expert'...  9.68 us
    all_to_all x1, waiting for transfers between devices, gather_fsdp(): got = lax.all_to_all(copies, 'fsdp', 0, 0, tiled=False)  9.07 us
    all_to_all x1, starting transfers between devices, gather_fsdp(): got = lax.all_to_all(copies, 'fsdp', 0, 0, tiled=False)  5.96 us
  transfers between devices with their start and end apart: 8, of which 6 were waited for; matrix products, arithmetic and copies ran while one was open for 11% of the time, Pallas kernels for 0%

profile of v15, /device:TPU:1, one launch (start us, length us, event | category | flops | bytes accessed | tf_op | source)
XLA Modules:
  0.0 165.4 jit_solution(17558166628468332354)
XLA Ops:
  0.6 0.0 copy-start
  0.7 0.9 copy.74
  1.5 0.1 eq.35
  1.7 0.6 reduce-window.6
  2.3 0.2 slice_reduce_fusion
  2.5 0.1 bitcast_bitcast_fusion.2
  2.7 0.1 reduce_sum.42
  2.8 0.1 copy.77
  2.8 0.7 multiply_add_fusion
  3.5 0.1 convert_reduce_fusion.1
  3.6 0.1 iota_compare_fusion
  3.7 0.8 copy.91
  4.5 0.3 fusion.26
  4.8 1.0 convolution_convert_fusion.2
  5.8 0.9 convolution_convert_fusion.3
  6.7 0.7 all_to_all.23
  7.4 11.3 %all-to-all-start = ((bf16[32,6,256]{2,1,0:T(8,128)(2,1)}), bf16[32,6,256]{2,1,0:T(8,128)(2,1)S(1)}, u32[]{:S(2)}, u32[]{:S(2)}) async-start(bf16[32,6,256]{2,1,0:T(8,128)(2,1)} %all_to_all.23), calls=%async_computation | async-start | bytes 262144 | tf_op jit(solution)/shard_map/all_to_all | solution.py:65
  18.7 0.1 copy.114
  18.9 9.7 %all-to-all-done = bf16[32,6,256]{2,1,0:T(8,128)(2,1)S(1)} async-done(((bf16[32,6,256]{2,1,0:T(8,128)(2,1)}), bf16[32,6,256]{2,1,0:T(8,128)(2,1)S(1)}, u32[]{:S(2)}, u32[]{:S(2)}) %all-to-all-start) | async-done | bytes 98336 | tf_op jit(solution)/shard_map/all_to_all | solution.py:65
  28.6 0.7 fusion.3
  29.3 1.0 copy.82
  30.3 18.9 %all-to-all-start.2 = ((bf16[16,32,2,3,88]{4,1,3,2,0:T(8,128)(2,1)}), bf16[16,32,2,3,88]{4,1,3,2,0:T(8,128)(2,1)S(1)}, u32[]{:S(2)}, u32[]{:S(2)}) async-start(bf16[16,32,2,3,88]{4,1,3,2,0:T(8,128)(2,1)} %copy.82), calls=%async_computation.2 | async-start | bytes 1572864 | tf_op jit(solution)/shard_map/all_to_all | solution.py:88
  49.3 1.0 bitcast_bitcast_fusion
  50.3 0.1 copy.113
  50.4 1.0 bitcast_bitcast_fusion.1
  51.4 31.8 %all_gather.3 = bf16[192,2048]{1,0:T(8,128)(2,1)S(1)} all-gather(bf16[192,128]{1,0:T(8,128)(2,1)S(1)} %get-tuple-element.15), channel_id=1, replica_groups=mesh['dp'=2,'expert'=32,'fsdp'=16] {'fsdp'}, dimensions={1}, use_global_device_ids=true | all-gather | bytes 835584 | tf_op jit(solution)/shard_map/all_gather | solution.py:69
  83.2 0.5 reshape.66
  83.7 0.0 copy-start.5
  83.7 2.6 %convolution_bitcast_fusion.4 = f32[32,2,3,88]{3,0,2,1:T(8,128)} fusion(bf16[2,88,2048]{2,1,0:T(8,128)(2,1)} %param.11, bf16[32,2,3,2048]{3,2,1,0:T(4,128)(2,1)S(1)} %reshape.66), kind=kOutput, calls=%fused_computation.12 | convolution fusion | flops 69206016 | bytes 1574912 | tf_op jit(solution)/shard_map/jecd,efd->jecf/dot_general | solution.py:73
  86.3 0.2 convert_reduce_fusion
  86.5 1.7 %multiply_convert_fusion.2 = (bf16[32,2,3,88]{3,0,2,1:T(8,128)(2,1)S(1)}, bf16[32,2,3,88]{3,0,2,1:T(8,128)(2,1)S(1)}, bf16[32,2,3,88]{3,0,2,1:T(8,128)(2,1)S(1)}) fusion(f32[32,2,3,88]{3,0,2,1:T(8,128)} %convolution_bitcast_fusion.4, f32[32,2,3,88]{3,0,2,1:T(8,128)S(1)} %convert_reduce_fusion, bf16[2,88,2048]{2,1,0:T(8,128)(2,1)S(1)} %copy-done.5, ...), kind=kOutput, calls=%fused_computation.74 | convolution fusion | flops 69459456 | bytes 1743872 | tf_op jit(solution)/shard_map/jecd,efd->jecf/dot_general | solution.py:74
  88.2 0.8 fusion.1
  89.0 1.7 %fusion.2 = bf16[2,88,2048]{2,1,0:T(8,128)(2,1)} fusion(bf16[32,2,3,88]{3,0,2,1:T(8,128)(2,1)S(1)} %get-tuple-element.13, bf16[32,2,3,2048]{3,2,1,0:T(4,128)(2,1)S(1)} %reshape.66), kind=kOutput, calls=%fused_computation.5 | convolution fusion | flops 69566464 | bytes 1541120 | tf_op jit(solution)/shard_map/jecf,jecd->efd/dot_general | solution.py:121
  90.7 0.1 slice_bitcast_fusion.4
  90.7 1.1 broadcast_in_dim.2
  91.8 6.0 %all-to-all-start.1 = ((bf16[16,32,2,3,88]{4,1,3,2,0:T(8,128)(2,1)}), bf16[16,32,2,3,88]{4,1,3,2,0:T(8,128)(2,1)S(1)}, u32[]{:S(2)}, u32[]{:S(2)}) async-start(bf16[16,32,2,3,88]{4,1,3,2,0:T(8,128)(2,1)} %broadcast_in_dim.2), calls=%async_computation.1 | async-start | bytes 1572864 | tf_op jit(solution)/shard_map/all_to_all | solution.py:31
  97.8 0.9 fusion.23
  98.6 4.4 %collective-permute-start = (bf16[2,88,1024]{2,1,0:T(8,128)(2,1)}, bf16[2,88,1024]{2,1,0:T(8,128)(2,1)S(1)}, u32[]{:S(2)}, u32[]{:S(2)}) collective-permute-start(bf16[2,88,1024]{2,1,0:T(8,128)(2,1)} %fusion.23), channel_id=1, source_target_pairs={{0,512},{512,0},{1,513},{513,1},{2,514},{514,2},{3,515},{515,3},{4... | collective-permute-start | bytes 1081352 | tf_op jit(solution)/shard_map/ppermute | solution.py:24
  103.1 1.1 slice_bitcast_fusion.2
  104.2 0.9 fusion.19
  105.1 4.8 %collective-permute-start.1 = (bf16[2,88,1024]{2,1,0:T(8,128)(2,1)}, bf16[2,88,1024]{2,1,0:T(8,128)(2,1)}, u32[]{:S(2)}, u32[]{:S(2)}) collective-permute-start(bf16[2,88,1024]{2,1,0:T(8,128)(2,1)} %fusion.19), channel_id=1, source_target_pairs={{0,512},{512,0},{1,513},{513,1},{2,514},{514,2},{3,515},{515,3},{4... | collective-permute-start | bytes 1081352 | tf_op jit(solution)/shard_map/ppermute | solution.py:24
  109.9 0.4 fusion.12
  110.3 0.4 fusion.4
  110.6 1.0 copy.85
  111.6 9.1 %all-to-all-done.1 = bf16[16,32,2,3,88]{4,1,3,2,0:T(8,128)(2,1)S(1)} async-done(((bf16[16,32,2,3,88]{4,1,3,2,0:T(8,128)(2,1)}), bf16[16,32,2,3,88]{4,1,3,2,0:T(8,128)(2,1)S(1)}, u32[]{:S(2)}, u32[]{:S(2)}) %all-to-all-start.1) | async-done | bytes 540704 | tf_op jit(solution)/shard_map/all_to_all | solution.py:31
  120.7 4.2 %all-to-all-start.3 = ((bf16[16,32,2,3,128]{4,1,3,2,0:T(8,128)(2,1)}), bf16[16,32,2,3,128]{4,1,3,2,0:T(8,128)(2,1)}, u32[]{:S(2)}, u32[]{:S(2)}) async-start(bf16[16,32,2,3,128]{4,1,3,2,0:T(8,128)(2,1)} %copy.85), calls=%async_computation.3 | async-start | bytes 1572864 | tf_op jit(solution)/shard_map/all_to_all | solution.py:98
  124.9 5.4 %collective-permute-done = bf16[2,88,1024]{2,1,0:T(8,128)(2,1)S(1)} collective-permute-done((bf16[2,88,1024]{2,1,0:T(8,128)(2,1)}, bf16[2,88,1024]{2,1,0:T(8,128)(2,1)S(1)}, u32[]{:S(2)}, u32[]{:S(2)}) %collective-permute-start) | collective-permute-done | bytes 360480 | tf_op jit(solution)/shard_map/ppermute | solution.py:24
  130.3 1.0 fusion.7
  131.2 6.9 %collective-permute-done.1 = bf16[2,88,1024]{2,1,0:T(8,128)(2,1)} collective-permute-done((bf16[2,88,1024]{2,1,0:T(8,128)(2,1)}, bf16[2,88,1024]{2,1,0:T(8,128)(2,1)}, u32[]{:S(2)}, u32[]{:S(2)}) %collective-permute-start.1) | collective-permute-done | bytes 360480 | tf_op jit(solution)/shard_map/ppermute | solution.py:24
  138.1 2.0 %fusion.6 = bf16[2,88,1024]{2,1,0:T(8,128)(2,1)} fusion(bf16[2,88,1024]{2,1,0:T(8,128)(2,1)} %collective-permute-done.1, s32[]{:T(128)S(6)} %select_n.12, bf16[1,2,88,1024]{3,2,1,0:T(8,128)(2,1)S(1)} %get-tuple-element.8, bf16[1,2,88,1024]{3,2,1,0:T(8,128)(2,1)S(1)} %get-tuple-element.7), kind=kLoop, calls=%fused_computation.35 | loop fusion | flops 901120 | bytes 1441796 | tf_op jit(solution)/shard_map/convert_element_type | solution.py:25
  140.0 0.5 copy.80
  140.6 0.9 reshape.67
  141.5 0.4 fusion
  141.9 0.1 fusion.15
  142.1 4.2 %collective-permute-start.2 = (bf16[2,704,128]{2,1,0:T(8,128)(2,1)S(1)}, bf16[2,704,128]{2,1,0:T(8,128)(2,1)S(1)}, u32[]{:S(2)}, u32[]{:S(2)}) collective-permute-start(bf16[2,704,128]{2,1,0:T(8,128)(2,1)S(1)} %fusion.15), channel_id=1, source_target_pairs={{0,512},{512,0},{1,513},{513,1},{2,514},{514,2},{3,515},{515,3},{4... | collective-permute-start | bytes 1081352 | tf_op jit(solution)/shard_map/ppermute | solution.py:24
  146.3 0.3 convolution_convert_fusion.1
  146.7 1.3 reduce_sum.45
  147.9 0.7 copy.86
  148.6 3.9 %all-to-all-start.4 = ((bf16[32,6,256]{2,1,0:T(8,128)(2,1)}), bf16[32,6,256]{2,1,0:T(8,128)(2,1)S(1)}, u32[]{:S(2)}, u32[]{:S(2)}) async-start(bf16[32,6,256]{2,1,0:T(8,128)(2,1)} %copy.86), calls=%async_computation.4 | async-start | bytes 262144 | tf_op jit(solution)/shard_map/all_to_all | solution.py:104
  152.5 4.6 %collective-permute-done.2 = bf16[2,704,128]{2,1,0:T(8,128)(2,1)S(1)} collective-permute-done((bf16[2,704,128]{2,1,0:T(8,128)(2,1)S(1)}, bf16[2,704,128]{2,1,0:T(8,128)(2,1)S(1)}, u32[]{:S(2)}, u32[]{:S(2)}) %collective-permute-start.2) | collective-permute-done | bytes 360480 | tf_op jit(solution)/shard_map/ppermute | solution.py:24
  157.0 0.9 fusion.5
  158.0 5.9 %all-to-all-done.4 = bf16[32,6,256]{2,1,0:T(8,128)(2,1)S(1)} async-done(((bf16[32,6,256]{2,1,0:T(8,128)(2,1)}), bf16[32,6,256]{2,1,0:T(8,128)(2,1)S(1)}, u32[]{:S(2)}, u32[]{:S(2)}) %all-to-all-start.4) | async-done | bytes 98336 | tf_op jit(solution)/shard_map/all_to_all | solution.py:104
  163.9 0.8 convolution_convert_fusion.4
  164.7 0.8 convolution_convert_fusion.5
  (28 shorter events, 0.3 us)
Async XLA Ops:
  0.6 28.0 %copy-start = (bf16[2,1408,128]{2,1,0:T(8,128)(2,1)S(1)}, bf16[2,1408,128]{2,1,0:T(8,128)(2,1)}, u32[]{:S(2)}) copy-start(bf16[2,1408,128]{2,1,0:T(8,128)(2,1)} %param.13) | copy-start | bytes 2162692
  0.6 18.1 %copy-start.4 = (bf16[2,88,2048]{2,1,0:T(8,128)(2,1)S(1)}, bf16[2,88,2048]{2,1,0:T(8,128)(2,1)}, u32[]{:S(2)}) copy-start(bf16[2,88,2048]{2,1,0:T(8,128)(2,1)} %param.12) | copy-start | bytes 2162692
  4.8 1.0 copy-start.6
  7.4 21.1 %all-to-all-start = ((bf16[32,6,256]{2,1,0:T(8,128)(2,1)}), bf16[32,6,256]{2,1,0:T(8,128)(2,1)S(1)}, u32[]{:S(2)}, u32[]{:S(2)}) async-start(bf16[32,6,256]{2,1,0:T(8,128)(2,1)} %all_to_all.23), calls=%async_computation | async-start | bytes 262144 | tf_op jit(solution)/shard_map/all_to_all | solution.py:65
  30.3 19.9 %copy-start.3 = (bf16[2,88,2048]{2,1,0:T(8,128)(2,1)S(1)}, bf16[2,88,2048]{2,1,0:T(8,128)(2,1)}, u32[]{:S(2)}) copy-start(bf16[2,88,2048]{2,1,0:T(8,128)(2,1)} %param.11) | copy-start | bytes 2162692
  30.3 56.0 %all-to-all-start.2 = ((bf16[16,32,2,3,88]{4,1,3,2,0:T(8,128)(2,1)}), bf16[16,32,2,3,88]{4,1,3,2,0:T(8,128)(2,1)S(1)}, u32[]{:S(2)}, u32[]{:S(2)}) async-start(bf16[16,32,2,3,88]{4,1,3,2,0:T(8,128)(2,1)} %copy.82), calls=%async_computation.2 | async-start | bytes 1572864 | tf_op jit(solution)/shard_map/all_to_all | solution.py:88
  83.7 2.8 %copy-start.5 = (bf16[2,88,2048]{2,1,0:T(8,128)(2,1)S(1)}, bf16[2,88,2048]{2,1,0:T(8,128)(2,1)}, u32[]{:S(2)}) copy-start(bf16[2,88,2048]{2,1,0:T(8,128)(2,1)} %param.12) | copy-start | bytes 2162692
  91.8 28.9 %all-to-all-start.1 = ((bf16[16,32,2,3,88]{4,1,3,2,0:T(8,128)(2,1)}), bf16[16,32,2,3,88]{4,1,3,2,0:T(8,128)(2,1)S(1)}, u32[]{:S(2)}, u32[]{:S(2)}) async-start(bf16[16,32,2,3,88]{4,1,3,2,0:T(8,128)(2,1)} %broadcast_in_dim.2), calls=%async_computation.1 | async-start | bytes 1572864 | tf_op jit(solution)/shard_map/all_to_all | solution.py:31
  97.8 12.1 %copy-start.2 = (bf16[2,88,16,128,1]{3,2,1,0,4:T(8,128)(2,1)S(1)}, bf16[2,88,16,128,1]{3,2,1,0,4:T(8,128)(2,1)}, u32[]{:S(2)}) copy-start(bf16[2,88,16,128,1]{3,2,1,0,4:T(8,128)(2,1)} %bitcast_bitcast_fusion.1) | copy-start | bytes 2162692
  98.6 31.6 %collective-permute-start = (bf16[2,88,1024]{2,1,0:T(8,128)(2,1)}, bf16[2,88,1024]{2,1,0:T(8,128)(2,1)S(1)}, u32[]{:S(2)}, u32[]{:S(2)}) collective-permute-start(bf16[2,88,1024]{2,1,0:T(8,128)(2,1)} %fusion.23), channel_id=1, source_target_pairs={{0,512},{512,0},{1,513},{513,1},{2,514},{514,2},{3,515},{515,3},{4... | collective-permute-start | bytes 1081352 | tf_op jit(solution)/shard_map/ppermute | solution.py:24
  104.2 6.0 %copy-start.1 = (bf16[2,88,16,128,1]{3,2,1,0,4:T(8,128)(2,1)S(1)}, bf16[2,88,16,128,1]{3,2,1,0,4:T(8,128)(2,1)}, u32[]{:S(2)}) copy-start(bf16[2,88,16,128,1]{3,2,1,0,4:T(8,128)(2,1)} %bitcast_bitcast_fusion) | copy-start | bytes 2162692
  105.1 33.0 %collective-permute-start.1 = (bf16[2,88,1024]{2,1,0:T(8,128)(2,1)}, bf16[2,88,1024]{2,1,0:T(8,128)(2,1)}, u32[]{:S(2)}, u32[]{:S(2)}) collective-permute-start(bf16[2,88,1024]{2,1,0:T(8,128)(2,1)} %fusion.19), channel_id=1, source_target_pairs={{0,512},{512,0},{1,513},{513,1},{2,514},{514,2},{3,515},{515,3},{4... | collective-permute-start | bytes 1081352 | tf_op jit(solution)/shard_map/ppermute | solution.py:24
  120.7 25.9 %all-to-all-start.3 = ((bf16[16,32,2,3,128]{4,1,3,2,0:T(8,128)(2,1)}), bf16[16,32,2,3,128]{4,1,3,2,0:T(8,128)(2,1)}, u32[]{:S(2)}, u32[]{:S(2)}) async-start(bf16[16,32,2,3,128]{4,1,3,2,0:T(8,128)(2,1)} %copy.85), calls=%async_computation.3 | async-start | bytes 1572864 | tf_op jit(solution)/shard_map/all_to_all | solution.py:98
  142.1 15.0 %collective-permute-start.2 = (bf16[2,704,128]{2,1,0:T(8,128)(2,1)S(1)}, bf16[2,704,128]{2,1,0:T(8,128)(2,1)S(1)}, u32[]{:S(2)}, u32[]{:S(2)}) collective-permute-start(bf16[2,704,128]{2,1,0:T(8,128)(2,1)S(1)} %fusion.15), channel_id=1, source_target_pairs={{0,512},{512,0},{1,513},{513,1},{2,514},{514,2},{3,515},{515,3},{4... | collective-permute-start | bytes 1081352 | tf_op jit(solution)/shard_map/ppermute | solution.py:24
  146.6 18.0 %copy-start.7 = (f32[32,1,192]{2,1,0:T(1,128)S(1)}, f32[32,1,192]{2,1,0:T(1,128)}, u32[]{:S(2)}) copy-start(f32[32,1,192]{2,1,0:T(1,128)} %copy-done.6) | copy-start | bytes 73732
  148.6 15.2 %all-to-all-start.4 = ((bf16[32,6,256]{2,1,0:T(8,128)(2,1)}), bf16[32,6,256]{2,1,0:T(8,128)(2,1)S(1)}, u32[]{:S(2)}, u32[]{:S(2)}) async-start(bf16[32,6,256]{2,1,0:T(8,128)(2,1)} %copy.86), calls=%async_computation.4 | async-start | bytes 262144 | tf_op jit(solution)/shard_map/all_to_all | solution.py:104
